TPU v7x, 32 devices: a whole 2x2x4 slice. The times are simulated.
32 devices in a mesh: dp: 4 (over x, core), fsdp: 8 (over z, y).
Axes of the slice: x: 2, y: 2, z: 4, core: 2. Of those that a mesh axis runs over, the one named last changes fastest.
Arguments:
- tokens: bfloat16 [8192, 640], P(('dp', 'fsdp')), may hold values from -6 to 6
- cotangent: bfloat16 [8192, 640], P(('dp', 'fsdp')), may hold values from -6 to 6
- masked_pos: int32 [8192], P(('dp', 'fsdp')), may hold values from 0 to 1
- labels: int32 [8192], P(('dp', 'fsdp')), may hold values from 0 to 3
- decoder: bfloat16 [4, 640], replicated, may hold values from -0.375 to 0.375
- master: float32 [640, 12800], P('fsdp'), may hold values from -0.6324555 to 0.6324555
- small_params: float32 [640, 16], P('fsdp'), may hold values from -0.8 to 1.4
- small_first: float32 [640, 16], P('fsdp'), may hold values from -128 to 128
- small_second: float32 [640, 16], P('fsdp'), may hold values from 163.84 to 4096
- block_slots: int32 [40], replicated, may hold values from 0 to 39, as said below
- first_moment: float32 [40, 640, 320], P('fsdp'), may hold values from -128 to 128
- second_moment: float32 [40, 640, 320], P('fsdp'), may hold values from 163.84 to 4096
- left_bases: float32 [40, 640, 640], P('fsdp'), may hold values from -1 to 1, as said below
- right_bases: float32 [40, 320, 320], P('fsdp'), may hold values from -1 to 1, as said below
Outputs:
- out_tokens: bfloat16 [8192, 640], P(('dp', 'fsdp'))
- grad_tokens: bfloat16 [8192, 640], P(('dp', 'fsdp'))
- grad_weights: float32 [640, 12800], P('fsdp')
- grad_small: float32 [640, 16], P('fsdp')
- new_first: float32 [40, 640, 320], P('fsdp')
- new_second: float32 [40, 640, 320], P('fsdp')
- new_master: float32 [640, 12800], P('fsdp')
- new_copy: bfloat16 [640, 12800], P('fsdp')
- new_small: float32 [640, 16], P('fsdp')
- new_small_first: float32 [640, 16], P('fsdp')
- new_small_second: float32 [640, 16], P('fsdp')
- loss_accuracy: float32 [5], replicated
- counts: int32 [4], replicated
Inputs may be any that keep to these rules, and one draw needn't show every extreme that they name: Distinct slot numbers; block b (columns b * 320 to (b + 1) * 320 - 1 of the weights) keeps its optimizer state in slot block_slots[b], held by fsdp index block_slots[b] // 5; at most 5 blocks on one index. `left_bases`: each slot's matrix is orthogonal. `right_bases`: each slot's matrix is orthogonal.
All inputs are finite; a program needn't handle non-finite values.
Results may differ from a plain program's by a relative error of at most 0.013.
The roundings to bfloat16 on the way count: a program that leaves them out, or rounds other values in their place, can miss the bound.
Values may be sent and summed in bfloat16 or wider, within the bound.
No kernel may reach another device: no remote copies, remote signals or barrier semaphores. Data moves between devices by JAX's collectives and lax.ppermute only.
A program may use at most 256 MiB of HBM per device.

v0:
```python
import jax
import jax.numpy as jnp
from jax import lax
from jax.sharding import PartitionSpec as P

HEAD_DIM = 32
SEQ_LEN = 256
STEP = 5


EPS_NORM = 1e-05
EPS_ADAM = 1e-08
BETA_FIRST = 0.5
BETA_SECOND = 0.5
RATE_MATRIX = 0.02
RATE_VECTOR = 0.05
EXACT_PRECISION = lax.Precision.HIGHEST


def normalize_layer(rows_in, norm_gain, norm_shift):
    centred = rows_in - jnp.mean(rows_in, axis=-1, keepdims=True)
    variance = jnp.mean(centred * centred, axis=-1, keepdims=True)
    return centred * lax.rsqrt(variance + EPS_NORM) * norm_gain + norm_shift


def exact_gelu(inputs):
    return jax.nn.gelu(inputs, approximate=False)


def adam_direction(first_new, second_new):
    return (
        first_new
        / (1.0 - BETA_FIRST**STEP)
        / (jnp.sqrt(second_new / (1.0 - BETA_SECOND**STEP)) + EPS_ADAM)
    )


def contract_rows(left_mat, right_mat):
    return lax.dot_general(
        left_mat, right_mat, (((0,), (0,)), ((), ())), preferred_element_type=jnp.float32
    )


def times_transpose(left_mat, right_mat):
    return lax.dot_general(
        left_mat, right_mat, (((1,), (1,)), ((), ())), preferred_element_type=jnp.float32
    )


def block_scores(queries, key_rows):
    return jnp.einsum(
        "slhd,smhd->shlm", queries, key_rows, preferred_element_type=jnp.float32
    ) * HEAD_DIM ** (-0.5)


def attend_block(weight_blocks):
    queries, key_rows, values = weight_blocks
    scores = block_scores(queries, key_rows)
    highest = jnp.max(scores, axis=-1, keepdims=True)
    exponent = jnp.exp(scores - highest)
    totals = jnp.sum(exponent, axis=-1, keepdims=True)
    weights_soft = (exponent / totals).astype(jnp.bfloat16)
    mixed_rows = jnp.einsum(
        "shlm,smhd->slhd", weights_soft, values, preferred_element_type=jnp.float32
    )
    return (mixed_rows.astype(jnp.bfloat16), (highest + jnp.log(totals))[..., 0])


def attend_back(weight_blocks):
    queries, key_rows, values, log_total, d_attended = weight_blocks
    probabilities = jnp.exp(block_scores(queries, key_rows) - log_total[..., None])
    d_values = jnp.einsum(
        "shlm,slhd->smhd",
        probabilities.astype(jnp.bfloat16),
        d_attended,
        preferred_element_type=jnp.float32,
    )
    d_probs = jnp.einsum("slhd,smhd->shlm", d_attended, values, preferred_element_type=jnp.float32)
    d_scores = (
        probabilities * (d_probs - jnp.sum(probabilities * d_probs, axis=-1, keepdims=True))
    ).astype(jnp.bfloat16)
    d_queries = jnp.einsum(
        "shlm,smhd->slhd", d_scores, key_rows, preferred_element_type=jnp.float32
    ) * HEAD_DIM ** (-0.5)
    d_keys = jnp.einsum(
        "shlm,slhd->smhd", d_scores, queries, preferred_element_type=jnp.float32
    ) * HEAD_DIM ** (-0.5)
    return (
        d_queries.astype(jnp.bfloat16),
        d_keys.astype(jnp.bfloat16),
        d_values.astype(jnp.bfloat16),
    )


def local(
    tokens,
    cotangent,
    masked_pos,
    labels,
    decoder,
    master,
    small_params,
    small_first,
    small_second,
    block_slots,
    first_moment,
    second_moment,
    left_bases,
    right_bases,
):
    model_width = decoder.shape[1]
    hidden = (master.shape[1] - 4 * model_width) // 2
    heads_count = model_width // HEAD_DIM
    token_count = tokens.shape[0]
    local_weights = master.astype(jnp.bfloat16)
    local_small = small_params.astype(jnp.bfloat16)
    weights, small_all = (
        lax.all_gather(local_weights, "fsdp", axis=0, tiled=True),
        lax.all_gather(local_small, "fsdp", axis=0, tiled=True),
    )
    params = small_all.astype(jnp.float32)
    gain_one, shift_one, bias_query, bias_value, bias_output, gain_two, shift_two, bias_down = [
        params[:, column] for column in range(8)
    ]
    bias_up = params[:, 8:].reshape(hidden)
    rows_in = tokens.astype(jnp.float32)
    normed = normalize_layer(rows_in, gain_one, shift_one).astype(jnp.bfloat16)
    bias_qkv = jnp.concatenate([bias_query, jnp.zeros_like(bias_query), bias_value])
    projected = (
        jnp.dot(normed, weights[:, : 3 * model_width], preferred_element_type=jnp.float32)
        + bias_qkv
    ).astype(jnp.bfloat16)
    seq_count = token_count // SEQ_LEN
    per_block = max(1, min(seq_count, 512 // SEQ_LEN))
    block_shape = (seq_count // per_block, per_block, SEQ_LEN, heads_count, HEAD_DIM)
    queries = projected[:, :model_width].reshape(block_shape)
    key_rows = projected[:, model_width : 2 * model_width].reshape(block_shape)
    values = projected[:, 2 * model_width :].reshape(block_shape)
    attention_result, log_total = lax.map(attend_block, (queries, key_rows, values))
    attention_result = attention_result.reshape(token_count, model_width)
    middle = (
        rows_in
        + jnp.dot(
            attention_result,
            weights[:, 3 * model_width : 4 * model_width],
            preferred_element_type=jnp.float32,
        )
        + bias_output
    )
    normed_two = normalize_layer(middle, gain_two, shift_two).astype(jnp.bfloat16)
    pre_active = (
        jnp.dot(
            normed_two,
            weights[:, 4 * model_width : 4 * model_width + hidden],
            preferred_element_type=jnp.float32,
        )
        + bias_up
    )
    active = exact_gelu(pre_active).astype(jnp.bfloat16)
    output_rows = (
        middle + times_transpose(active, weights[:, 4 * model_width + hidden :]) + bias_down
    )
    out_tokens = output_rows.astype(jnp.bfloat16)
    logits = times_transpose(out_tokens, decoder)
    log_norm = jax.nn.logsumexp(logits, axis=-1)
    one_hot = (labels[:, None] == jnp.arange(decoder.shape[0], dtype=jnp.int32)[None, :]).astype(
        jnp.float32
    )
    hidden_tokens = masked_pos.astype(jnp.float32)
    chosen = one_hot * hidden_tokens[:, None]
    entropy = log_norm - jnp.sum(one_hot * logits, axis=-1)
    right_prob = jnp.sum(one_hot * jnp.exp(logits - log_norm[:, None]), axis=-1)
    local_sums = jnp.concatenate(
        [jnp.sum(hidden_tokens * entropy)[None], jnp.sum(chosen * right_prob[:, None], axis=0)]
    )
    global_sums, global_counts = lax.psum((local_sums, jnp.sum(chosen, axis=0)), ("dp", "fsdp"))
    loss_accuracy = jnp.concatenate(
        [
            global_sums[:1] / jnp.maximum(jnp.sum(global_counts), 1.0),
            global_sums[1:] / jnp.maximum(global_counts, 1.0),
        ]
    )
    counts = global_counts.astype(jnp.int32)
    weights_back, small_back = (
        lax.all_gather(local_weights, "fsdp", axis=0, tiled=True),
        lax.all_gather(local_small, "fsdp", axis=0, tiled=True),
    )
    params_back = small_back.astype(jnp.float32)
    back_rows = cotangent.astype(jnp.float32)
    d_active = jnp.dot(
        cotangent, weights_back[:, 4 * model_width + hidden :], preferred_element_type=jnp.float32
    )
    unused, gelu_pull = jax.vjp(exact_gelu, pre_active)
    d_pre = gelu_pull(d_active)[0].astype(jnp.bfloat16)
    d_normed_two = times_transpose(
        d_pre, weights_back[:, 4 * model_width : 4 * model_width + hidden]
    )
    unused, norm_pull_two = jax.vjp(normalize_layer, middle, params_back[:, 5], params_back[:, 6])
    d_middle_norm, d_gain_two, d_shift_two = norm_pull_two(d_normed_two)
    d_middle = back_rows + d_middle_norm
    d_branch = d_middle.astype(jnp.bfloat16)
    d_attended = times_transpose(
        d_branch, weights_back[:, 3 * model_width : 4 * model_width]
    ).astype(jnp.bfloat16)
    d_queries, d_keys, d_values = lax.map(
        attend_back, (queries, key_rows, values, log_total, d_attended.reshape(block_shape))
    )
    d_projected = jnp.concatenate(
        [
            d_queries.reshape(token_count, model_width),
            d_keys.reshape(token_count, model_width),
            d_values.reshape(token_count, model_width),
        ],
        axis=1,
    )
    d_normed = times_transpose(d_projected, weights_back[:, : 3 * model_width])
    unused, norm_pull_one = jax.vjp(normalize_layer, rows_in, params_back[:, 0], params_back[:, 1])
    d_rows_norm, d_gain_one, d_shift_one = norm_pull_one(d_normed)
    grad_tokens = (d_middle + d_rows_norm).astype(jnp.bfloat16)
    grad_w_local = jnp.concatenate(
        [
            contract_rows(normed, d_projected),
            contract_rows(attention_result, d_branch),
            contract_rows(normed_two, d_pre),
            contract_rows(cotangent, active),
        ],
        axis=1,
    )
    proj_sums = jnp.sum(d_projected.astype(jnp.float32), axis=0)
    small_cols = jnp.stack(
        [
            d_gain_one,
            d_shift_one,
            proj_sums[:model_width],
            proj_sums[2 * model_width :],
            jnp.sum(d_branch.astype(jnp.float32), axis=0),
            d_gain_two,
            d_shift_two,
            jnp.sum(back_rows, axis=0),
        ],
        axis=1,
    )
    grad_s_local = jnp.concatenate(
        [small_cols, jnp.sum(d_pre.astype(jnp.float32), axis=0).reshape(model_width, -1)], axis=1
    )
    part_w, part_s = (
        lax.psum_scatter(grad_w_local, "dp", scatter_dimension=1, tiled=True),
        lax.psum_scatter(grad_s_local, "dp", scatter_dimension=1, tiled=True),
    )
    part_w, part_s = (
        lax.psum_scatter(part_w, "fsdp", scatter_dimension=0, tiled=True),
        lax.psum_scatter(part_s, "fsdp", scatter_dimension=0, tiled=True),
    )
    grad_w, grad_s = (
        lax.all_gather(part_w, "dp", axis=1, tiled=True),
        lax.all_gather(part_s, "dp", axis=1, tiled=True),
    )
    row_count = grad_w.shape[0]
    block_width = model_width // 2
    block_count = grad_w.shape[1] // block_width
    owned_slots = first_moment.shape[0]
    devices = lax.axis_size("fsdp")
    slot_ids = jnp.arange(owned_slots * devices, dtype=jnp.int32)
    matches = block_slots[None, :] == slot_ids[:, None]
    in_use = jnp.any(matches, axis=1)
    source_block = jnp.sum(
        jnp.where(matches, jnp.arange(block_count, dtype=jnp.int32)[None, :], 0), axis=1
    )
    outgoing = jnp.take(grad_w.reshape(row_count, block_count, block_width), source_block, axis=1)
    outgoing = jnp.where(in_use[None, :, None], outgoing, 0.0).reshape(
        row_count, devices, owned_slots, block_width
    )
    incoming = lax.all_to_all(outgoing, "fsdp", split_axis=1, concat_axis=0, tiled=True).reshape(
        row_count * devices, owned_slots, block_width
    )
    my_use = lax.dynamic_slice_in_dim(in_use, lax.axis_index("fsdp") * owned_slots, owned_slots)
    eigen_turned = jnp.einsum("kdi,dkc->kic", left_bases, incoming, precision=EXACT_PRECISION)
    eigen_turned = jnp.einsum("kic,kcj->kij", eigen_turned, right_bases, precision=EXACT_PRECISION)
    first_new = BETA_FIRST * first_moment + (1.0 - BETA_FIRST) * eigen_turned
    second_new = BETA_SECOND * second_moment + (1.0 - BETA_SECOND) * eigen_turned * eigen_turned
    direction = adam_direction(first_new, second_new)
    rotated_gradient = jnp.einsum("kij,klj->kil", direction, right_bases, precision=EXACT_PRECISION)
    rotated_gradient = jnp.einsum(
        "kdi,kil->dkl", left_bases, rotated_gradient, precision=EXACT_PRECISION
    )
    returned = lax.all_to_all(
        rotated_gradient.reshape(devices, row_count, owned_slots, block_width),
        "fsdp",
        split_axis=0,
        concat_axis=0,
        tiled=True,
    )
    by_slot = jnp.moveaxis(returned, 1, 0).reshape(row_count, devices * owned_slots, block_width)
    update = jnp.take(by_slot, block_slots, axis=1).reshape(row_count, block_count * block_width)
    new_master = master - RATE_MATRIX * update
    new_copy = new_master.astype(jnp.bfloat16)
    keep_slot = my_use[:, None, None]
    new_first = jnp.where(keep_slot, first_new, 0.0)
    new_second = jnp.where(keep_slot, second_new, 0.0)
    new_small_first = BETA_FIRST * small_first + (1.0 - BETA_FIRST) * grad_s
    new_small_second = BETA_SECOND * small_second + (1.0 - BETA_SECOND) * grad_s * grad_s
    new_small = small_params - RATE_VECTOR * adam_direction(new_small_first, new_small_second)
    return (
        out_tokens,
        grad_tokens,
        grad_w,
        grad_s,
        new_first,
        new_second,
        new_master,
        new_copy,
        new_small,
        new_small_first,
        new_small_second,
        loss_accuracy,
        counts,
    )


def solution(mesh):
    return jax.shard_map(
        local,
        mesh=mesh,
        in_specs=(
            P(("dp", "fsdp"), None),
            P(("dp", "fsdp"), None),
            P(("dp", "fsdp")),
            P(("dp", "fsdp")),
            P(),
            P("fsdp", None),
            P("fsdp", None),
            P("fsdp", None),
            P("fsdp", None),
            P(),
            P("fsdp", None, None),
            P("fsdp", None, None),
            P("fsdp", None, None),
            P("fsdp", None, None),
        ),
        out_specs=(
            P(("dp", "fsdp"), None),
            P(("dp", "fsdp"), None),
            P("fsdp", None),
            P("fsdp", None),
            P("fsdp", None, None),
            P("fsdp", None, None),
            P("fsdp", None),
            P("fsdp", None),
            P("fsdp", None),
            P("fsdp", None),
            P("fsdp", None),
            P(),
            P(),
        ),
        check_vma=False,
    )
```

profile of v0, /device:TPU:0, one launch (start us, length us, event | category | flops | bytes accessed | tf_op | source)
XLA Modules:
  0.0 1169.3 jit_solution(2485766205392647652)
XLA Ops:
  7.3 3.8 convert_element_type.121
  11.2 33.4 %all-gather = bf16[8,80,16]{1,2,0:T(8,128)(2,1)S(1)} all-gather(bf16[1,80,16]{1,2,0:T(8,128)(2,1)S(1)} %convert_bitcast_fusion), channel_id=1, replica_groups=mesh['dp'=4,'fsdp'=8] {'fsdp'}, dimensions={0}, use_global_device_ids=true | all-gather | bytes 23040 | tf_op jit(solution)/shard_map/all_gather | solution.py:119
  46.0 190.6 %all-gather.5.cloned.1.call-done = bf16[640,12800]{1,0:T(8,128)(2,1)} async-done(((bf16[80,12800]{1,0:T(8,128)(2,1)}), bf16[640,12800]{1,0:T(8,128)(2,1)}) %all-gather.5.cloned.1.call-update) | async-done | bytes 16384016 | tf_op jit(solution)/shard_map/all_gather | solution.py:118
  236.6 2.8 fusion.29
  239.4 0.9 fusion.87
  240.5 1.3 copy.111
  241.8 2.0 copy.110
  243.8 0.9 multiply_reduce_fusion.1
  244.7 0.9 fusion.15
  245.7 1.1 fusion.45
  247.3 1.9 slice-done.3
  249.2 1.4 slice-done.4
  250.6 1.1 slice-done.5
  252.5 15.0 %multiply_convert_fusion.1 = (bf16[256,5120]{1,0:T(8,128)(2,1)}, f32[256,5120]{1,0:T(8,128)}, f32[256,5120]{1,0:T(8,128)}) fusion(f32[5120]{0:T(1024)S(1)} %add.172, bf16[640,12800]{1,0:T(8,128)(2,1)S(1)} %bitcast.115, f32[256,640]{1,0:T(8,128)S(1)} %get-tuple-element.106, f32[640]{0:T(1024)S(1)} %get-tuple-element.67, f32[640]{0:T(1024)S(1)} %get-tuple-element.68, ...), kind=kOutput, calls=%fused_computation.21 | convolution fusion | flops 1765048320 | bytes 20346880 | tf_op jit(solution)/shard_map/dot_general | solution.py:152
  267.5 6.6 convert_reduce_fusion
  274.1 2.4 multiply_reduce_fusion.2
  276.9 0.9 copy-done.6
  278.0 1.6 fusion.92
  279.5 1.2 convolution_convert_fusion
  280.7 1.9 copy.115
  282.6 3.7 fusion.48
  286.9 1.4 multiply_reduce_fusion
  288.3 1.4 multiply_convert_fusion
  291.4 6.7 fusion.80
  298.1 6.6 convolution_bitcast_fusion
  304.7 3.3 fusion.76
  308.0 21.8 %pad_maximum_fusion = f32[640,12800]{1,0:T(8,128)} fusion(f32[640,5120]{1,0:T(8,128)} %convolution_bitcast_fusion, f32[640,5120]{1,0:T(8,128)} %fusion.80, f32[640,640]{1,0:T(8,128)S(1)} %copy-done.5, f32[640,1920]{1,0:T(8,128)} %fusion.76), kind=kLoop, calls=%fused_computation.2 | loop fusion | flops 24576000 | bytes 65536000 | tf_op jit(solution)/shard_map/concatenate | solution.py:220
  329.9 225.7 %reduce-scatter.5.cloned.1.call-done = f32[640,3200]{1,0:T(8,128)} async-done(((f32[640,12800]{1,0:T(8,128)}), f32[640,3200]{1,0:T(8,128)}) %reduce-scatter.5.cloned.1.call-update) | async-done | bytes 8192016 | tf_op jit(solution)/shard_map/reduce_scatter | solution.py:247
  555.7 149.0 %reduce-scatter.7.cloned.1.call-done = f32[80,3200]{1,0:T(8,128)} async-done(((f32[640,3200]{1,0:T(8,128)}), f32[80,3200]{1,0:T(8,128)}) %reduce-scatter.7.cloned.1.call-update) | async-done | bytes 1024016 | tf_op jit(solution)/shard_map/reduce_scatter | solution.py:251
  705.0 34.2 %all-gather.7.cloned.1.call-done = f32[80,12800]{1,0:T(8,128)} async-done(((f32[80,3200]{1,0:T(8,128)}), f32[80,12800]{1,0:T(8,128)}) %all-gather.7.cloned.1.call-update) | async-done | bytes 4096016 | tf_op jit(solution)/shard_map/all_gather | solution.py:255
  739.2 5.7 reshape.267
  744.9 5.5 copy.130
  750.4 5.5 gather_fusion
  755.9 5.6 bitcast_select_fusion
  761.6 5.5 all-to-all-start
  767.1 109.1 %all-to-all-done = f32[80,8,5,320]{3,0,2,1:T(8,128)} async-done(((f32[80,8,5,320]{3,0,2,1:T(8,128)}), f32[80,8,5,320]{3,0,2,1:T(8,128)}, u32[]{:S(2)}, u32[]{:S(2)}) %all-to-all-start) | async-done | bytes 4096032 | tf_op jit(solution)/shard_map/all_to_all | solution.py:273
  876.2 2.8 copy.131
  879.0 33.4 %fusion.93 = f32[5,320,640]{2,1,0:T(8,128)S(1)} fusion(f32[640,5,320]{2,0,1:T(8,128)S(1)} %bitcast.89, f32[5,640,640]{2,1,0:T(8,128)} %param.28), kind=kOutput, calls=%fused_computation.168 | convolution fusion | flops 7864320000 | bytes 16384000 | tf_op jit(solution)/shard_map/kdi,dkc->kic/dot_general | solution.py:277
  912.4 18.5 %broadcast_select_fusion = (f32[5,640,320]{1,2,0:T(8,128)}, f32[5,640,320]{1,2,0:T(8,128)}, f32[5,640,320]{1,2,0:T(8,128)}) fusion(pred[5]{0:T(512)(128)(4,1)S(1)} %dynamic_slice.21, f32[5,640,320]{1,2,0:T(8,128)} %param.27, f32[5,640,320]{1,2,0:T(8,128)} %param.26, f32[5,320,640]{2,1,0:T(8,128)S(1)} %fusion.93, f32[5,320,320]{2,1,0:T(8,128)S(1)} %copy-done), kind=kOutput, calls=%fused_computation.61 | convolution fusion | flops 3940352000 | bytes 26624004 | tf_op jit(solution)/shard_map/kic,kcj->kij/dot_general | solution.py:278
  930.9 19.0 %fusion.17 = f32[5,640,320]{1,2,0:T(8,128)S(1)} fusion(f32[5,320,320]{2,1,0:T(8,128)S(1)} %copy-done, f32[5,640,320]{1,2,0:T(8,128)} %get-tuple-element.114, f32[5,640,320]{1,2,0:T(8,128)} %param.26, f32[5,640,320]{1,2,0:T(8,128)} %param.27), kind=kOutput, calls=%fused_computation.42 | convolution fusion | flops 3942400000 | bytes 18432000 | tf_op jit(solution)/shard_map/kij,klj->kil/dot_general | solution.py:282
  950.0 20.1 %convolution_bitcast_fusion.1 = f32[640,5,320]{0,2,1:T(8,128)} fusion(f32[5,640,320]{1,2,0:T(8,128)S(1)} %fusion.17, f32[5,640,640]{2,1,0:T(8,128)S(1)} %bitcast.87), kind=kOutput, calls=%fused_computation.58 | convolution fusion | flops 7864320000 | bytes 16384000 | tf_op jit(solution)/shard_map/kdi,kil->dkl/dot_general | solution.py:283
  970.2 6.6 copy.134
  976.7 4.9 copy.135
  981.7 4.7 all-to-all-start.1
  988.0 0.9 reshape.266
  989.8 0.9 stack.38
  991.6 1.6 convert_reduce_fusion.1
  994.0 3.1 fusion.81
  997.6 1.1 convert_reduce_fusion.3
  998.8 0.9 stack.39
  1002.3 2.3 concatenate.21
  1004.6 15.0 %all-reduce = f32[640,16]{1,0:T(8,128)} all-reduce(f32[640,16]{1,0:T(8,128)S(1)} %concatenate.21), channel_id=4, replica_groups=mesh['dp'=4,'fsdp'=8] {'dp'}, use_global_device_ids=true, to_apply=%region_21.22.clone | all-reduce | flops 10240 | bytes 81920
  1019.6 1.8 constant_dynamic-slice_fusion
  1021.5 5.9 fusion.42
  1029.3 88.3 %all-reduce.1 = (f32[4]{0:T(128)S(1)}, f32[5]{0:T(128)S(1)}) all-reduce(f32[4]{0:T(128)S(1)} %get-tuple-element.77, f32[5]{0:T(128)S(1)} %pad_maximum_fusion.3), channel_id=1, replica_groups=mesh['dp'=4,'fsdp'=8] {'dp','fsdp'}, use_global_device_ids=true, to_apply=%region_33.35 | all-reduce | flops 9 | bytes 72 | tf_op jit(solution)/shard_map/psum | solution.py:176
  1117.6 1.1 fusion.89
  1120.0 8.9 reduce-scatter.9.cloned.1.call-done
  1129.7 5.2 all-gather.1
  1135.5 5.5 gather_fusion.1
  1141.0 3.0 bitcast_multiply_fusion
  1144.1 3.7 copy.136
  1147.8 5.5 mul.298
  1153.3 6.7 fusion.83
  1160.0 2.0 copy.148
  (153 shorter events, 17.4 us)
Async XLA Ops:
  7.2 905.2 %copy-start = (f32[5,320,320]{2,1,0:T(8,128)S(1)}, f32[5,320,320]{2,1,0:T(8,128)}, u32[]{:S(2)}) copy-start(f32[5,320,320]{2,1,0:T(8,128)} %param.29) | copy-start | bytes 6144004
  7.2 4.0 copy-start.25
  7.2 38.5 %copy-start.4 = (bf16[256,640]{1,0:T(8,128)(2,1)S(1)}, bf16[256,640]{1,0:T(8,128)(2,1)}, u32[]{:S(2)}) copy-start(bf16[256,640]{1,0:T(8,128)(2,1)} %param.16) | copy-start | bytes 983044
  7.2 229.4 %all-gather.5.cloned.1.call-start = ((), (), s32[]{:S(2)}) async-start(), calls=%async_computation.5 | async-start | bytes 18432000 | tf_op jit(solution)/shard_map/all_gather | solution.py:118
  11.1 544.6 %reduce-scatter.5.cloned.1.call-start = ((), (), s32[]{:S(2)}) async-start(), calls=%async_computation.6 | async-start | bytes 40960000 | tf_op jit(solution)/shard_map/reduce_scatter | solution.py:247
  46.0 198.6 %copy-start.27 = (f32[256]{0:T(256)}, f32[256]{0:T(256)S(1)}, u32[]{:S(2)}) copy-start(f32[256]{0:T(256)S(1)} %fusion.63) | copy-start | bytes 3076
  240.5 5.1 copy-start.12
  241.7 3.9 copy-start.14
  243.8 1.9 copy-start.22
  243.8 3.6 slice-start.2
  244.7 2.7 copy-start.1
  244.7 4.5 slice-start.3
  245.6 4.9 slice-start.4
  245.7 6.0 slice-start.5
  252.5 15.0 %copy-start.16 = (bf16[256,640]{1,0:T(8,128)(2,1)S(1)}, bf16[256,640]{1,0:T(8,128)(2,1)}, u32[]{:S(2)}) copy-start(bf16[256,640]{1,0:T(8,128)(2,1)} %param.17) | copy-start | bytes 983044
  274.1 2.4 copy-start.19
  276.9 0.9 copy-start.6
  282.6 4.1 copy-start.2
  282.6 4.2 copy-start.9
  282.6 4.3 copy-start.23
  286.9 17.8 %copy-start.8 = (bf16[20,32,256]{2,1,0:T(8,128)(2,1)}, bf16[20,32,256]{2,1,0:T(8,128)(2,1)S(1)}, u32[]{:S(2)}) copy-start(bf16[20,32,256]{2,1,0:T(8,128)(2,1)S(1)} %fusion.48) | copy-start | bytes 983044
  288.2 1.4 copy-start.15
  288.2 2.3 copy-start.13
  289.7 1.7 copy-start.20
  290.6 14.1 %copy-start.10 = (bf16[20,32,256]{2,1,0:T(8,128)(2,1)}, bf16[20,32,256]{2,1,0:T(8,128)(2,1)S(1)}, u32[]{:S(2)}) copy-start(bf16[20,32,256]{2,1,0:T(8,128)(2,1)S(1)} %fusion.47) | copy-start | bytes 983044
  291.4 13.3 %copy-start.11 = (bf16[20,32,256]{2,1,0:T(8,128)(2,1)}, bf16[20,32,256]{2,1,0:T(8,128)(2,1)S(1)}, u32[]{:S(2)}) copy-start(bf16[20,32,256]{2,1,0:T(8,128)(2,1)S(1)} %fusion.46) | copy-start | bytes 983044
  291.4 6.7 copy-start.17
  291.4 6.7 copy-start.21
  304.7 3.3 copy-start.5
  329.9 374.9 %copy-start.35 = (s32[40]{0:T(128)S(1)}, s32[40]{0:T(128)}, u32[]{:S(2)}) copy-start(s32[40]{0:T(128)} %param.25) | copy-start | bytes 484
  329.9 374.8 %reduce-scatter.7.cloned.1.call-start = ((), (), s32[]{:S(2)}) async-start(), calls=%async_computation.7 | async-start | bytes 9216000 | tf_op jit(solution)/shard_map/reduce_scatter | solution.py:251
  555.7 183.5 %all-gather.7.cloned.1.call-start = ((), (), s32[]{:S(2)}) async-start(), calls=%async_computation.8 | async-start | bytes 5120000 | tf_op jit(solution)/shard_map/all_gather | solution.py:255
  761.6 114.7 %all-to-all-start = ((f32[80,8,5,320]{3,0,2,1:T(8,128)}), f32[80,8,5,320]{3,0,2,1:T(8,128)}, u32[]{:S(2)}, u32[]{:S(2)}) async-start(f32[80,8,5,320]{3,0,2,1:T(8,128)} %bitcast.88), calls=%async_computation.3 | async-start | bytes 9830400 | tf_op jit(solution)/shard_map/all_to_all | solution.py:273
  879.0 71.0 %slice-start = ((s8[8192000]{0:T(1024)(128)(4,1)}), s8[4194304]{0:T(1024)(128)(4,1)S(1)}, s32[]{:S(2)}) async-start(s8[8192000]{0:T(1024)(128)(4,1)} %bitcast.86), calls=%async_computation.10 | async-start | bytes 8388608
  912.4 37.6 %slice-start.1 = ((s8[8192000]{0:T(1024)(128)(4,1)}), s8[3997696]{0:T(1024)(128)(4,1)S(1)}, s32[]{:S(2)}) async-start(s8[8192000]{0:T(1024)(128)(4,1)} %bitcast.86), calls=%async_computation.11 | async-start | bytes 7995392
  981.7 5.0 copy-start.32
  981.7 5.0 copy-start.36
  981.7 153.8 %all-to-all-start.1 = ((f32[8,80,5,320]{3,1,2,0:T(8,128)}), f32[8,80,5,320]{3,1,2,0:T(8,128)}, u32[]{:S(2)}, u32[]{:S(2)}) async-start(f32[8,80,5,320]{3,1,2,0:T(8,128)} %copy.135), calls=%async_computation.4 | async-start | bytes 9830400 | tf_op jit(solution)/shard_map/all_to_all | solution.py:286
  986.4 142.4 %reduce-scatter.9.cloned.1.call-start = ((), (), s32[]{:S(2)}) async-start(), calls=%async_computation.9 | async-start | bytes 368640 | tf_op jit(solution)/shard_map/reduce_scatter | solution.py:252
  988.9 8.3 copy-start.28
  991.6 6.1 copy-start.7
  991.6 6.1 copy-start.18
  997.2 24.3 %copy-start.34 = (f32[640]{0:T(1024)S(1)}, f32[640]{0:T(1024)}, u32[]{:S(2)}) copy-start(f32[640]{0:T(1024)} %get-tuple-element.66) | copy-start | bytes 7684
  1021.5 6.0 copy-start.31
  1021.5 6.3 copy-start.33
  1021.5 113.4 %copy-start.26 = (f32[80,16]{0,1:T(8,128)S(1)}, f32[80,16]{0,1:T(8,128)}, u32[]{:S(2)}) copy-start(f32[80,16]{0,1:T(8,128)} %param.22) | copy-start | bytes 15364
  1021.5 113.4 %copy-start.29 = (f32[80,16]{0,1:T(8,128)S(1)}, f32[80,16]{0,1:T(8,128)}, u32[]{:S(2)}) copy-start(f32[80,16]{0,1:T(8,128)} %param.23) | copy-start | bytes 15364
  1021.5 113.4 %copy-start.30 = (f32[80,16]{0,1:T(8,128)S(1)}, f32[80,16]{0,1:T(8,128)}, u32[]{:S(2)}) copy-start(f32[80,16]{0,1:T(8,128)} %param.24) | copy-start | bytes 15364
  1027.5 116.6 %copy-start.24 = (bf16[256,640]{1,0:T(8,128)(2,1)}, bf16[256,640]{1,0:T(8,128)(2,1)S(1)}, u32[]{:S(2)}) copy-start(bf16[256,640]{1,0:T(8,128)(2,1)S(1)} %fusion.42) | copy-start | bytes 983044
  1153.3 6.7 copy-start.3
Sparse Core Ops, SparseCore 0:
  11.2 225.3 all-gather.4
  330.0 225.6 reduce-scatter.4
  559.4 145.2 reduce-scatter.6
  706.1 32.9 all-gather.6
  1021.6 107.2 reduce-scatter.8
where the time goes:
time: 1180 us; the launch traced here: 1170 us
  waiting for transfers between devices  717 us (61%)
  matrix products  156 us (13%)
  blocking collectives  142 us (12%)
  local copies, waits for them, and re-layouts  76.1 us (6%)
  other arithmetic  51.6 us (4%)
  between operations  16 us (1%)
    reduce_scatter x1, waiting for transfers between devices, local(): lax.psum_scatter(grad_w_local, 'dp', scatter_dimension=1, tiled=True)  226 us
    all_gather x1, waiting for transfers between devices, local(): lax.all_gather(local_weights, 'fsdp', axis=0, tiled=True)  191 us
    reduce_scatter x1, waiting for transfers between devices, local(): lax.psum_scatter(part_w, 'fsdp', scatter_dimension=0, tiled=True)  149 us
    all_to_all x1, waiting for transfers between devices, local(): lax.all_to_all(outgoing, 'fsdp', split_axis=1, concat_axis=0, tiled=True)  109 us
    psum x1, blocking collectives, local(): lax.psum((local_sums, jnp.sum(chosen, axis=0)), ('dp', 'fsdp'))  88.3 us
    all_gather x1, waiting for transfers between devices, local(): lax.all_gather(part_w, 'dp', axis=1, tiled=True)  34.2 us
    all_gather x1, blocking collectives, local(): lax.all_gather(local_small, 'fsdp', axis=0, tiled=True)  33.4 us
    dot_general x1, matrix products, local(): jnp.einsum('kdi,dkc->kic', left_bases, incoming, precision=EXACT_PRECISION)  33.4 us
  transfers between devices with their start and end apart: 7, of which 6 were waited for; matrix products, arithmetic and copies ran while one was open for 3% of the time, Pallas kernels for 0%

commit v1 on v0

--- a/solution.py
+++ b/solution.py
@@ -112,13 +112,13 @@
     hidden = (master.shape[1] - 4 * model_width) // 2
     heads_count = model_width // HEAD_DIM
     token_count = tokens.shape[0]
-    local_weights = master.astype(jnp.bfloat16)
-    local_small = small_params.astype(jnp.bfloat16)
-    weights, small_all = (
-        lax.all_gather(local_weights, "fsdp", axis=0, tiled=True),
-        lax.all_gather(local_small, "fsdp", axis=0, tiled=True),
-    )
-    params = small_all.astype(jnp.float32)
+    weight_cols = master.shape[1]
+    packed_local = jnp.concatenate(
+        [master.astype(jnp.bfloat16), small_params.astype(jnp.bfloat16)], axis=1
+    )
+    packed = lax.all_gather(packed_local, "fsdp", axis=0, tiled=True)
+    weights = packed[:, :weight_cols]
+    params = packed[:, weight_cols:].astype(jnp.float32)
     gain_one, shift_one, bias_query, bias_value, bias_output, gain_two, shift_two, bias_down = [
         params[:, column] for column in range(8)
     ]
@@ -181,11 +181,8 @@
         ]
     )
     counts = global_counts.astype(jnp.int32)
-    weights_back, small_back = (
-        lax.all_gather(local_weights, "fsdp", axis=0, tiled=True),
-        lax.all_gather(local_small, "fsdp", axis=0, tiled=True),
-    )
-    params_back = small_back.astype(jnp.float32)
+    weights_back = weights
+    params_back = params
     back_rows = cotangent.astype(jnp.float32)
     d_active = jnp.dot(
         cotangent, weights_back[:, 4 * model_width + hidden :], preferred_element_type=jnp.float32
@@ -243,18 +240,25 @@
     grad_s_local = jnp.concatenate(
         [small_cols, jnp.sum(d_pre.astype(jnp.float32), axis=0).reshape(model_width, -1)], axis=1
     )
-    part_w, part_s = (
-        lax.psum_scatter(grad_w_local, "dp", scatter_dimension=1, tiled=True),
-        lax.psum_scatter(grad_s_local, "dp", scatter_dimension=1, tiled=True),
-    )
-    part_w, part_s = (
-        lax.psum_scatter(part_w, "fsdp", scatter_dimension=0, tiled=True),
-        lax.psum_scatter(part_s, "fsdp", scatter_dimension=0, tiled=True),
-    )
-    grad_w, grad_s = (
-        lax.all_gather(part_w, "dp", axis=1, tiled=True),
-        lax.all_gather(part_s, "dp", axis=1, tiled=True),
-    )
+    replicas = lax.axis_size("dp")
+    small_cols = grad_s_local.shape[1]
+    chunk_w = weight_cols // replicas
+    chunk_s = small_cols // replicas
+    pad_s = 128 - chunk_s
+    joined = jnp.concatenate(
+        [
+            grad_w_local.reshape(-1, replicas, chunk_w),
+            grad_s_local.reshape(-1, replicas, chunk_s),
+            jnp.zeros((grad_w_local.shape[0], replicas, pad_s), jnp.float32),
+        ],
+        axis=2,
+    ).reshape(grad_w_local.shape[0], -1).astype(jnp.bfloat16)
+    joined = lax.psum_scatter(joined, "dp", scatter_dimension=1, tiled=True)
+    joined = lax.psum_scatter(joined, "fsdp", scatter_dimension=0, tiled=True)
+    joined = lax.all_gather(joined, "dp", axis=1, tiled=True).astype(jnp.float32)
+    joined = joined.reshape(joined.shape[0], replicas, chunk_w + chunk_s + pad_s)
+    grad_w = joined[:, :, :chunk_w].reshape(joined.shape[0], weight_cols)
+    grad_s = joined[:, :, chunk_w : chunk_w + chunk_s].reshape(joined.shape[0], small_cols)
     row_count = grad_w.shape[0]
     block_width = model_width // 2
     block_count = grad_w.shape[1] // block_width
@@ -270,9 +274,9 @@
     outgoing = jnp.where(in_use[None, :, None], outgoing, 0.0).reshape(
         row_count, devices, owned_slots, block_width
     )
-    incoming = lax.all_to_all(outgoing, "fsdp", split_axis=1, concat_axis=0, tiled=True).reshape(
-        row_count * devices, owned_slots, block_width
-    )
+    incoming = lax.all_to_all(
+        outgoing.astype(jnp.bfloat16), "fsdp", split_axis=1, concat_axis=0, tiled=True
+    ).reshape(row_count * devices, owned_slots, block_width).astype(jnp.float32)
     my_use = lax.dynamic_slice_in_dim(in_use, lax.axis_index("fsdp") * owned_slots, owned_slots)
     eigen_turned = jnp.einsum("kdi,dkc->kic", left_bases, incoming, precision=EXACT_PRECISION)
     eigen_turned = jnp.einsum("kic,kcj->kij", eigen_turned, right_bases, precision=EXACT_PRECISION)
@@ -284,12 +288,14 @@
         "kdi,kil->dkl", left_bases, rotated_gradient, precision=EXACT_PRECISION
     )
     returned = lax.all_to_all(
-        rotated_gradient.reshape(devices, row_count, owned_slots, block_width),
+        rotated_gradient.reshape(devices, row_count, owned_slots, block_width).astype(
+            jnp.bfloat16
+        ),
         "fsdp",
         split_axis=0,
         concat_axis=0,
         tiled=True,
-    )
+    ).astype(jnp.float32)
     by_slot = jnp.moveaxis(returned, 1, 0).reshape(row_count, devices * owned_slots, block_width)
     update = jnp.take(by_slot, block_slots, axis=1).reshape(row_count, block_count * block_width)
     new_master = master - RATE_MATRIX * update

time: 1180 us -> 981 us (0.83)
  waiting for transfers between devices: 717 us -> 525 us
  local copies, waits for them, and re-layouts: 76.1 us -> 162 us
  blocking collectives: 142 us -> 67.1 us
  matrix products: 156 us -> 140 us
    reduce_scatter x3 -> x2, waiting for transfers between devices: 384 us -> 219 us  [the longest x1 125 us: local(): joined = lax.psum_scatter(joined, 'dp', scatter_dimension=1, tiled=True)]
    all_to_all x1, waiting for transfers between devices: 109 us -> 56.3 us  [local(): lax.all_to_all(outgoing.astype(jnp.bfloat16), 'fsdp', split_axis=1, conca...]
    concatenate x0 -> x1, local copies, waits for them, and re-layouts: none -> 46.6 us  [local(): jnp.concatenate([grad_w_local.reshape(-1, replicas, chunk_w), grad_s_loca...]
    all_gather x2 -> x0, blocking collectives: 38.6 us -> none  [the longest x1 33.4 us: local(): lax.all_gather(local_small, 'fsdp', axis=0, tiled=True)]
    all_gather x2, waiting for transfers between devices: 225 us -> 250 us  [the longest x1 227 us: local(): packed = lax.all_gather(packed_local, 'fsdp', axis=0, tiled=True)]
    psum x1, blocking collectives: 88.3 us -> 67.1 us  [local(): lax.psum((local_sums, jnp.sum(chosen, axis=0)), ('dp', 'fsdp'))]
    reshape x3 -> x4, local copies, waits for them, and re-layouts: 16.2 us -> 34 us  [the longest x1 27.5 us: local(): grad_w_local.reshape(-1, replicas, chunk_w)]
    dot_general x1, matrix products: 33.4 us -> 16.4 us  [local(): jnp.einsum('kdi,dkc->kic', left_bases, incoming, precision=EXACT_PRECISION)]
  transfers between devices with their start and end apart: 7 -> 6, of which waited for: 6 -> 5; matrix products, arithmetic and copies ran while one was open for 3% -> 2% of each run, Pallas kernels for 0% -> 0%
where the time goes in v1:
time: 981 us; the launch traced here: 969 us
  waiting for transfers between devices  525 us (54%)
  local copies, waits for them, and re-layouts  162 us (17%)
  matrix products  140 us (14%)
  blocking collectives  67.1 us (7%)
  other arithmetic  49 us (5%)
  between operations  15.6 us (2%)
  starting transfers between devices  10.3 us (1%)
    all_gather x1, waiting for transfers between devices, local(): packed = lax.all_gather(packed_local, 'fsdp', axis=0, tiled=True)  227 us
    reduce_scatter x1, waiting for transfers between devices, local(): joined = lax.psum_scatter(joined, 'dp', scatter_dimension=1, tiled=True)  125 us
    reduce_scatter x1, waiting for transfers between devices, local(): joined = lax.psum_scatter(joined, 'fsdp', scatter_dimension=0, tiled=True)  93.8 us
    psum x1, blocking collectives, local(): lax.psum((local_sums, jnp.sum(chosen, axis=0)), ('dp', 'fsdp'))  67.1 us
    all_to_all x1, waiting for transfers between devices, local(): lax.all_to_all(outgoing.astype(jnp.bfloat16), 'fsdp', split_axis=1, conca...  56.3 us
    concatenate x1, local copies, waits for them, and re-layouts, local(): jnp.concatenate([grad_w_local.reshape(-1, replicas, chunk_w), grad_s_loca...  46.6 us
    reshape x1, local copies, waits for them, and re-layouts, local(): grad_w_local.reshape(-1, replicas, chunk_w)  27.5 us
    unnamed x78, local copies, waits for them, and re-layouts  24 us
  transfers between devices with their start and end apart: 6, of which 5 were waited for; matrix products, arithmetic and copies ran while one was open for 2% of the time, Pallas kernels for 0%

profile of v1, /device:TPU:0, one launch (start us, length us, event | category | flops | bytes accessed | tf_op | source)
XLA Modules:
  0.0 969.2 jit_solution(11507424296923593817)
XLA Ops:
  8.2 2.4 convert_element_type.139
  10.6 1.4 pad_maximum_fusion.1
  12.5 226.9 %all-gather.3.cloned.1.call-done = bf16[640,12816]{1,0:T(8,128)(2,1)} async-done(((bf16[80,12816]{1,0:T(8,128)(2,1)}), bf16[640,12816]{1,0:T(8,128)(2,1)}) %all-gather.3.cloned.1.call-update) | async-done | bytes 16404496 | tf_op jit(solution)/shard_map/all_gather | solution.py:119
  239.4 0.9 slice_convert_fusion
  240.4 1.9 slice_reduce_fusion
  243.1 2.8 fusion.30
  246.7 0.9 copy.180
  247.8 1.3 copy.182
  250.0 0.9 fusion.16
  251.0 1.4 copy-done.1
  252.3 1.8 fusion.46
  254.3 2.0 fusion.91
  256.6 16.7 %multiply_convert_fusion.1 = (bf16[256,5120]{1,0:T(8,128)(2,1)}, f32[256,5120]{1,0:T(8,128)}, f32[256,5120]{1,0:T(8,128)}) fusion(f32[5120]{0:T(1024)S(1)} %add.168, bf16[640,12816]{1,0:T(8,128)(2,1)} %all-gather.3.cloned.1.call-done, f32[256,640]{1,0:T(8,128)S(1)} %get-tuple-element.105, f32[640]{0:T(1024)S(1)} %get-tuple-element.67, ...), kind=kOutput, calls=%fused_computation.22 | convolution fusion | flops 1765048320 | bytes 20343808 | tf_op jit(solution)/shard_map/dot_general | solution.py:152
  273.3 6.3 fusion.92
  279.7 2.4 multiply_reduce_fusion.2
  284.2 1.2 convolution_convert_fusion.4
  285.3 1.9 copy.184
  287.2 3.7 fusion.49
  291.0 4.0 multiply_reduce_fusion
  295.0 1.4 multiply_convert_fusion
  298.2 4.8 convolution_convert_fusion.1
  302.9 1.4 convolution_convert_fusion.3
  304.3 2.5 convolution_convert_fusion.2
  307.1 3.8 fusion.81
  311.0 5.1 fusion
  316.1 2.2 copy.189
  318.3 13.2 %pad_maximum_fusion = bf16[640,12800]{1,0:T(8,128)(2,1)} fusion(bf16[640,5120]{1,0:T(8,128)(2,1)} %fusion, bf16[640,5120]{1,0:T(8,128)(2,1)} %convolution_convert_fusion.1, bf16[640,640]{1,0:T(8,128)(2,1)} %copy.189, bf16[640,1920]{1,0:T(8,128)(2,1)} %convolution_convert_fusion.2), kind=kLoop, calls=%fused_computation.2 | loop fusion | flops 65536000 | bytes 32768000 | tf_op jit(solution)/shard_map/concatenate | solution.py:217
  331.5 27.5 %reshape.287 = bf16[640,4,3200]{2,1,0:T(4,128)(2,1)} reshape(bf16[640,12800]{1,0:T(8,128)(2,1)} %pad_maximum_fusion) | data formatting | bytes 32768000 | tf_op jit(solution)/shard_map/reshape | solution.py:250
  358.9 1.5 fusion.63
  361.4 1.0 copy.190
  362.5 1.2 copy.191
  363.7 1.0 broadcast_in_dim.119
  364.7 46.6 %concatenate.32 = bf16[640,4,3328]{2,1,0:T(4,128)(2,1)} concatenate(bf16[640,4,3200]{2,1,0:T(4,128)(2,1)} %reshape.287, bf16[640,4,4]{2,1,0:T(4,128)(2,1)} %copy.191, bf16[640,4,124]{2,1,0:T(4,128)(2,1)} %broadcast_in_dim.119), dimensions={2} | concatenate | bytes 34078720 | tf_op jit(solution)/shard_map/concatenate | solution.py:248
  411.4 15.5 %copy.207 = bf16[80,8,4,3328]{3,1,2,0:T(8,128)(2,1)} copy(bf16[80,8,4,3328]{3,2,1,0:T(4,128)(2,1)} %bitcast.89) | data formatting | bytes 34078720
  426.9 124.9 %reduce-scatter.3.cloned.1.call-done = bf16[640,3328]{1,0:T(8,128)(2,1)} async-done(((bf16[640,13312]{1,0:T(8,128)(2,1)}), bf16[640,3328]{1,0:T(8,128)(2,1)}) %reduce-scatter.3.cloned.1.call-update) | async-done | bytes 4259856 | tf_op jit(solution)/shard_map/reduce_scatter | solution.py:256
  551.8 93.8 %reduce-scatter.5.cloned.1.call-done = bf16[80,3328]{1,0:T(8,128)(2,1)} async-done(((bf16[640,3328]{1,0:T(8,128)(2,1)}), bf16[80,3328]{1,0:T(8,128)(2,1)}) %reduce-scatter.5.cloned.1.call-update) | async-done | bytes 532496 | tf_op jit(solution)/shard_map/reduce_scatter | solution.py:257
  645.9 23.5 %all-gather.5.cloned.1.call-done = bf16[80,13312]{1,0:T(8,128)(2,1)} async-done(((bf16[80,3328]{1,0:T(8,128)(2,1)}), bf16[80,13312]{1,0:T(8,128)(2,1)}) %all-gather.5.cloned.1.call-update) | async-done | bytes 2129936 | tf_op jit(solution)/shard_map/all_gather | solution.py:258
  669.5 5.3 reshape.298
  674.8 4.4 slice.128
  679.2 6.4 reshape_reshape.3
  685.5 3.4 copy.193
  689.0 4.2 gather_fusion
  693.2 4.4 fusion.15
  697.6 5.7 all-to-all-start
  703.5 56.3 %all-to-all-done = bf16[80,8,5,320]{3,0,2,1:T(8,128)(2,1)} async-done(((bf16[80,8,5,320]{3,0,2,1:T(8,128)(2,1)}), bf16[80,8,5,320]{3,0,2,1:T(8,128)(2,1)}, u32[]{:S(2)}, u32[]{:S(2)}) %all-to-all-start) | async-done | bytes 2048032 | tf_op jit(solution)/shard_map/all_to_all | solution.py:277
  759.8 1.9 copy.194
  761.7 16.4 %fusion.94 = f32[5,320,640]{2,1,0:T(8,128)S(1)} fusion(bf16[640,5,320]{2,0,1:T(8,128)(2,1)S(1)} %bitcast.94, f32[5,640,640]{2,1,0:T(8,128)} %param.28), kind=kOutput, calls=%fused_computation.169 | convolution fusion | flops 7864320000 | bytes 14336000 | tf_op jit(solution)/shard_map/kdi,dkc->kic/dot_general | solution.py:281
  778.2 18.3 %broadcast_select_fusion = (f32[5,640,320]{1,2,0:T(8,128)}, f32[5,640,320]{1,2,0:T(8,128)}, f32[5,640,320]{1,2,0:T(8,128)}) fusion(pred[5]{0:T(512)(128)(4,1)S(1)} %dynamic_slice.21, f32[5,640,320]{1,2,0:T(8,128)} %param.27, f32[5,640,320]{1,2,0:T(8,128)} %param.26, f32[5,320,640]{2,1,0:T(8,128)S(1)} %fusion.94, f32[5,320,320]{2,1,0:T(8,128)S(1)} %copy-done), kind=kOutput, calls=%fused_computation.65 | convolution fusion | flops 3940352000 | bytes 26624004 | tf_op jit(solution)/shard_map/kic,kcj->kij/dot_general | solution.py:282
  796.5 19.0 %fusion.18 = f32[5,640,320]{1,2,0:T(8,128)S(1)} fusion(f32[5,320,320]{2,1,0:T(8,128)S(1)} %copy-done, f32[5,640,320]{1,2,0:T(8,128)} %get-tuple-element.113, f32[5,640,320]{1,2,0:T(8,128)} %param.26, f32[5,640,320]{1,2,0:T(8,128)} %param.27), kind=kOutput, calls=%fused_computation.44 | convolution fusion | flops 3942400000 | bytes 18432000 | tf_op jit(solution)/shard_map/kij,klj->kil/dot_general | solution.py:286
  815.6 19.7 %convert_bitcast_fusion = bf16[640,5,320]{0,2,1:T(8,128)(2,1)} fusion(f32[5,640,320]{1,2,0:T(8,128)S(1)} %fusion.18, f32[5,640,640]{2,1,0:T(8,128)S(1)} %bitcast.92), kind=kOutput, calls=%fused_computation.62 | convolution fusion | flops 7865344000 | bytes 14336000 | tf_op jit(solution)/shard_map/kdi,kil->dkl/dot_general | solution.py:287
  835.2 4.9 copy.197
  840.1 3.5 copy.198
  843.6 4.4 all-to-all-start.1
  848.1 5.9 fusion.43
  856.5 67.1 %all-reduce = (f32[4]{0:T(128)S(1)}, f32[5]{0:T(128)S(1)}) all-reduce(f32[4]{0:T(128)S(1)} %get-tuple-element.77, f32[5]{0:T(128)S(1)} %pad_maximum_fusion.4), channel_id=1, replica_groups=mesh['dp'=4,'fsdp'=8] {'dp','fsdp'}, use_global_device_ids=true, to_apply=%region_31.33 | all-reduce | flops 9 | bytes 72 | tf_op jit(solution)/shard_map/psum | solution.py:176
  923.6 1.1 fusion.90
  926.0 2.5 add_convert_fusion.1
  928.5 4.4 copy.208
  933.7 4.2 reshape.301
  937.9 5.5 gather_fusion.1
  943.4 3.1 bitcast_multiply_fusion
  946.4 3.7 copy.199
  950.1 5.5 mul.298
  955.7 6.5 fusion.83
  (148 shorter events, 14.3 us)
Async XLA Ops:
  7.2 771.0 %copy-start = (f32[5,320,320]{2,1,0:T(8,128)S(1)}, f32[5,320,320]{2,1,0:T(8,128)}, u32[]{:S(2)}) copy-start(f32[5,320,320]{2,1,0:T(8,128)} %param.29) | copy-start | bytes 6144004
  7.2 232.2 %all-gather.3.cloned.1.call-start = ((), (), s32[]{:S(2)}) async-start(), calls=%async_computation.4 | async-start | bytes 18616320 | tf_op jit(solution)/shard_map/all_gather | solution.py:119
  8.2 3.9 copy-start.3
  12.1 539.7 %reduce-scatter.3.cloned.1.call-start = ((), (), s32[]{:S(2)}) async-start(), calls=%async_computation.5 | async-start | bytes 21299200 | tf_op jit(solution)/shard_map/reduce_scatter | solution.py:256
  247.8 3.1 copy-start.6
  249.1 1.9 copy-start.8
  249.1 3.2 copy-start.14
  250.0 2.3 copy-start.1
  252.3 1.8 copy-start.16
  254.3 18.9 %slice-start.5 = ((s8[16547840]{0:T(1024)(128)(4,1)}), s8[4194304]{0:T(1024)(128)(4,1)S(1)}, s32[]{:S(2)}) async-start(s8[16547840]{0:T(1024)(128)(4,1)} %bitcast.119), calls=%async_computation.13 | async-start | bytes 8388608
  256.5 16.7 %copy-start.10 = (bf16[256,640]{1,0:T(8,128)(2,1)S(1)}, bf16[256,640]{1,0:T(8,128)(2,1)}, u32[]{:S(2)}) copy-start(bf16[256,640]{1,0:T(8,128)(2,1)} %param.17) | copy-start | bytes 983044
  256.6 16.7 %slice-start.6 = ((s8[16547840]{0:T(1024)(128)(4,1)}), s8[4194304]{0:T(1024)(128)(4,1)S(1)}, s32[]{:S(2)}) async-start(s8[16547840]{0:T(1024)(128)(4,1)} %bitcast.119), calls=%async_computation.14 | async-start | bytes 8388608
  256.6 16.7 %slice-start.7 = ((s8[16547840]{0:T(1024)(128)(4,1)}), s8[4194304]{0:T(1024)(128)(4,1)S(1)}, s32[]{:S(2)}) async-start(s8[16547840]{0:T(1024)(128)(4,1)} %bitcast.119), calls=%async_computation.15 | async-start | bytes 8388608
  256.6 16.7 %slice-start.8 = ((s8[16547840]{0:T(1024)(128)(4,1)}), s8[3964928]{0:T(1024)(128)(4,1)S(1)}, s32[]{:S(2)}) async-start(s8[16547840]{0:T(1024)(128)(4,1)} %bitcast.119), calls=%async_computation.16 | async-start | bytes 7929856
  279.6 2.4 copy-start.12
  282.3 0.8 copy-start.2
  283.4 0.7 copy-start.17
  287.2 3.7 copy-start.5
  287.2 3.7 copy-start.15
  287.2 7.7 slice-start
  291.0 4.0 slice-start.1
  295.0 1.4 copy-start.7
  295.0 2.3 copy-start.9
  296.4 1.7 copy-start.13
  298.2 4.8 copy-start.18
  298.2 4.8 copy-start.20
  306.8 4.1 copy-start.4
  306.8 4.1 copy-start.11
  426.8 218.8 %copy-start.29 = (s32[40]{0:T(128)S(1)}, s32[40]{0:T(128)}, u32[]{:S(2)}) copy-start(s32[40]{0:T(128)} %param.25) | copy-start | bytes 484
  426.8 218.8 %reduce-scatter.5.cloned.1.call-start = ((), (), s32[]{:S(2)}) async-start(), calls=%async_computation.6 | async-start | bytes 4792320 | tf_op jit(solution)/shard_map/reduce_scatter | solution.py:257
  551.8 117.7 %all-gather.5.cloned.1.call-start = ((), (), s32[]{:S(2)}) async-start(), calls=%async_computation.7 | async-start | bytes 2662400 | tf_op jit(solution)/shard_map/all_gather | solution.py:258
  693.2 10.2 %copy-start.27 = (s32[256]{0:T(256)S(1)}, s32[256]{0:T(256)}, u32[]{:S(2)}) copy-start(s32[256]{0:T(256)} %param.18) | copy-start | bytes 3076
  697.6 62.1 %all-to-all-start = ((bf16[80,8,5,320]{3,0,2,1:T(8,128)(2,1)}), bf16[80,8,5,320]{3,0,2,1:T(8,128)(2,1)}, u32[]{:S(2)}, u32[]{:S(2)}) async-start(bf16[80,8,5,320]{3,0,2,1:T(8,128)(2,1)} %bitcast.95), calls=%async_computation.2 | async-start | bytes 4915200 | tf_op jit(solution)/shard_map/all_to_all | solution.py:277
  761.7 53.8 %slice-start.2 = ((s8[8192000]{0:T(1024)(128)(4,1)}), s8[4194304]{0:T(1024)(128)(4,1)S(1)}, s32[]{:S(2)}) async-start(s8[8192000]{0:T(1024)(128)(4,1)} %bitcast.91), calls=%async_computation.10 | async-start | bytes 8388608
  778.2 37.4 %slice-start.3 = ((s8[8192000]{0:T(1024)(128)(4,1)}), s8[3997696]{0:T(1024)(128)(4,1)S(1)}, s32[]{:S(2)}) async-start(s8[8192000]{0:T(1024)(128)(4,1)} %bitcast.91), calls=%async_computation.11 | async-start | bytes 7995392
  840.1 7.9 copy-start.26
  843.6 90.1 %all-to-all-start.1 = ((bf16[8,80,5,320]{3,1,2,0:T(8,128)(2,1)}), bf16[8,80,5,320]{3,1,2,0:T(8,128)(2,1)}, u32[]{:S(2)}, u32[]{:S(2)}) async-start(bf16[8,80,5,320]{3,1,2,0:T(8,128)(2,1)} %copy.198), calls=%async_computation.3 | async-start | bytes 4915200 | tf_op jit(solution)/shard_map/all_to_all | solution.py:290
  848.1 6.7 copy-start.25
  848.1 6.9 copy-start.28
  854.0 0.7 copy-start.19
  926.0 6.9 slice-start.4
  926.0 7.0 copy-start.21
  926.0 7.0 copy-start.23
  926.0 7.0 copy-start.24
  933.0 10.4 %copy-start.22 = (f32[80,4,4]{0,2,1:T(4,128)}, f32[80,4,4]{0,2,1:T(4,128)S(1)}, u32[]{:S(2)}) copy-start(f32[80,4,4]{0,2,1:T(4,128)S(1)} %copy.192) | copy-start | bytes 15364
Sparse Core Ops, SparseCore 0:
  12.2 227.1 all-gather.2
  427.0 124.7 reduce-scatter.2
  555.4 90.2 reduce-scatter.4
  647.0 22.3 all-gather.4

commit v2 on v0

v2 whole, which is shorter than its diff:
```python
import jax
import jax.numpy as jnp
from jax import lax
from jax.sharding import PartitionSpec as P

HEAD_DIM = 32
SEQ_LEN = 256
STEP = 5
LANE = 128


EPS_NORM = 1e-05
EPS_ADAM = 1e-08
BETA_FIRST = 0.5
BETA_SECOND = 0.5
RATE_MATRIX = 0.02
RATE_VECTOR = 0.05
EXACT_PRECISION = lax.Precision.HIGHEST
OPT_PRECISION = lax.Precision.HIGH


def normalize_layer(rows_in, norm_gain, norm_shift):
    centred = rows_in - jnp.mean(rows_in, axis=-1, keepdims=True)
    variance = jnp.mean(centred * centred, axis=-1, keepdims=True)
    return centred * lax.rsqrt(variance + EPS_NORM) * norm_gain + norm_shift


def exact_gelu(inputs):
    return jax.nn.gelu(inputs, approximate=False)


def adam_direction(first_new, second_new):
    return (
        first_new
        / (1.0 - BETA_FIRST**STEP)
        / (jnp.sqrt(second_new / (1.0 - BETA_SECOND**STEP)) + EPS_ADAM)
    )


def contract_rows(left_mat, right_mat):
    return jnp.dot(left_mat.T, right_mat, preferred_element_type=jnp.float32)


def times_transpose(left_mat, right_mat):
    return lax.dot_general(
        left_mat, right_mat, (((1,), (1,)), ((), ())), preferred_element_type=jnp.float32
    )


def block_scores(queries, key_rows):
    return jnp.einsum(
        "slhd,smhd->shlm", queries, key_rows, preferred_element_type=jnp.float32
    ) * HEAD_DIM ** (-0.5)


def attend_block(weight_blocks):
    queries, key_rows, values = weight_blocks
    scores = block_scores(queries, key_rows)
    highest = jnp.max(scores, axis=-1, keepdims=True)
    exponent = jnp.exp(scores - highest)
    totals = jnp.sum(exponent, axis=-1, keepdims=True)
    weights_soft = (exponent / totals).astype(jnp.bfloat16)
    mixed_rows = jnp.einsum(
        "shlm,smhd->slhd", weights_soft, values, preferred_element_type=jnp.float32
    )
    return (mixed_rows.astype(jnp.bfloat16), (highest + jnp.log(totals))[..., 0])


def attend_back(weight_blocks):
    queries, key_rows, values, log_total, d_attended = weight_blocks
    probabilities = jnp.exp(block_scores(queries, key_rows) - log_total[..., None])
    d_values = jnp.einsum(
        "shlm,slhd->smhd",
        probabilities.astype(jnp.bfloat16),
        d_attended,
        preferred_element_type=jnp.float32,
    )
    d_probs = jnp.einsum("slhd,smhd->shlm", d_attended, values, preferred_element_type=jnp.float32)
    d_scores = (
        probabilities * (d_probs - jnp.sum(probabilities * d_probs, axis=-1, keepdims=True))
    ).astype(jnp.bfloat16)
    d_queries = jnp.einsum(
        "shlm,smhd->slhd", d_scores, key_rows, preferred_element_type=jnp.float32
    ) * HEAD_DIM ** (-0.5)
    d_keys = jnp.einsum(
        "shlm,slhd->smhd", d_scores, queries, preferred_element_type=jnp.float32
    ) * HEAD_DIM ** (-0.5)
    return (
        d_queries.astype(jnp.bfloat16),
        d_keys.astype(jnp.bfloat16),
        d_values.astype(jnp.bfloat16),
    )


def ring_order(coords):
    count = len(coords)
    if count <= 2 or coords[0] is None:
        return list(range(count))

    def near(a, b):
        return sum(abs(p - q) for p, q in zip(coords[a], coords[b])) == 1

    links = [[b for b in range(count) if near(a, b)] for a in range(count)]
    path, seen, budget = [0], {0}, [20000]

    def extend():
        budget[0] -= 1
        if budget[0] < 0:
            return False
        if len(path) == count:
            return near(path[-1], path[0])
        options = [b for b in links[path[-1]] if b not in seen]
        options.sort(key=lambda b: sum(1 for q in links[b] if q not in seen))
        for b in options:
            path.append(b)
            seen.add(b)
            if extend():
                return True
            path.pop()
            seen.discard(b)
        return False

    return path if extend() else list(range(count))


class Ring:
    def __init__(self, order):
        self.order = order
        self.count = len(order)
        self.forward = [(order[p], order[(p + 1) % self.count]) for p in range(self.count)]
        self.backward = [(order[p], order[(p - 1) % self.count]) for p in range(self.count)]
        position = [0] * self.count
        for p, member in enumerate(order):
            position[member] = p
        self.position = position

    def sources(self):
        me = jnp.asarray(self.position, jnp.int32)[lax.axis_index("fsdp")]
        steps = jnp.arange(self.count, dtype=jnp.int32)
        return jnp.asarray(self.order, jnp.int32)[(me - steps) % self.count]

    def chains(self, width, parts):
        cuts = [round(width * i / (2 * parts) / LANE) * LANE for i in range(2 * parts + 1)]
        cuts[-1] = width
        return [(cuts[i], cuts[i + 1], i % 2 == 0) for i in range(2 * parts)]

    def all_gather(self, local, core, side, core_pairs, parts):
        count = self.count
        mine_cols = lax.dynamic_slice_in_dim(local, core * side, side, axis=1)
        other_cols = lax.dynamic_slice_in_dim(local, (1 - core) * side, side, axis=1)
        mine_parts, other_parts = [], []
        for lo, hi, ahead in self.chains(side, parts):
            pairs = self.forward if ahead else self.backward
            piece = mine_cols[:, lo:hi]
            got, passed = [None] * count, [None] * count
            got[0], passed[0] = piece, other_cols[:, lo:hi]
            for step in range(1, count):
                piece = lax.ppermute(piece, "fsdp", pairs)
                k = step if ahead else count - step
                got[k] = piece
                passed[k] = lax.ppermute(piece, "dp", core_pairs)
            mine_parts.append(jnp.concatenate(got, axis=0))
            other_parts.append(jnp.concatenate(passed, axis=0))
        return jnp.concatenate(mine_parts, axis=1), jnp.concatenate(other_parts, axis=1)

    def reduce_scatter(self, full, rows, outer_pairs, core_pairs, parts):
        count = self.count
        width = full.shape[1]
        outs, partners = [], []
        for lo, hi, ahead in self.chains(width, parts):
            pairs = self.forward if ahead else self.backward

            def block(k):
                return full[k * rows : (k + 1) * rows, lo:hi]

            acc = block(1 % count if ahead else count - 1)
            for step in range(1, count):
                got = lax.ppermute(acc.astype(jnp.bfloat16), "fsdp", pairs)
                k = (step + 1) % count if ahead else (count - step - 1) % count
                acc = got.astype(jnp.float32) + block(k)
            other = lax.ppermute(acc.astype(jnp.bfloat16), "dp", outer_pairs)
            acc = acc + other.astype(jnp.float32)
            outs.append(acc)
            partners.append(lax.ppermute(acc, "dp", core_pairs))
        return jnp.concatenate(outs, axis=1), jnp.concatenate(partners, axis=1)


def make_local(ring):
    def local(
        tokens,
        cotangent,
        masked_pos,
        labels,
        decoder,
        master,
        small_params,
        small_first,
        small_second,
        block_slots,
        first_moment,
        second_moment,
        left_bases,
        right_bases,
    ):
        model_width = decoder.shape[1]
        hidden = (master.shape[1] - 4 * model_width) // 2
        heads_count = model_width // HEAD_DIM
        token_count = tokens.shape[0]
        row_count, weight_cols = master.shape
        small_cols = small_params.shape[1]
        members = lax.axis_size("fsdp")
        core = lax.axis_index("dp") % 2
        replicas = lax.axis_size("dp")
        core_pairs = [(i, i ^ 1) for i in range(replicas)]
        outer_pairs = [(i, i ^ 2) for i in range(replicas)]
        half = weight_cols // 2
        lead = LANE
        side = half + lead
        split = (side // LANE + 1) // 2 * LANE

        sources = ring.sources()
        feature_of = (
            sources[:, None] * row_count + jnp.arange(row_count, dtype=jnp.int32)[None, :]
        ).reshape(-1)
        natural_of = jnp.zeros_like(feature_of).at[feature_of].set(
            jnp.arange(feature_of.shape[0], dtype=jnp.int32)
        )

        picker = (
            jnp.arange(model_width, dtype=jnp.int32)[:, None] == feature_of[None, :]
        ).astype(jnp.bfloat16)

        def to_rel(a):
            return jnp.dot(a, picker, preferred_element_type=jnp.float32).astype(a.dtype)

        def to_nat(a):
            return lax.dot_general(
                a, picker, (((1,), (1,)), ((), ())), precision=EXACT_PRECISION,
                preferred_element_type=jnp.float32,
            )

        w_low = master.astype(jnp.bfloat16)
        s_low = small_params.astype(jnp.bfloat16)
        packed_local = jnp.concatenate(
            [
                s_low,
                jnp.zeros((row_count, lead - small_cols), jnp.bfloat16),
                w_low,
                jnp.zeros((row_count, lead), jnp.bfloat16),
            ],
            axis=1,
        )
        mine, other = ring.all_gather(packed_local, core, side, core_pairs, 1)
        full = lax.cond(
            core == 0,
            lambda a, b: jnp.concatenate([a, b], axis=1),
            lambda a, b: jnp.concatenate([b, a], axis=1),
            mine,
            other,
        )
        weights = full[:, lead : lead + weight_cols]
        params = jnp.take(full[:, :small_cols].astype(jnp.float32), natural_of, axis=0)

        gain_one, shift_one, bias_query, bias_value, bias_output, gain_two, shift_two, bias_down = [
            params[:, column] for column in range(8)
        ]
        bias_up = params[:, 8:].reshape(hidden)
        rows_in = tokens.astype(jnp.float32)
        normed = normalize_layer(rows_in, gain_one, shift_one).astype(jnp.bfloat16)
        normed_rel = to_rel(normed)
        bias_qkv = jnp.concatenate([bias_query, jnp.zeros_like(bias_query), bias_value])
        projected = (
            jnp.dot(normed_rel, weights[:, : 3 * model_width], preferred_element_type=jnp.float32)
            + bias_qkv
        ).astype(jnp.bfloat16)
        seq_count = token_count // SEQ_LEN
        per_block = max(1, min(seq_count, 512 // SEQ_LEN))
        block_shape = (seq_count // per_block, per_block, SEQ_LEN, heads_count, HEAD_DIM)
        queries = projected[:, :model_width].reshape(block_shape)
        key_rows = projected[:, model_width : 2 * model_width].reshape(block_shape)
        values = projected[:, 2 * model_width :].reshape(block_shape)
        attention_result, log_total = lax.map(attend_block, (queries, key_rows, values))
        attention_result = attention_result.reshape(token_count, model_width)
        attended_rel = to_rel(attention_result)
        middle = (
            rows_in
            + jnp.dot(
                attended_rel,
                weights[:, 3 * model_width : 4 * model_width],
                preferred_element_type=jnp.float32,
            )
            + bias_output
        )
        normed_two = normalize_layer(middle, gain_two, shift_two).astype(jnp.bfloat16)
        normed_two_rel = to_rel(normed_two)
        pre_active = (
            jnp.dot(
                normed_two_rel,
                weights[:, 4 * model_width : 4 * model_width + hidden],
                preferred_element_type=jnp.float32,
            )
            + bias_up
        )
        active = exact_gelu(pre_active).astype(jnp.bfloat16)
        output_rows = (
            middle
            + to_nat(times_transpose(active, weights[:, 4 * model_width + hidden :]))
            + bias_down
        )
        out_tokens = output_rows.astype(jnp.bfloat16)
        logits = times_transpose(out_tokens, decoder)
        log_norm = jax.nn.logsumexp(logits, axis=-1)
        one_hot = (
            labels[:, None] == jnp.arange(decoder.shape[0], dtype=jnp.int32)[None, :]
        ).astype(jnp.float32)
        hidden_tokens = masked_pos.astype(jnp.float32)
        chosen = one_hot * hidden_tokens[:, None]
        entropy = log_norm - jnp.sum(one_hot * logits, axis=-1)
        right_prob = jnp.sum(one_hot * jnp.exp(logits - log_norm[:, None]), axis=-1)
        local_sums = jnp.concatenate(
            [jnp.sum(hidden_tokens * entropy)[None], jnp.sum(chosen * right_prob[:, None], axis=0)]
        )
        totals = jnp.concatenate([local_sums, jnp.sum(chosen, axis=0)])
        for axis in ("dp", "fsdp"):
            size = lax.axis_size(axis)
            reach = 1
            while reach < size:
                totals = totals + lax.ppermute(
                    totals, axis, [(i, i ^ reach) for i in range(size)]
                )
                reach *= 2
        global_sums, global_counts = totals[: local_sums.shape[0]], totals[local_sums.shape[0] :]
        loss_accuracy = jnp.concatenate(
            [
                global_sums[:1] / jnp.maximum(jnp.sum(global_counts), 1.0),
                global_sums[1:] / jnp.maximum(global_counts, 1.0),
            ]
        )
        counts = global_counts.astype(jnp.int32)
        back_rows = cotangent.astype(jnp.float32)
        cotangent_rel = to_rel(cotangent)
        d_active = jnp.dot(
            cotangent_rel, weights[:, 4 * model_width + hidden :], preferred_element_type=jnp.float32
        )
        unused, gelu_pull = jax.vjp(exact_gelu, pre_active)
        d_pre = gelu_pull(d_active)[0].astype(jnp.bfloat16)
        d_normed_two = to_nat(
            times_transpose(d_pre, weights[:, 4 * model_width : 4 * model_width + hidden])
        )
        unused, norm_pull_two = jax.vjp(normalize_layer, middle, params[:, 5], params[:, 6])
        d_middle_norm, d_gain_two, d_shift_two = norm_pull_two(d_normed_two)
        d_middle = back_rows + d_middle_norm
        d_branch = d_middle.astype(jnp.bfloat16)
        d_attended = to_nat(
            times_transpose(d_branch, weights[:, 3 * model_width : 4 * model_width])
        ).astype(jnp.bfloat16)
        d_queries, d_keys, d_values = lax.map(
            attend_back, (queries, key_rows, values, log_total, d_attended.reshape(block_shape))
        )
        d_projected = jnp.concatenate(
            [
                d_queries.reshape(token_count, model_width),
                d_keys.reshape(token_count, model_width),
                d_values.reshape(token_count, model_width),
            ],
            axis=1,
        )
        d_normed = to_nat(times_transpose(d_projected, weights[:, : 3 * model_width]))
        unused, norm_pull_one = jax.vjp(normalize_layer, rows_in, params[:, 0], params[:, 1])
        d_rows_norm, d_gain_one, d_shift_one = norm_pull_one(d_normed)
        grad_tokens = (d_middle + d_rows_norm).astype(jnp.bfloat16)
        proj_sums = jnp.sum(d_projected.astype(jnp.float32), axis=0)
        small_grads = jnp.stack(
            [
                d_gain_one,
                d_shift_one,
                proj_sums[:model_width],
                proj_sums[2 * model_width :],
                jnp.sum(d_branch.astype(jnp.float32), axis=0),
                d_gain_two,
                d_shift_two,
                jnp.sum(back_rows, axis=0),
            ],
            axis=1,
        )
        small_grads = jnp.concatenate(
            [small_grads, jnp.sum(d_pre.astype(jnp.float32), axis=0).reshape(model_width, -1)], axis=1
        )
        grad_dev = jnp.concatenate(
            [
                jnp.take(small_grads, feature_of, axis=0),
                jnp.zeros((model_width, lead - small_cols), jnp.float32),
                contract_rows(normed_rel, d_projected),
                contract_rows(attended_rel, d_branch),
                contract_rows(normed_two_rel, d_pre),
                contract_rows(cotangent_rel, active),
                jnp.zeros((model_width, lead), jnp.float32),
            ],
            axis=1,
        )
        keep = lax.dynamic_slice_in_dim(grad_dev, core * side, side, axis=1)
        send = lax.dynamic_slice_in_dim(grad_dev, (1 - core) * side, side, axis=1)
        chip = keep + lax.ppermute(send.astype(jnp.bfloat16), "dp", core_pairs).astype(jnp.float32)
        total, partner = ring.reduce_scatter(chip, row_count, outer_pairs, core_pairs, 2)
        joined = lax.cond(
            core == 0,
            lambda a, b: jnp.concatenate([a, b], axis=1),
            lambda a, b: jnp.concatenate([b, a], axis=1),
            total,
            partner,
        )
        grad_w = joined[:, lead : lead + weight_cols]
        grad_s = joined[:, :small_cols]

        block_width = model_width // 2
        block_count = grad_w.shape[1] // block_width
        owned_slots = first_moment.shape[0]
        devices = members
        slot_ids = jnp.arange(owned_slots * devices, dtype=jnp.int32)
        matches = block_slots[None, :] == slot_ids[:, None]
        in_use = jnp.any(matches, axis=1)
        source_block = jnp.sum(
            jnp.where(matches, jnp.arange(block_count, dtype=jnp.int32)[None, :], 0), axis=1
        )
        quarter = block_width // 2
        outgoing = jnp.take(grad_w.reshape(row_count, block_count, block_width), source_block, axis=1)
        outgoing = lax.dynamic_slice_in_dim(outgoing, core * quarter, quarter, axis=2)
        outgoing = jnp.where(in_use[None, :, None], outgoing, 0.0).reshape(
            row_count, devices, owned_slots, quarter
        )
        incoming = lax.all_to_all(
            outgoing.astype(jnp.bfloat16), "fsdp", split_axis=1, concat_axis=0, tiled=True
        ).reshape(row_count * devices, owned_slots, quarter)
        incoming_other = lax.ppermute(incoming, "dp", core_pairs)
        incoming_full = jnp.zeros((row_count * devices, owned_slots, block_width), jnp.bfloat16)
        incoming_full = lax.dynamic_update_slice(incoming_full, incoming, (0, 0, core * quarter))
        incoming_full = lax.dynamic_update_slice(
            incoming_full, incoming_other, (0, 0, (1 - core) * quarter)
        )
        incoming = incoming_full.astype(jnp.float32)
        my_use = lax.dynamic_slice_in_dim(in_use, lax.axis_index("fsdp") * owned_slots, owned_slots)
        eigen_turned = jnp.einsum("kdi,dkc->kic", left_bases, incoming, precision=OPT_PRECISION)
        eigen_turned = jnp.einsum("kic,kcj->kij", eigen_turned, right_bases, precision=OPT_PRECISION)
        first_new = BETA_FIRST * first_moment + (1.0 - BETA_FIRST) * eigen_turned
        second_new = BETA_SECOND * second_moment + (1.0 - BETA_SECOND) * eigen_turned * eigen_turned
        direction = adam_direction(first_new, second_new)
        rotated_gradient = jnp.einsum("kij,klj->kil", direction, right_bases, precision=OPT_PRECISION)
        rotated_gradient = jnp.einsum(
            "kdi,kil->dkl", left_bases, rotated_gradient, precision=OPT_PRECISION
        )
        going = lax.dynamic_slice_in_dim(rotated_gradient, core * quarter, quarter, axis=2)
        returned = lax.all_to_all(
            going.reshape(devices, row_count, owned_slots, quarter).astype(jnp.bfloat16),
            "fsdp",
            split_axis=0,
            concat_axis=0,
            tiled=True,
        )
        returned_other = lax.ppermute(returned, "dp", core_pairs)
        returned_full = jnp.zeros((devices, row_count, owned_slots, block_width), jnp.bfloat16)
        returned_full = lax.dynamic_update_slice(returned_full, returned, (0, 0, 0, core * quarter))
        returned_full = lax.dynamic_update_slice(
            returned_full, returned_other, (0, 0, 0, (1 - core) * quarter)
        )
        owner_of = block_slots // owned_slots
        slot_in = block_slots % owned_slots
        update = returned_full[owner_of, :, slot_in, :].astype(jnp.float32)
        update = jnp.transpose(update, (1, 0, 2)).reshape(row_count, block_count * block_width)
        new_master = master - RATE_MATRIX * update
        new_copy = new_master.astype(jnp.bfloat16)
        keep_slot = my_use[:, None, None]
        new_first = jnp.where(keep_slot, first_new, 0.0)
        new_second = jnp.where(keep_slot, second_new, 0.0)
        new_small_first = BETA_FIRST * small_first + (1.0 - BETA_FIRST) * grad_s
        new_small_second = BETA_SECOND * small_second + (1.0 - BETA_SECOND) * grad_s * grad_s
        new_small = small_params - RATE_VECTOR * adam_direction(new_small_first, new_small_second)
        return (
            out_tokens,
            grad_tokens,
            grad_w,
            grad_s,
            new_first,
            new_second,
            new_master,
            new_copy,
            new_small,
            new_small_first,
            new_small_second,
            loss_accuracy,
            counts,
        )

    return local


def solution(mesh):
    members = mesh.devices[0]
    coords = [tuple(getattr(d, "coords", None) or ()) or None for d in members]
    ring = Ring(ring_order(coords))
    return jax.shard_map(
        make_local(ring),
        mesh=mesh,
        in_specs=(
            P(("dp", "fsdp"), None),
            P(("dp", "fsdp"), None),
            P(("dp", "fsdp")),
            P(("dp", "fsdp")),
            P(),
            P("fsdp", None),
            P("fsdp", None),
            P("fsdp", None),
            P("fsdp", None),
            P(),
            P("fsdp", None, None),
            P("fsdp", None, None),
            P("fsdp", None, None),
            P("fsdp", None, None),
        ),
        out_specs=(
            P(("dp", "fsdp"), None),
            P(("dp", "fsdp"), None),
            P("fsdp", None),
            P("fsdp", None),
            P("fsdp", None, None),
            P("fsdp", None, None),
            P("fsdp", None),
            P("fsdp", None),
            P("fsdp", None),
            P("fsdp", None),
            P("fsdp", None),
            P(),
            P(),
        ),
        check_vma=False,
    )
```

time: 1180 us -> 706 us (0.60)
  waiting for transfers between devices: 717 us -> 171 us
  local copies, waits for them, and re-layouts: 76.1 us -> 210 us
  blocking collectives: 142 us -> 41.9 us
  starting transfers between devices: 10.6 us -> 60.1 us
  other arithmetic: 51.6 us -> 90.5 us
  matrix products: 156 us -> 118 us
  between operations: 16 us -> 2.89 us
    reduce_scatter x3 -> x0, waiting for transfers between devices: 384 us -> none  [the longest x1 226 us: local(): lax.psum_scatter(grad_w_local, 'dp', scatter_dimension=1, tiled=True)]
    all_gather x2 -> x0, waiting for transfers between devices: 225 us -> none  [the longest x1 191 us: local(): lax.all_gather(local_weights, 'fsdp', axis=0, tiled=True)]
    ppermute x0 -> x72, waiting for transfers between devices: none -> 140 us  [the longest x14 52.2 us: all_gather(): piece = lax.ppermute(piece, 'fsdp', pairs)]
    psum x1 -> x0, blocking collectives: 88.3 us -> none  [local(): lax.psum((local_sums, jnp.sum(chosen, axis=0)), ('dp', 'fsdp'))]
    all_to_all x2 -> x1, waiting for transfers between devices: 109 us -> 31.3 us  [local(): lax.all_to_all(going.reshape(devices, row_count, owned_slots, quarter).as...]
    ppermute x0 -> x72, starting transfers between devices: none -> 55.6 us  [the longest x28 29.1 us: reduce_scatter(): got = lax.ppermute(acc.astype(jnp.bfloat16), 'fsdp', pairs)]
    concatenate x1 -> x8, local copies, waits for them, and re-layouts: 2.33 us -> 50.6 us  [the longest x1 37.5 us: local(): jnp.concatenate([jnp.take(small_grads, feature_of, axis=0), jnp.zeros((mo...]
    dynamic_update_slice x0 -> x4, local copies, waits for them, and re-layouts: none -> 42.7 us  [the longest x1 22 us: local(): lax.dynamic_update_slice(returned_full, returned_other, (0, 0, 0, (1 - co...]
  transfers between devices with their start and end apart: 7 -> 73, of which waited for: 6 -> 41; matrix products, arithmetic and copies ran while one was open for 3% -> 16% of each run, Pallas kernels for 0% -> 0%
where the time goes in v2:
time: 706 us; the launch traced here: 694 us
  local copies, waits for them, and re-layouts  210 us (30%)
  waiting for transfers between devices  171 us (24%)
  matrix products  118 us (17%)
  other arithmetic  90.5 us (13%)
  starting transfers between devices  60.1 us (9%)
  blocking collectives  41.9 us (6%)
    ppermute x14, waiting for transfers between devices, all_gather(): piece = lax.ppermute(piece, 'fsdp', pairs)  52.2 us
    ppermute x28, waiting for transfers between devices, reduce_scatter(): got = lax.ppermute(acc.astype(jnp.bfloat16), 'fsdp', pairs)  46.6 us
    all_to_all x1, blocking collectives, local(): lax.all_to_all(outgoing.astype(jnp.bfloat16), 'fsdp', split_axis=1, conca...  41.9 us
    unnamed x132, local copies, waits for them, and re-layouts  40.9 us
    concatenate x1, local copies, waits for them, and re-layouts, local(): jnp.concatenate([jnp.take(small_grads, feature_of, axis=0), jnp.zeros((mo...  37.5 us
    all_to_all x1, waiting for transfers between devices, local(): lax.all_to_all(going.reshape(devices, row_count, owned_slots, quarter).as...  31.3 us
    ppermute x28, starting transfers between devices, reduce_scatter(): got = lax.ppermute(acc.astype(jnp.bfloat16), 'fsdp', pairs)  29.1 us
    dynamic_update_slice x1, local copies, waits for them, and re-layouts, local(): lax.dynamic_update_slice(returned_full, returned_other, (0, 0, 0, (1 - co...  22 us
  transfers between devices with their start and end apart: 73, of which 41 were waited for; matrix products, arithmetic and copies ran while one was open for 16% of the time, Pallas kernels for 0%

profile of v2, /device:TPU:0, one launch (start us, length us, event | category | flops | bytes accessed | tf_op | source)
XLA Modules:
  0.0 694.2 jit_solution(8026963287488865190)
XLA Ops:
  1.6 3.7 convert_element_type.348
  5.4 4.5 concatenate.66
  12.3 3.1 collective-permute-start.14
  20.3 4.1 scatter_custom_fusion
  34.3 6.1 collective-permute-done.15
  46.8 5.9 collective-permute-done.16
  53.9 2.9 collective-permute-done.4
  59.1 5.6 collective-permute-done.17
  66.0 3.1 collective-permute-done.6
  71.3 4.2 collective-permute-done.18
  76.0 5.4 collective-permute-done.8
  86.0 4.8 collective-permute-done.10
  95.1 5.1 collective-permute-done.20
  111.9 7.3 %pad_maximum_fusion.5 = bf16[640,6528]{1,0:T(8,128)(2,1)} fusion(bf16[640,3200]{1,0:T(8,128)(2,1)} %constant_dynamic-update-slice_fusion.22, bf16[640,3328]{1,0:T(8,128)(2,1)} %constant_dynamic-update-slice_fusion.14), kind=kLoop, calls=%fused_computation.13 | loop fusion | flops 16711680 | bytes 16711680 | tf_op jit(solution)/shard_map/concatenate | solution.py:164
  132.9 7.3 %pad_maximum_fusion.4 = bf16[640,6528]{1,0:T(8,128)(2,1)} fusion(bf16[640,3200]{1,0:T(8,128)(2,1)} %constant_dynamic-update-slice_fusion.7, bf16[640,3328]{1,0:T(8,128)(2,1)} %constant_dynamic-update-slice_fusion), kind=kLoop, calls=%fused_computation.12 | loop fusion | flops 16711680 | bytes 16711680 | tf_op jit(solution)/shard_map/concatenate | solution.py:164
  140.2 13.7 %conditional.2 = (bf16[640,13056]{1,0:T(8,128)(2,1)}) conditional(s32[]{:T(128)} %convert_element_type.346, (bf16[640,6528]{1,0:T(8,128)(2,1)}, bf16[640,6528]{1,0:T(8,128)(2,1)}) %tuple.49, (bf16[640,6528]{1,0:T(8,128)(2,1)}, bf16[640,6528]{1,0:T(8,128)(2,1)}) %tuple.50), branch_computations={%region_2.3_spmd, %region_3.4_spmd} | conditional | flops 33423360 | bytes 33423368 | solution.py:254
  140.2 13.6 %pad_maximum_fusion.1 = bf16[640,13056]{1,0:T(8,128)(2,1)} fusion(bf16[640,6528]{1,0:T(8,128)(2,1)} %get-tuple-element.107, bf16[640,6528]{1,0:T(8,128)(2,1)} %get-tuple-element.106), kind=kLoop, calls=%fused_computation.7 | loop fusion | flops 33423360 | bytes 33423360 | tf_op jit(solution)/shard_map/cond/branch_1_fun/concatenate | solution.py:256
  172.6 16.9 %multiply_convert_fusion.1 = (bf16[256,5120]{1,0:T(8,128)(2,1)}, f32[256,5120]{1,0:T(8,128)}, f32[256,5120]{1,0:T(8,128)}) fusion(f32[5120]{0:T(1024)S(1)} %add.417, bf16[256,640]{1,0:T(8,128)(2,1)S(1)} %fusion.54, bf16[640,13056]{1,0:T(8,128)(2,1)} %get-tuple-element.242), kind=kOutput, calls=%fused_computation.31 | convolution fusion | flops 1764229120 | bytes 20008960 | tf_op jit(solution)/shard_map/dot_general | solution.py:297
  189.6 7.2 %convert_reduce_fusion = (f32[5120]{0:T(1024)S(1)}, bf16[256,5120]{1,0:T(8,128)(2,1)S(1)}) fusion(f32[256,5120]{1,0:T(8,128)} %get-tuple-element.174, f32[256,5120]{1,0:T(8,128)} %get-tuple-element.224, bf16[640,256]{1,0:T(8,128)(2,1)S(1)} %copy-done.31, bf16[640,13056]{1,0:T(8,128)(2,1)S(1)} %bitcast.94), kind=kOutput, calls=%fused_computation.26 | convolution fusion | flops 1698688000 | bytes 20008960 | tf_op jit(solution)/shard_map/dot_general | solution.py:342
  205.6 3.7 fusion.56
  209.3 4.0 multiply_reduce_fusion
  219.4 3.2 fusion.143
  224.3 6.9 fusion.158
  240.5 8.5 %fusion.159 = f32[640,5120]{1,0:T(8,128)} fusion(bf16[640,256]{1,0:T(8,128)(2,1)} %convolution_convert_fusion, bf16[256,5120]{1,0:T(8,128)(2,1)} %get-tuple-element.173), kind=kOutput, calls=%fused_computation.343 | convolution fusion | flops 1677721600 | bytes 16056320 | tf_op jit(solution)/shard_map/dot_general | solution.py:41
  253.1 37.5 %concatenate.76 = f32[640,13056]{1,0:T(8,128)} concatenate(f32[640,16]{1,0:T(8,128)S(1)} %broadcast_select_fusion.2, f32[640,112]{1,0:T(8,128)S(1)} %broadcast_in_dim.157, f32[640,1920]{1,0:T(8,128)} %fusion.143, f32[640,640]{1,0:T(8,128)} %fusion.157, f32[640,5120]{1,0:T(8,128)} %fusion.158, f32[640,5120]{1,0:T(8,128)} %fusion.159, f32[640,128]{1,0:T(8,128)S(1)} %broadcast_in_dim.158), dimensions={1} | concatenate | bytes 66846720 | tf_op jit(solution)/shard_map/concatenate | solution.py:389
  290.6 8.9 %dynamic-slice_convert_fusion = bf16[640,6528]{1,0:T(8,128)(2,1)} fusion(f32[640,13056]{1,0:T(8,128)} %concatenate.76, s32[]{:T(128)S(6)} %select_n.133), kind=kLoop, calls=%fused_computation.11 | loop fusion | bytes 16711684 | tf_op jit(solution)/shard_map/convert_element_type | solution.py:403
  300.2 12.8 %collective-permute-done.28 = bf16[640,6528]{1,0:T(8,128)(2,1)} collective-permute-done((bf16[640,6528]{1,0:T(8,128)(2,1)}, bf16[640,6528]{1,0:T(8,128)(2,1)}, u32[]{:S(2)}, u32[]{:S(2)}) %collective-permute-start.28) | collective-permute-done | bytes 8355872 | tf_op jit(solution)/shard_map/ppermute | solution.py:403
  313.0 8.9 %fusion.148 = (bf16[640,6528]{1,0:T(8,128)(2,1)S(1)}, f32[640,6528]{1,0:T(8,128)S(1)}) fusion(bf16[640,6528]{1,0:T(8,128)(2,1)} %collective-permute-done.28, f32[640,13056]{1,0:T(8,128)} %concatenate.76, s32[]{:T(128)S(6)} %select_n.134), kind=kLoop, calls=%fused_computation.334 | loop fusion | flops 12533760 | bytes 50135044 | tf_op jit(solution)/shard_map/convert.3
  326.1 4.7 collective-permute-done.47
  332.9 4.8 collective-permute-done.38
  344.5 4.1 collective-permute-done.57
  348.6 4.0 collective-permute-done.39
  359.4 4.1 collective-permute-done.58
  363.5 3.1 collective-permute-done.40
  373.4 3.5 collective-permute-done.59
  400.6 3.7 collective-permute-done.43
  421.4 4.6 collective-permute-done.63
  426.0 3.9 collective-permute-done.45
  439.8 5.2 conditional.3
  439.8 3.9 pad_maximum_fusion.3
  445.0 5.0 reshape.453
  450.1 3.4 copy.153
  453.5 4.2 gather_fusion.1
  457.8 3.3 fusion.25
  461.1 41.9 %all_to_all.20 = bf16[80,8,5,160]{3,0,2,1:T(8,128)(2,1)} all-to-all(bf16[80,8,5,160]{3,0,2,1:T(8,128)(2,1)S(1)} %bitcast.95), channel_id=1, replica_groups=mesh['dp'=4,'fsdp'=8] {'fsdp'}, dimensions={1} | all-to-all | bytes 2048000 | tf_op jit(solution)/shard_map/all_to_all | solution.py:431
  503.0 3.7 copy.154
  506.7 3.3 reshape.386
  514.3 7.5 %fusion.160 = f32[5,320,640]{2,1,0:T(8,128)S(1)} fusion(bf16[640,5,320]{0,2,1:T(8,128)(2,1)S(1)} %constant_dynamic-update-slice_fusion.34, f32[5,640,640]{2,1,0:T(8,128)} %param.34), kind=kOutput, calls=%fused_computation.344 | convolution fusion | flops 3932160000 | bytes 14336000 | tf_op jit(solution)/shard_map/kdi,dkc->kic/dot_general | solution.py:442
  521.8 11.6 %broadcast_select_fusion = (f32[5,640,320]{1,2,0:T(8,128)}, f32[5,640,320]{1,2,0:T(8,128)}, f32[5,640,320]{1,2,0:T(8,128)}) fusion(pred[5]{0:T(512)(128)(4,1)S(1)} %dynamic_slice.47, f32[5,640,320]{1,2,0:T(8,128)S(1)} %copy-done.5, f32[5,640,320]{1,2,0:T(8,128)} %param.32, f32[5,320,640]{2,1,0:T(8,128)S(1)} %fusion.160, f32[5,320,320]{2,1,0:T(8,128)S(1)} %copy-done), kind=kOutput, calls=%fused_computation.74 | convolution fusion | flops 1974272000 | bytes 26624004 | tf_op jit(solution)/shard_map/kic,kcj->kij/dot_general | solution.py:443
  533.4 9.7 %fusion.17 = f32[5,640,320]{1,2,0:T(8,128)S(1)} fusion(f32[5,320,320]{2,1,0:T(8,128)S(1)} %copy-done, f32[5,640,320]{1,2,0:T(8,128)} %get-tuple-element.231, f32[5,640,320]{1,2,0:T(8,128)} %param.32, f32[5,640,320]{1,2,0:T(8,128)S(1)} %copy-done.5), kind=kOutput, calls=%fused_computation.51 | convolution fusion | flops 1976320000 | bytes 18432000 | tf_op jit(solution)/shard_map/kij,klj->kil/dot_general | solution.py:447
  543.2 8.6 %fusion.161 = bf16[5,320,640]{2,1,0:T(8,128)(2,1)S(1)} fusion(f32[5,640,320]{1,2,0:T(8,128)S(1)} %fusion.17, f32[5,640,640]{2,1,0:T(8,128)S(1)} %bitcast.92), kind=kOutput, calls=%fused_computation.345 | convolution fusion | flops 3932160000 | bytes 14336000 | tf_op jit(solution)/shard_map/kdi,kil->dkl/dot_general | solution.py:448
  554.5 3.9 copy.156
  558.4 4.5 all-to-all-start.1
  562.9 5.9 fusion.2
  570.5 31.3 %all-to-all-done.1 = bf16[8,80,5,160]{3,1,2,0:T(8,128)(2,1)} async-done(((bf16[8,80,5,160]{3,1,2,0:T(8,128)(2,1)}), bf16[8,80,5,160]{3,1,2,0:T(8,128)(2,1)}, u32[]{:S(2)}, u32[]{:S(2)}) %all-to-all-start.1) | async-done | bytes 1024032 | tf_op jit(solution)/shard_map/all_to_all | solution.py:452
  613.6 3.6 collective-permute-done.70
  618.0 3.6 collective-permute-done.71
  624.1 3.5 copy.152
  630.5 19.1 %dynamic_update_slice.26 = bf16[8,80,5,320]{3,1,2,0:T(8,128)(2,1)} dynamic-update-slice(bf16[8,80,5,320]{3,1,2,0:T(8,128)(2,1)} %broadcast_in_dim.168, bf16[8,80,5,160]{3,1,2,0:T(8,128)(2,1)} %all-to-all-done.1, s32[]{:T(128)} %constant.81.clone.1, s32[]{:T(128)} %constant.81.clone.1, s32[]{:T(128)} %constant.81.clone.1, s32[]{:T(128)S(6)} %select_n.144) | dynamic-update-slice | bytes 2048004 | tf_op jit(solution)/shard_map/dynamic_update_slice | solution.py:461
  649.7 22.0 %dynamic_update_slice.27 = bf16[8,80,5,320]{3,1,2,0:T(8,128)(2,1)} dynamic-update-slice(bf16[8,80,5,320]{3,1,2,0:T(8,128)(2,1)} %dynamic_update_slice.26, bf16[8,80,5,160]{3,1,2,0:T(8,128)(2,1)} %collective-permute-done.66, s32[]{:T(128)} %constant.81.clone.1, s32[]{:T(128)} %constant.81.clone.1, s32[]{:T(128)} %constant.81.clone.1, s32[]{:T(128)S(6)} %select_n.146) | dynamic-update-slice | bytes 2048004 | tf_op jit(solution)/shard_map/dynamic_update_slice | solution.py:462
  671.7 4.3 gather_fusion.2
  678.2 3.7 copy.157
  681.9 5.5 mul.333
  687.4 6.5 fusion.147
  (394 shorter events, 221.9 us)
Async XLA Ops:
  12.3 15.0 %collective-permute-start.14 = (bf16[80,3200]{1,0:T(8,128)(2,1)}, bf16[80,3200]{1,0:T(8,128)(2,1)}, u32[]{:S(2)}, u32[]{:S(2)}) collective-permute-start(bf16[80,3200]{1,0:T(8,128)(2,1)} %get-tuple-element.178), channel_id=1, source_target_pairs={{0,2},{1,0},{3,1},{5,3},{7,5},{6,7},{4,6},{2,4},{8,10},{9,8},{11,9... | collective-permute-start | bytes 1536008 | tf_op jit(solution)/shard_map/ppermute | solution.py:158
  17.8 13.9 %collective-permute-start = (bf16[80,3328]{1,0:T(8,128)(2,1)}, bf16[80,3328]{1,0:T(8,128)(2,1)}, u32[]{:S(2)}, u32[]{:S(2)}) collective-permute-start(bf16[80,3328]{1,0:T(8,128)(2,1)} %get-tuple-element.176), channel_id=1, source_target_pairs={{0,1},{1,3},{3,5},{5,7},{7,6},{6,4},{4,2},{2,0},{8,9},{9,11},{11,1... | collective-permute-start | bytes 1597448 | tf_op jit(solution)/shard_map/ppermute | solution.py:158
  27.3 13.1 %collective-permute-start.15 = (bf16[80,3200]{1,0:T(8,128)(2,1)}, bf16[80,3200]{1,0:T(8,128)(2,1)}, u32[]{:S(2)}, u32[]{:S(2)}) collective-permute-start(bf16[80,3200]{1,0:T(8,128)(2,1)} %collective-permute-done.14), channel_id=1, source_target_pairs={{0,2},{1,0},{3,1},{5,3},{7,5},{6,7},{4,6},{2,4},{8,10},{9,8},{11,9... | collective-permute-start | bytes 1536008 | tf_op jit(solution)/shard_map/ppermute | solution.py:158
  31.6 12.9 %collective-permute-start.2 = (bf16[80,3328]{1,0:T(8,128)(2,1)}, bf16[80,3328]{1,0:T(8,128)(2,1)S(1)}, u32[]{:S(2)}, u32[]{:S(2)}) collective-permute-start(bf16[80,3328]{1,0:T(8,128)(2,1)} %collective-permute-done), channel_id=1, source_target_pairs={{0,1},{1,3},{3,5},{5,7},{7,6},{6,4},{4,2},{2,0},{8,9},{9,11},{11,1... | collective-permute-start | bytes 1597448 | tf_op jit(solution)/shard_map/ppermute | solution.py:158
  31.9 98.3 %collective-permute-start.27 = (bf16[80,3200]{1,0:T(8,128)(2,1)}, bf16[80,3200]{1,0:T(8,128)(2,1)}, u32[]{:S(2)}, u32[]{:S(2)}) collective-permute-start(bf16[80,3200]{1,0:T(8,128)(2,1)} %collective-permute-done.14), channel_id=1, source_target_pairs={{0,8},{8,0},{16,24},{24,16},{1,9},{9,1},{17,25},{25,17},{2,10},{10... | collective-permute-start | bytes 1536008 | tf_op jit(solution)/shard_map/ppermute | solution.py:161
  31.9 14.1 %collective-permute-start.1 = (bf16[80,3328]{1,0:T(8,128)(2,1)}, bf16[80,3328]{1,0:T(8,128)(2,1)S(1)}, u32[]{:S(2)}, u32[]{:S(2)}) collective-permute-start(bf16[80,3328]{1,0:T(8,128)(2,1)} %collective-permute-done), channel_id=1, source_target_pairs={{0,8},{8,0},{16,24},{24,16},{1,9},{9,1},{17,25},{25,17},{2,10},{10... | collective-permute-start | bytes 1597448 | tf_op jit(solution)/shard_map/ppermute | solution.py:161
  40.4 12.3 %collective-permute-start.16 = (bf16[80,3200]{1,0:T(8,128)(2,1)}, bf16[80,3200]{1,0:T(8,128)(2,1)}, u32[]{:S(2)}, u32[]{:S(2)}) collective-permute-start(bf16[80,3200]{1,0:T(8,128)(2,1)} %collective-permute-done.15), channel_id=1, source_target_pairs={{0,2},{1,0},{3,1},{5,3},{7,5},{6,7},{4,6},{2,4},{8,10},{9,8},{11,9... | collective-permute-start | bytes 1536008 | tf_op jit(solution)/shard_map/ppermute | solution.py:158
  41.9 86.4 %collective-permute-start.26 = (bf16[80,3200]{1,0:T(8,128)(2,1)}, bf16[80,3200]{1,0:T(8,128)(2,1)}, u32[]{:S(2)}, u32[]{:S(2)}) collective-permute-start(bf16[80,3200]{1,0:T(8,128)(2,1)} %collective-permute-done.15), channel_id=1, source_target_pairs={{0,8},{8,0},{16,24},{24,16},{1,9},{9,1},{17,25},{25,17},{2,10},{10... | collective-permute-start | bytes 1536008 | tf_op jit(solution)/shard_map/ppermute | solution.py:161
  44.6 12.3 %collective-permute-start.4 = (bf16[80,3328]{1,0:T(8,128)(2,1)S(1)}, bf16[80,3328]{1,0:T(8,128)(2,1)S(1)}, u32[]{:S(2)}, u32[]{:S(2)}) collective-permute-start(bf16[80,3328]{1,0:T(8,128)(2,1)S(1)} %collective-permute-done.2), channel_id=1, source_target_pairs={{0,1},{1,3},{3,5},{5,7},{7,6},{6,4},{4,2},{2,0},{8,9},{9,11},{11,1... | collective-permute-start | bytes 1597448 | tf_op jit(solution)/shard_map/ppermute | solution.py:158
  46.0 12.3 %collective-permute-start.3 = (bf16[80,3328]{1,0:T(8,128)(2,1)S(1)}, bf16[80,3328]{1,0:T(8,128)(2,1)S(1)}, u32[]{:S(2)}, u32[]{:S(2)}) collective-permute-start(bf16[80,3328]{1,0:T(8,128)(2,1)S(1)} %collective-permute-done.2), channel_id=1, source_target_pairs={{0,8},{8,0},{16,24},{24,16},{1,9},{9,1},{17,25},{25,17},{2,10},{10... | collective-permute-start | bytes 1597448 | tf_op jit(solution)/shard_map/ppermute | solution.py:161
  52.7 12.0 %collective-permute-start.17 = (bf16[80,3200]{1,0:T(8,128)(2,1)}, bf16[80,3200]{1,0:T(8,128)(2,1)S(1)}, u32[]{:S(2)}, u32[]{:S(2)}) collective-permute-start(bf16[80,3200]{1,0:T(8,128)(2,1)} %collective-permute-done.16), channel_id=1, source_target_pairs={{0,2},{1,0},{3,1},{5,3},{7,5},{6,7},{4,6},{2,4},{8,10},{9,8},{11,9... | collective-permute-start | bytes 1536008 | tf_op jit(solution)/shard_map/ppermute | solution.py:158
  56.8 12.3 %collective-permute-start.6 = (bf16[80,3328]{1,0:T(8,128)(2,1)S(1)}, bf16[80,3328]{1,0:T(8,128)(2,1)S(1)}, u32[]{:S(2)}, u32[]{:S(2)}) collective-permute-start(bf16[80,3328]{1,0:T(8,128)(2,1)S(1)} %collective-permute-done.4), channel_id=1, source_target_pairs={{0,1},{1,3},{3,5},{5,7},{7,6},{6,4},{4,2},{2,0},{8,9},{9,11},{11,1... | collective-permute-start | bytes 1597448 | tf_op jit(solution)/shard_map/ppermute | solution.py:158
  58.2 12.2 %collective-permute-start.5 = (bf16[80,3328]{1,0:T(8,128)(2,1)S(1)}, bf16[80,3328]{1,0:T(8,128)(2,1)S(1)}, u32[]{:S(2)}, u32[]{:S(2)}) collective-permute-start(bf16[80,3328]{1,0:T(8,128)(2,1)S(1)} %collective-permute-done.4), channel_id=1, source_target_pairs={{0,8},{8,0},{16,24},{24,16},{1,9},{9,1},{17,25},{25,17},{2,10},{10... | collective-permute-start | bytes 1597448 | tf_op jit(solution)/shard_map/ppermute | solution.py:161
  64.7 10.8 %collective-permute-start.18 = (bf16[80,3200]{1,0:T(8,128)(2,1)S(1)}, bf16[80,3200]{1,0:T(8,128)(2,1)S(1)}, u32[]{:S(2)}, u32[]{:S(2)}) collective-permute-start(bf16[80,3200]{1,0:T(8,128)(2,1)S(1)} %collective-permute-done.17), channel_id=1, source_target_pairs={{0,2},{1,0},{3,1},{5,3},{7,5},{6,7},{4,6},{2,4},{8,10},{9,8},{11,9... | collective-permute-start | bytes 1536008 | tf_op jit(solution)/shard_map/ppermute | solution.py:158
  69.1 12.3 %collective-permute-start.8 = (bf16[80,3328]{1,0:T(8,128)(2,1)S(1)}, bf16[80,3328]{1,0:T(8,128)(2,1)S(1)}, u32[]{:S(2)}, u32[]{:S(2)}) collective-permute-start(bf16[80,3328]{1,0:T(8,128)(2,1)S(1)} %collective-permute-done.6), channel_id=1, source_target_pairs={{0,1},{1,3},{3,5},{5,7},{7,6},{6,4},{4,2},{2,0},{8,9},{9,11},{11,1... | collective-permute-start | bytes 1597448 | tf_op jit(solution)/shard_map/ppermute | solution.py:158
  70.5 12.3 %collective-permute-start.7 = (bf16[80,3328]{1,0:T(8,128)(2,1)S(1)}, bf16[80,3328]{1,0:T(8,128)(2,1)S(1)}, u32[]{:S(2)}, u32[]{:S(2)}) collective-permute-start(bf16[80,3328]{1,0:T(8,128)(2,1)S(1)} %collective-permute-done.6), channel_id=1, source_target_pairs={{0,8},{8,0},{16,24},{24,16},{1,9},{9,1},{17,25},{25,17},{2,10},{10... | collective-permute-start | bytes 1597448 | tf_op jit(solution)/shard_map/ppermute | solution.py:161
  75.5 10.4 %collective-permute-start.19 = (bf16[80,3200]{1,0:T(8,128)(2,1)S(1)}, bf16[80,3200]{1,0:T(8,128)(2,1)S(1)}, u32[]{:S(2)}, u32[]{:S(2)}) collective-permute-start(bf16[80,3200]{1,0:T(8,128)(2,1)S(1)} %collective-permute-done.18), channel_id=1, source_target_pairs={{0,2},{1,0},{3,1},{5,3},{7,5},{6,7},{4,6},{2,4},{8,10},{9,8},{11,9... | collective-permute-start | bytes 1536008 | tf_op jit(solution)/shard_map/ppermute | solution.py:158
  81.4 9.4 %collective-permute-start.10 = (bf16[80,3328]{1,0:T(8,128)(2,1)S(1)}, bf16[80,3328]{1,0:T(8,128)(2,1)}, u32[]{:S(2)}, u32[]{:S(2)}) collective-permute-start(bf16[80,3328]{1,0:T(8,128)(2,1)S(1)} %collective-permute-done.8), channel_id=1, source_target_pairs={{0,1},{1,3},{3,5},{5,7},{7,6},{6,4},{4,2},{2,0},{8,9},{9,11},{11,1... | collective-permute-start | bytes 1597448 | tf_op jit(solution)/shard_map/ppermute | solution.py:158
  82.7 11.5 %collective-permute-start.9 = (bf16[80,3328]{1,0:T(8,128)(2,1)S(1)}, bf16[80,3328]{1,0:T(8,128)(2,1)S(1)}, u32[]{:S(2)}, u32[]{:S(2)}) collective-permute-start(bf16[80,3328]{1,0:T(8,128)(2,1)S(1)} %collective-permute-done.8), channel_id=1, source_target_pairs={{0,8},{8,0},{16,24},{24,16},{1,9},{9,1},{17,25},{25,17},{2,10},{10... | collective-permute-start | bytes 1597448 | tf_op jit(solution)/shard_map/ppermute | solution.py:161
  86.0 40.5 %collective-permute-start.25 = (bf16[80,3200]{1,0:T(8,128)(2,1)}, bf16[80,3200]{1,0:T(8,128)(2,1)}, u32[]{:S(2)}, u32[]{:S(2)}) collective-permute-start(bf16[80,3200]{1,0:T(8,128)(2,1)} %collective-permute-done.16), channel_id=1, source_target_pairs={{0,8},{8,0},{16,24},{24,16},{1,9},{9,1},{17,25},{25,17},{2,10},{10... | collective-permute-start | bytes 1536008 | tf_op jit(solution)/shard_map/ppermute | solution.py:161
  90.8 9.4 %collective-permute-start.20 = (bf16[80,3200]{1,0:T(8,128)(2,1)S(1)}, bf16[80,3200]{1,0:T(8,128)(2,1)}, u32[]{:S(2)}, u32[]{:S(2)}) collective-permute-start(bf16[80,3200]{1,0:T(8,128)(2,1)S(1)} %collective-permute-done.19), channel_id=1, source_target_pairs={{0,2},{1,0},{3,1},{5,3},{7,5},{6,7},{4,6},{2,4},{8,10},{9,8},{11,9... | collective-permute-start | bytes 1536008 | tf_op jit(solution)/shard_map/ppermute | solution.py:158
  94.3 24.9 %collective-permute-start.11 = (bf16[80,3328]{1,0:T(8,128)(2,1)}, bf16[80,3328]{1,0:T(8,128)(2,1)}, u32[]{:S(2)}, u32[]{:S(2)}) collective-permute-start(bf16[80,3328]{1,0:T(8,128)(2,1)} %collective-permute-done.10), channel_id=1, source_target_pairs={{0,8},{8,0},{16,24},{24,16},{1,9},{9,1},{17,25},{25,17},{2,10},{10... | collective-permute-start | bytes 1597448 | tf_op jit(solution)/shard_map/ppermute | solution.py:161
  100.1 10.8 %collective-permute-start.12 = (bf16[80,3328]{1,0:T(8,128)(2,1)}, bf16[80,3328]{1,0:T(8,128)(2,1)S(1)}, u32[]{:S(2)}, u32[]{:S(2)}) collective-permute-start(bf16[80,3328]{1,0:T(8,128)(2,1)} %collective-permute-done.10), channel_id=1, source_target_pairs={{0,1},{1,3},{3,5},{5,7},{7,6},{6,4},{4,2},{2,0},{8,9},{9,11},{11,1... | collective-permute-start | bytes 1597448 | tf_op jit(solution)/shard_map/ppermute | solution.py:158
  111.0 10.6 %collective-permute-start.21 = (bf16[80,3200]{1,0:T(8,128)(2,1)}, bf16[80,3200]{1,0:T(8,128)(2,1)}, u32[]{:S(2)}, u32[]{:S(2)}) collective-permute-start(bf16[80,3200]{1,0:T(8,128)(2,1)} %collective-permute-done.20), channel_id=1, source_target_pairs={{0,8},{8,0},{16,24},{24,16},{1,9},{9,1},{17,25},{25,17},{2,10},{10... | collective-permute-start | bytes 1536008 | tf_op jit(solution)/shard_map/ppermute | solution.py:161
  119.2 4.2 collective-permute-start.22
  124.7 7.3 %collective-permute-start.13 = (bf16[80,3328]{1,0:T(8,128)(2,1)S(1)}, bf16[80,3328]{1,0:T(8,128)(2,1)S(1)}, u32[]{:S(2)}, u32[]{:S(2)}) collective-permute-start(bf16[80,3328]{1,0:T(8,128)(2,1)S(1)} %collective-permute-done.12), channel_id=1, source_target_pairs={{0,8},{8,0},{16,24},{24,16},{1,9},{9,1},{17,25},{25,17},{2,10},{10... | collective-permute-start | bytes 1597448 | tf_op jit(solution)/shard_map/ppermute | solution.py:161
  299.5 13.5 %collective-permute-start.28 = (bf16[640,6528]{1,0:T(8,128)(2,1)}, bf16[640,6528]{1,0:T(8,128)(2,1)}, u32[]{:S(2)}, u32[]{:S(2)}) collective-permute-start(bf16[640,6528]{1,0:T(8,128)(2,1)} %dynamic-slice_convert_fusion), channel_id=1, source_target_pairs={{0,8},{8,0},{16,24},{24,16},{1,9},{9,1},{17,25},{25,17},{2,10},{10... | collective-permute-start | bytes 25067528 | tf_op jit(solution)/shard_map/ppermute | solution.py:403
  321.9 8.9 %collective-permute-start.47 = (bf16[80,1536]{1,0:T(8,128)(2,1)S(1)}, bf16[80,1536]{1,0:T(8,128)(2,1)S(1)}, u32[]{:S(2)}, u32[]{:S(2)}) collective-permute-start(bf16[80,1536]{1,0:T(8,128)(2,1)S(1)} %slice.323), channel_id=1, source_target_pairs={{0,1},{1,3},{3,5},{5,7},{7,6},{6,4},{4,2},{2,0},{8,9},{9,11},{11,1... | collective-permute-start | bytes 737288 | tf_op jit(solution)/shard_map/ppermute | solution.py:178
  323.6 9.3 %collective-permute-start.56 = (bf16[80,1664]{1,0:T(8,128)(2,1)S(1)}, bf16[80,1664]{1,0:T(8,128)(2,1)S(1)}, u32[]{:S(2)}, u32[]{:S(2)}) collective-permute-start(bf16[80,1664]{1,0:T(8,128)(2,1)S(1)} %get-tuple-element.203), channel_id=1, source_target_pairs={{0,2},{1,0},{3,1},{5,3},{7,5},{6,7},{4,6},{2,4},{8,10},{9,8},{11,9... | collective-permute-start | bytes 798728 | tf_op jit(solution)/shard_map/ppermute | solution.py:178
  324.1 13.7 %collective-permute-start.38 = (bf16[80,1664]{1,0:T(8,128)(2,1)S(1)}, bf16[80,1664]{1,0:T(8,128)(2,1)S(1)}, u32[]{:S(2)}, u32[]{:S(2)}) collective-permute-start(bf16[80,1664]{1,0:T(8,128)(2,1)S(1)} %get-tuple-element.204), channel_id=1, source_target_pairs={{0,2},{1,0},{3,1},{5,3},{7,5},{6,7},{4,6},{2,4},{8,10},{9,8},{11,9... | collective-permute-start | bytes 798728 | tf_op jit(solution)/shard_map/ppermute | solution.py:178
  325.2 12.6 %collective-permute-start.29 = (bf16[80,1664]{1,0:T(8,128)(2,1)S(1)}, bf16[80,1664]{1,0:T(8,128)(2,1)S(1)}, u32[]{:S(2)}, u32[]{:S(2)}) collective-permute-start(bf16[80,1664]{1,0:T(8,128)(2,1)S(1)} %get-tuple-element.205), channel_id=1, source_target_pairs={{0,1},{1,3},{3,5},{5,7},{7,6},{6,4},{4,2},{2,0},{8,9},{9,11},{11,1... | collective-permute-start | bytes 798728 | tf_op jit(solution)/shard_map/ppermute | solution.py:178
  330.8 11.0 %collective-permute-start.48 = (bf16[80,1536]{1,0:T(8,128)(2,1)S(1)}, bf16[80,1536]{1,0:T(8,128)(2,1)S(1)}, u32[]{:S(2)}, u32[]{:S(2)}) collective-permute-start(bf16[80,1536]{1,0:T(8,128)(2,1)S(1)} %fusion.107), channel_id=1, source_target_pairs={{0,1},{1,3},{3,5},{5,7},{7,6},{6,4},{4,2},{2,0},{8,9},{9,11},{11,1... | collective-permute-start | bytes 737288 | tf_op jit(solution)/shard_map/ppermute | solution.py:178
  339.3 9.3 %collective-permute-start.57 = (bf16[80,1664]{1,0:T(8,128)(2,1)S(1)}, bf16[80,1664]{1,0:T(8,128)(2,1)S(1)}, u32[]{:S(2)}, u32[]{:S(2)}) collective-permute-start(bf16[80,1664]{1,0:T(8,128)(2,1)S(1)} %get-tuple-element.200), channel_id=1, source_target_pairs={{0,2},{1,0},{3,1},{5,3},{7,5},{6,7},{4,6},{2,4},{8,10},{9,8},{11,9... | collective-permute-start | bytes 798728 | tf_op jit(solution)/shard_map/ppermute | solution.py:178
  339.8 12.8 %collective-permute-start.39 = (bf16[80,1664]{1,0:T(8,128)(2,1)S(1)}, bf16[80,1664]{1,0:T(8,128)(2,1)S(1)}, u32[]{:S(2)}, u32[]{:S(2)}) collective-permute-start(bf16[80,1664]{1,0:T(8,128)(2,1)S(1)} %get-tuple-element.201), channel_id=1, source_target_pairs={{0,2},{1,0},{3,1},{5,3},{7,5},{6,7},{4,6},{2,4},{8,10},{9,8},{11,9... | collective-permute-start | bytes 798728 | tf_op jit(solution)/shard_map/ppermute | solution.py:178
  340.9 11.7 %collective-permute-start.30 = (bf16[80,1664]{1,0:T(8,128)(2,1)S(1)}, bf16[80,1664]{1,0:T(8,128)(2,1)S(1)}, u32[]{:S(2)}, u32[]{:S(2)}) collective-permute-start(bf16[80,1664]{1,0:T(8,128)(2,1)S(1)} %get-tuple-element.202), channel_id=1, source_target_pairs={{0,1},{1,3},{3,5},{5,7},{7,6},{6,4},{4,2},{2,0},{8,9},{9,11},{11,1... | collective-permute-start | bytes 798728 | tf_op jit(solution)/shard_map/ppermute | solution.py:178
  342.9 13.8 %collective-permute-start.49 = (bf16[80,1536]{1,0:T(8,128)(2,1)S(1)}, bf16[80,1536]{1,0:T(8,128)(2,1)S(1)}, u32[]{:S(2)}, u32[]{:S(2)}) collective-permute-start(bf16[80,1536]{1,0:T(8,128)(2,1)S(1)} %fusion.106), channel_id=1, source_target_pairs={{0,1},{1,3},{3,5},{5,7},{7,6},{6,4},{4,2},{2,0},{8,9},{9,11},{11,1... | collective-permute-start | bytes 737288 | tf_op jit(solution)/shard_map/ppermute | solution.py:178
  354.1 9.3 %collective-permute-start.58 = (bf16[80,1664]{1,0:T(8,128)(2,1)S(1)}, bf16[80,1664]{1,0:T(8,128)(2,1)S(1)}, u32[]{:S(2)}, u32[]{:S(2)}) collective-permute-start(bf16[80,1664]{1,0:T(8,128)(2,1)S(1)} %get-tuple-element.197), channel_id=1, source_target_pairs={{0,2},{1,0},{3,1},{5,3},{7,5},{6,7},{4,6},{2,4},{8,10},{9,8},{11,9... | collective-permute-start | bytes 798728 | tf_op jit(solution)/shard_map/ppermute | solution.py:178
  354.6 12.0 %collective-permute-start.40 = (bf16[80,1664]{1,0:T(8,128)(2,1)S(1)}, bf16[80,1664]{1,0:T(8,128)(2,1)S(1)}, u32[]{:S(2)}, u32[]{:S(2)}) collective-permute-start(bf16[80,1664]{1,0:T(8,128)(2,1)S(1)} %get-tuple-element.198), channel_id=1, source_target_pairs={{0,2},{1,0},{3,1},{5,3},{7,5},{6,7},{4,6},{2,4},{8,10},{9,8},{11,9... | collective-permute-start | bytes 798728 | tf_op jit(solution)/shard_map/ppermute | solution.py:178
  355.7 10.8 %collective-permute-start.31 = (bf16[80,1664]{1,0:T(8,128)(2,1)S(1)}, bf16[80,1664]{1,0:T(8,128)(2,1)S(1)}, u32[]{:S(2)}, u32[]{:S(2)}) collective-permute-start(bf16[80,1664]{1,0:T(8,128)(2,1)S(1)} %get-tuple-element.199), channel_id=1, source_target_pairs={{0,1},{1,3},{3,5},{5,7},{7,6},{6,4},{4,2},{2,0},{8,9},{9,11},{11,1... | collective-permute-start | bytes 798728 | tf_op jit(solution)/shard_map/ppermute | solution.py:178
  357.7 12.9 %collective-permute-start.50 = (bf16[80,1536]{1,0:T(8,128)(2,1)S(1)}, bf16[80,1536]{1,0:T(8,128)(2,1)S(1)}, u32[]{:S(2)}, u32[]{:S(2)}) collective-permute-start(bf16[80,1536]{1,0:T(8,128)(2,1)S(1)} %fusion.105), channel_id=1, source_target_pairs={{0,1},{1,3},{3,5},{5,7},{7,6},{6,4},{4,2},{2,0},{8,9},{9,11},{11,1... | collective-permute-start | bytes 737288 | tf_op jit(solution)/shard_map/ppermute | solution.py:178
  368.1 8.7 %collective-permute-start.59 = (bf16[80,1664]{1,0:T(8,128)(2,1)S(1)}, bf16[80,1664]{1,0:T(8,128)(2,1)S(1)}, u32[]{:S(2)}, u32[]{:S(2)}) collective-permute-start(bf16[80,1664]{1,0:T(8,128)(2,1)S(1)} %get-tuple-element.194), channel_id=1, source_target_pairs={{0,2},{1,0},{3,1},{5,3},{7,5},{6,7},{4,6},{2,4},{8,10},{9,8},{11,9... | collective-permute-start | bytes 798728 | tf_op jit(solution)/shard_map/ppermute | solution.py:178
  368.6 11.1 %collective-permute-start.41 = (bf16[80,1664]{1,0:T(8,128)(2,1)S(1)}, bf16[80,1664]{1,0:T(8,128)(2,1)S(1)}, u32[]{:S(2)}, u32[]{:S(2)}) collective-permute-start(bf16[80,1664]{1,0:T(8,128)(2,1)S(1)} %get-tuple-element.195), channel_id=1, source_target_pairs={{0,2},{1,0},{3,1},{5,3},{7,5},{6,7},{4,6},{2,4},{8,10},{9,8},{11,9... | collective-permute-start | bytes 798728 | tf_op jit(solution)/shard_map/ppermute | solution.py:178
  369.7 10.0 %collective-permute-start.32 = (bf16[80,1664]{1,0:T(8,128)(2,1)S(1)}, bf16[80,1664]{1,0:T(8,128)(2,1)S(1)}, u32[]{:S(2)}, u32[]{:S(2)}) collective-permute-start(bf16[80,1664]{1,0:T(8,128)(2,1)S(1)} %get-tuple-element.196), channel_id=1, source_target_pairs={{0,1},{1,3},{3,5},{5,7},{7,6},{6,4},{4,2},{2,0},{8,9},{9,11},{11,1... | collective-permute-start | bytes 798728 | tf_op jit(solution)/shard_map/ppermute | solution.py:178
  371.7 12.0 %collective-permute-start.51 = (bf16[80,1536]{1,0:T(8,128)(2,1)S(1)}, bf16[80,1536]{1,0:T(8,128)(2,1)S(1)}, u32[]{:S(2)}, u32[]{:S(2)}) collective-permute-start(bf16[80,1536]{1,0:T(8,128)(2,1)S(1)} %fusion.104), channel_id=1, source_target_pairs={{0,1},{1,3},{3,5},{5,7},{7,6},{6,4},{4,2},{2,0},{8,9},{9,11},{11,1... | collective-permute-start | bytes 737288 | tf_op jit(solution)/shard_map/ppermute | solution.py:178
  381.3 7.9 %collective-permute-start.60 = (bf16[80,1664]{1,0:T(8,128)(2,1)S(1)}, bf16[80,1664]{1,0:T(8,128)(2,1)S(1)}, u32[]{:S(2)}, u32[]{:S(2)}) collective-permute-start(bf16[80,1664]{1,0:T(8,128)(2,1)S(1)} %get-tuple-element.191), channel_id=1, source_target_pairs={{0,2},{1,0},{3,1},{5,3},{7,5},{6,7},{4,6},{2,4},{8,10},{9,8},{11,9... | collective-permute-start | bytes 798728 | tf_op jit(solution)/shard_map/ppermute | solution.py:178
  381.8 10.2 %collective-permute-start.42 = (bf16[80,1664]{1,0:T(8,128)(2,1)S(1)}, bf16[80,1664]{1,0:T(8,128)(2,1)S(1)}, u32[]{:S(2)}, u32[]{:S(2)}) collective-permute-start(bf16[80,1664]{1,0:T(8,128)(2,1)S(1)} %get-tuple-element.192), channel_id=1, source_target_pairs={{0,2},{1,0},{3,1},{5,3},{7,5},{6,7},{4,6},{2,4},{8,10},{9,8},{11,9... | collective-permute-start | bytes 798728 | tf_op jit(solution)/shard_map/ppermute | solution.py:178
  382.9 9.1 %collective-permute-start.33 = (bf16[80,1664]{1,0:T(8,128)(2,1)S(1)}, bf16[80,1664]{1,0:T(8,128)(2,1)S(1)}, u32[]{:S(2)}, u32[]{:S(2)}) collective-permute-start(bf16[80,1664]{1,0:T(8,128)(2,1)S(1)} %get-tuple-element.193), channel_id=1, source_target_pairs={{0,1},{1,3},{3,5},{5,7},{7,6},{6,4},{4,2},{2,0},{8,9},{9,11},{11,1... | collective-permute-start | bytes 798728 | tf_op jit(solution)/shard_map/ppermute | solution.py:178
  384.9 11.2 %collective-permute-start.52 = (bf16[80,1536]{1,0:T(8,128)(2,1)S(1)}, bf16[80,1536]{1,0:T(8,128)(2,1)S(1)}, u32[]{:S(2)}, u32[]{:S(2)}) collective-permute-start(bf16[80,1536]{1,0:T(8,128)(2,1)S(1)} %fusion.103), channel_id=1, source_target_pairs={{0,1},{1,3},{3,5},{5,7},{7,6},{6,4},{4,2},{2,0},{8,9},{9,11},{11,1... | collective-permute-start | bytes 737288 | tf_op jit(solution)/shard_map/ppermute | solution.py:178
  393.5 7.0 %collective-permute-start.61 = (bf16[80,1664]{1,0:T(8,128)(2,1)S(1)}, bf16[80,1664]{1,0:T(8,128)(2,1)S(1)}, u32[]{:S(2)}, u32[]{:S(2)}) collective-permute-start(bf16[80,1664]{1,0:T(8,128)(2,1)S(1)} %get-tuple-element.188), channel_id=1, source_target_pairs={{0,2},{1,0},{3,1},{5,3},{7,5},{6,7},{4,6},{2,4},{8,10},{9,8},{11,9... | collective-permute-start | bytes 798728 | tf_op jit(solution)/shard_map/ppermute | solution.py:178
  394.0 10.2 %collective-permute-start.43 = (bf16[80,1664]{1,0:T(8,128)(2,1)S(1)}, bf16[80,1664]{1,0:T(8,128)(2,1)S(1)}, u32[]{:S(2)}, u32[]{:S(2)}) collective-permute-start(bf16[80,1664]{1,0:T(8,128)(2,1)S(1)} %get-tuple-element.189), channel_id=1, source_target_pairs={{0,2},{1,0},{3,1},{5,3},{7,5},{6,7},{4,6},{2,4},{8,10},{9,8},{11,9... | collective-permute-start | bytes 798728 | tf_op jit(solution)/shard_map/ppermute | solution.py:178
  395.2 9.1 %collective-permute-start.34 = (bf16[80,1664]{1,0:T(8,128)(2,1)S(1)}, bf16[80,1664]{1,0:T(8,128)(2,1)S(1)}, u32[]{:S(2)}, u32[]{:S(2)}) collective-permute-start(bf16[80,1664]{1,0:T(8,128)(2,1)S(1)} %get-tuple-element.190), channel_id=1, source_target_pairs={{0,1},{1,3},{3,5},{5,7},{7,6},{6,4},{4,2},{2,0},{8,9},{9,11},{11,1... | collective-permute-start | bytes 798728 | tf_op jit(solution)/shard_map/ppermute | solution.py:178
  397.2 11.2 %collective-permute-start.53 = (bf16[80,1536]{1,0:T(8,128)(2,1)S(1)}, bf16[80,1536]{1,0:T(8,128)(2,1)S(1)}, u32[]{:S(2)}, u32[]{:S(2)}) collective-permute-start(bf16[80,1536]{1,0:T(8,128)(2,1)S(1)} %fusion.102), channel_id=1, source_target_pairs={{0,1},{1,3},{3,5},{5,7},{7,6},{6,4},{4,2},{2,0},{8,9},{9,11},{11,1... | collective-permute-start | bytes 737288 | tf_op jit(solution)/shard_map/ppermute | solution.py:178
  405.8 6.5 collective-permute-start.62
  406.3 8.8 %collective-permute-start.44 = (bf16[80,1664]{1,0:T(8,128)(2,1)S(1)}, bf16[80,1664]{1,0:T(8,128)(2,1)S(1)}, u32[]{:S(2)}, u32[]{:S(2)}) collective-permute-start(bf16[80,1664]{1,0:T(8,128)(2,1)S(1)} %get-tuple-element.186), channel_id=1, source_target_pairs={{0,2},{1,0},{3,1},{5,3},{7,5},{6,7},{4,6},{2,4},{8,10},{9,8},{11,9... | collective-permute-start | bytes 798728 | tf_op jit(solution)/shard_map/ppermute | solution.py:178
  407.4 7.7 %collective-permute-start.35 = (bf16[80,1664]{1,0:T(8,128)(2,1)S(1)}, bf16[80,1664]{1,0:T(8,128)(2,1)S(1)}, u32[]{:S(2)}, u32[]{:S(2)}) collective-permute-start(bf16[80,1664]{1,0:T(8,128)(2,1)S(1)} %get-tuple-element.187), channel_id=1, source_target_pairs={{0,1},{1,3},{3,5},{5,7},{7,6},{6,4},{4,2},{2,0},{8,9},{9,11},{11,1... | collective-permute-start | bytes 798728 | tf_op jit(solution)/shard_map/ppermute | solution.py:178
  409.4 10.8 %collective-permute-start.54 = (bf16[80,1536]{1,0:T(8,128)(2,1)S(1)}, bf16[80,1536]{1,0:T(8,128)(2,1)S(1)}, u32[]{:S(2)}, u32[]{:S(2)}) collective-permute-start(bf16[80,1536]{1,0:T(8,128)(2,1)S(1)} %fusion.121), channel_id=1, source_target_pairs={{0,16},{8,24},{16,0},{24,8},{1,17},{9,25},{17,1},{25,9},{2,18},{10... | collective-permute-start | bytes 737288 | tf_op jit(solution)/shard_map/ppermute | solution.py:181
  416.7 9.3 %collective-permute-start.63 = (bf16[80,1664]{1,0:T(8,128)(2,1)S(1)}, bf16[80,1664]{1,0:T(8,128)(2,1)S(1)}, u32[]{:S(2)}, u32[]{:S(2)}) collective-permute-start(bf16[80,1664]{1,0:T(8,128)(2,1)S(1)} %get-tuple-element.182), channel_id=1, source_target_pairs={{0,16},{8,24},{16,0},{24,8},{1,17},{9,25},{17,1},{25,9},{2,18},{10... | collective-permute-start | bytes 798728 | tf_op jit(solution)/shard_map/ppermute | solution.py:181
  418.2 11.7 %collective-permute-start.45 = (bf16[80,1664]{1,0:T(8,128)(2,1)S(1)}, bf16[80,1664]{1,0:T(8,128)(2,1)S(1)}, u32[]{:S(2)}, u32[]{:S(2)}) collective-permute-start(bf16[80,1664]{1,0:T(8,128)(2,1)S(1)} %get-tuple-element.183), channel_id=1, source_target_pairs={{0,16},{8,24},{16,0},{24,8},{1,17},{9,25},{17,1},{25,9},{2,18},{10... | collective-permute-start | bytes 798728 | tf_op jit(solution)/shard_map/ppermute | solution.py:181
  418.8 14.0 %collective-permute-start.36 = (bf16[80,1664]{1,0:T(8,128)(2,1)S(1)}, bf16[80,1664]{1,0:T(8,128)(2,1)S(1)}, u32[]{:S(2)}, u32[]{:S(2)}) collective-permute-start(bf16[80,1664]{1,0:T(8,128)(2,1)S(1)} %get-tuple-element.184), channel_id=1, source_target_pairs={{0,16},{8,24},{16,0},{24,8},{1,17},{9,25},{17,1},{25,9},{2,18},{10... | collective-permute-start | bytes 798728 | tf_op jit(solution)/shard_map/ppermute | solution.py:181
  421.4 16.8 %collective-permute-start.55 = (f32[80,1536]{1,0:T(8,128)S(1)}, f32[80,1536]{1,0:T(8,128)S(1)}, u32[]{:S(2)}, u32[]{:S(2)}) collective-permute-start(f32[80,1536]{1,0:T(8,128)S(1)} %convert_add_fusion.5), channel_id=1, source_target_pairs={{0,8},{8,0},{16,24},{24,16},{1,9},{9,1},{17,25},{25,17},{2,10},{10... | collective-permute-start | bytes 1474568 | tf_op jit(solution)/shard_map/ppermute | solution.py:184
  435.0 4.0 collective-permute-start.64
  558.4 43.5 %all-to-all-start.1 = ((bf16[8,80,5,160]{3,1,2,0:T(8,128)(2,1)}), bf16[8,80,5,160]{3,1,2,0:T(8,128)(2,1)}, u32[]{:S(2)}, u32[]{:S(2)}) async-start(bf16[8,80,5,160]{3,1,2,0:T(8,128)(2,1)} %copy.156), calls=%async_computation.1 | async-start | bytes 3276800 | tf_op jit(solution)/shard_map/all_to_all | solution.py:452
  601.9 47.8 %collective-permute-start.66 = (bf16[8,80,5,160]{3,1,2,0:T(8,128)(2,1)}, bf16[8,80,5,160]{3,1,2,0:T(8,128)(2,1)}, u32[]{:S(2)}, u32[]{:S(2)}) collective-permute-start(bf16[8,80,5,160]{3,1,2,0:T(8,128)(2,1)} %all-to-all-done.1), channel_id=1, source_target_pairs={{0,8},{8,0},{16,24},{24,16},{1,9},{9,1},{17,25},{25,17},{2,10},{10... | collective-permute-start | bytes 3072008 | tf_op jit(solution)/shard_map/ppermute | solution.py:459
  617.1 4.5 collective-permute-start.71
  (60 other events, 1336.2 us)

commit v3 on v2

--- a/solution.py
+++ b/solution.py
@@ -159,9 +159,9 @@
                 k = step if ahead else count - step
                 got[k] = piece
                 passed[k] = lax.ppermute(piece, "dp", core_pairs)
-            mine_parts.append(jnp.concatenate(got, axis=0))
-            other_parts.append(jnp.concatenate(passed, axis=0))
-        return jnp.concatenate(mine_parts, axis=1), jnp.concatenate(other_parts, axis=1)
+            mine_parts.append(got)
+            other_parts.append(passed)
+        return mine_parts, other_parts
 
     def reduce_scatter(self, full, rows, outer_pairs, core_pairs, parts):
         count = self.count
@@ -251,13 +251,13 @@
             axis=1,
         )
         mine, other = ring.all_gather(packed_local, core, side, core_pairs, 1)
-        full = lax.cond(
-            core == 0,
-            lambda a, b: jnp.concatenate([a, b], axis=1),
-            lambda a, b: jnp.concatenate([b, a], axis=1),
-            mine,
-            other,
-        )
+
+        def assemble(first, second):
+            return jnp.concatenate(
+                [jnp.concatenate(chain, axis=0) for chain in first + second], axis=1
+            )
+
+        full = lax.cond(core == 0, lambda: assemble(mine, other), lambda: assemble(other, mine))
         weights = full[:, lead : lead + weight_cols]
         params = jnp.take(full[:, :small_cols].astype(jnp.float32), natural_of, axis=0)
 
@@ -386,21 +386,37 @@
         small_grads = jnp.concatenate(
             [small_grads, jnp.sum(d_pre.astype(jnp.float32), axis=0).reshape(model_width, -1)], axis=1
         )
-        grad_dev = jnp.concatenate(
-            [
-                jnp.take(small_grads, feature_of, axis=0),
-                jnp.zeros((model_width, lead - small_cols), jnp.float32),
-                contract_rows(normed_rel, d_projected),
-                contract_rows(attended_rel, d_branch),
-                contract_rows(normed_two_rel, d_pre),
-                contract_rows(cotangent_rel, active),
-                jnp.zeros((model_width, lead), jnp.float32),
-            ],
-            axis=1,
-        )
-        keep = lax.dynamic_slice_in_dim(grad_dev, core * side, side, axis=1)
-        send = lax.dynamic_slice_in_dim(grad_dev, (1 - core) * side, side, axis=1)
-        chip = keep + lax.ppermute(send.astype(jnp.bfloat16), "dp", core_pairs).astype(jnp.float32)
+        small_rel = jnp.take(small_grads, feature_of, axis=0)
+        up_first = side - lead - 4 * model_width
+
+        def halves(flip):
+            def build():
+                grad_up = contract_rows(normed_two_rel, d_pre)
+                first = jnp.concatenate(
+                    [
+                        small_rel,
+                        jnp.zeros((model_width, lead - small_cols), jnp.float32),
+                        contract_rows(normed_rel, d_projected),
+                        contract_rows(attended_rel, d_branch),
+                        grad_up[:, :up_first],
+                    ],
+                    axis=1,
+                )
+                second = jnp.concatenate(
+                    [
+                        grad_up[:, up_first:],
+                        contract_rows(cotangent_rel, active),
+                        jnp.zeros((model_width, lead), jnp.float32),
+                    ],
+                    axis=1,
+                )
+                kept, given = (second, first) if flip else (first, second)
+                return kept, given.astype(jnp.bfloat16)
+
+            return build
+
+        keep, send = lax.cond(core == 0, halves(False), halves(True))
+        chip = keep + lax.ppermute(send, "dp", core_pairs).astype(jnp.float32)
         total, partner = ring.reduce_scatter(chip, row_count, outer_pairs, core_pairs, 2)
         joined = lax.cond(
             core == 0,
@@ -432,12 +448,11 @@
             outgoing.astype(jnp.bfloat16), "fsdp", split_axis=1, concat_axis=0, tiled=True
         ).reshape(row_count * devices, owned_slots, quarter)
         incoming_other = lax.ppermute(incoming, "dp", core_pairs)
-        incoming_full = jnp.zeros((row_count * devices, owned_slots, block_width), jnp.bfloat16)
-        incoming_full = lax.dynamic_update_slice(incoming_full, incoming, (0, 0, core * quarter))
-        incoming_full = lax.dynamic_update_slice(
-            incoming_full, incoming_other, (0, 0, (1 - core) * quarter)
-        )
-        incoming = incoming_full.astype(jnp.float32)
+        incoming = lax.cond(
+            core == 0,
+            lambda: jnp.concatenate([incoming, incoming_other], axis=2),
+            lambda: jnp.concatenate([incoming_other, incoming], axis=2),
+        ).astype(jnp.float32)
         my_use = lax.dynamic_slice_in_dim(in_use, lax.axis_index("fsdp") * owned_slots, owned_slots)
         eigen_turned = jnp.einsum("kdi,dkc->kic", left_bases, incoming, precision=OPT_PRECISION)
         eigen_turned = jnp.einsum("kic,kcj->kij", eigen_turned, right_bases, precision=OPT_PRECISION)
@@ -457,10 +472,10 @@
             tiled=True,
         )
         returned_other = lax.ppermute(returned, "dp", core_pairs)
-        returned_full = jnp.zeros((devices, row_count, owned_slots, block_width), jnp.bfloat16)
-        returned_full = lax.dynamic_update_slice(returned_full, returned, (0, 0, 0, core * quarter))
-        returned_full = lax.dynamic_update_slice(
-            returned_full, returned_other, (0, 0, 0, (1 - core) * quarter)
+        returned_full = lax.cond(
+            core == 0,
+            lambda: jnp.concatenate([returned, returned_other], axis=3),
+            lambda: jnp.concatenate([returned_other, returned], axis=3),
         )
         owner_of = block_slots // owned_slots
         slot_in = block_slots % owned_slots

time: 706 us -> 665 us (0.942)
  local copies, waits for them, and re-layouts: 210 us -> 169 us
  waiting for transfers between devices: 171 us -> 181 us
  other arithmetic: 90.5 us -> 83.2 us
    dynamic_update_slice x4 -> x0, local copies, waits for them, and re-layouts: 42.7 us -> none  [the longest x1 22 us: local(): lax.dynamic_update_slice(returned_full, returned_other, (0, 0, 0, (1 - co...]
    cond x1 -> x37, local copies, waits for them, and re-layouts: 1.33 us -> 35.9 us
    unnamed x132 -> x102, local copies, waits for them, and re-layouts: 40.9 us -> 8.25 us
    concatenate x5 -> x4, local copies, waits for them, and re-layouts: 43 us -> 21.6 us  [the longest x1 19.1 us: build(): jnp.concatenate([small_rel, jnp.zeros((model_width, lead - small_cols), j...]
    another operation x0 -> x18, local copies, waits for them, and re-layouts: none -> 15.3 us
    concatenate x2 -> x1, other arithmetic: 17.4 us -> 3.86 us  [local(): jnp.concatenate([a, b], axis=1)]
    slice x0 -> x4, local copies, waits for them, and re-layouts: none -> 11.1 us  [the longest x1 4.89 us: build(): grad_up[:, :up_first]]
    ppermute x14, waiting for transfers between devices: 52.2 us -> 61.8 us  [all_gather(): piece = lax.ppermute(piece, 'fsdp', pairs)]
  transfers between devices with their start and end apart: 73 -> 73, of which waited for: 41 -> 40; matrix products, arithmetic and copies ran while one was open for 16% -> 8% of each run, Pallas kernels for 0% -> 0%
where the time goes in v3:
time: 665 us; the launch traced here: 655 us
  waiting for transfers between devices  181 us (27%)
  local copies, waits for them, and re-layouts  169 us (25%)
  matrix products  113 us (17%)
  other arithmetic  83.2 us (13%)
  starting transfers between devices  61.2 us (9%)
  blocking collectives  42.5 us (6%)
    ppermute x14, waiting for transfers between devices, all_gather(): piece = lax.ppermute(piece, 'fsdp', pairs)  61.8 us
    ppermute x28, waiting for transfers between devices, reduce_scatter(): got = lax.ppermute(acc.astype(jnp.bfloat16), 'fsdp', pairs)  45.8 us
    all_to_all x1, blocking collectives, local(): lax.all_to_all(outgoing.astype(jnp.bfloat16), 'fsdp', split_axis=1, conca...  42.5 us
    all_to_all x1, waiting for transfers between devices, local(): lax.all_to_all(going.reshape(devices, row_count, owned_slots, quarter).as...  31.3 us
    ppermute x28, starting transfers between devices, reduce_scatter(): got = lax.ppermute(acc.astype(jnp.bfloat16), 'fsdp', pairs)  29.1 us
    cond x35, local copies, waits for them, and re-layouts  28.6 us
    concatenate x1, local copies, waits for them, and re-layouts, build(): jnp.concatenate([small_rel, jnp.zeros((model_width, lead - small_cols), j...  19.1 us
    dot_general x1, matrix products, local(): jnp.dot(normed_two_rel, weights[:, 4 * model_width:4 * model_width + hidd...  17 us
  transfers between devices with their start and end apart: 73, of which 40 were waited for; matrix products, arithmetic and copies ran while one was open for 8% of the time, Pallas kernels for 0%

profile of v3, /device:TPU:0, one launch (start us, length us, event | category | flops | bytes accessed | tf_op | source)
XLA Modules:
  0.0 654.7 jit_solution(14601587671581075483)
XLA Ops:
  1.6 3.7 convert_element_type.355
  5.4 4.5 concatenate.93
  11.9 3.0 collective-permute-start
  17.0 10.1 %collective-permute-done = bf16[80,3328]{1,0:T(8,128)(2,1)} collective-permute-done((bf16[80,3328]{1,0:T(8,128)(2,1)S(1)}, bf16[80,3328]{1,0:T(8,128)(2,1)}, u32[]{:S(2)}, u32[]{:S(2)}) %collective-permute-start) | collective-permute-done | bytes 532512 | tf_op jit(solution)/shard_map/ppermute | solution.py:158
  31.2 9.5 %collective-permute-done.2 = bf16[80,3328]{1,0:T(8,128)(2,1)} collective-permute-done((bf16[80,3328]{1,0:T(8,128)(2,1)}, bf16[80,3328]{1,0:T(8,128)(2,1)}, u32[]{:S(2)}, u32[]{:S(2)}) %collective-permute-start.2) | collective-permute-done | bytes 532512 | tf_op jit(solution)/shard_map/ppermute | solution.py:158
  45.2 9.8 %collective-permute-done.16 = bf16[80,3200]{1,0:T(8,128)(2,1)} collective-permute-done((bf16[80,3200]{1,0:T(8,128)(2,1)}, bf16[80,3200]{1,0:T(8,128)(2,1)}, u32[]{:S(2)}, u32[]{:S(2)}) %collective-permute-start.16) | collective-permute-done | bytes 512032 | tf_op jit(solution)/shard_map/ppermute | solution.py:158
  58.4 8.5 %collective-permute-done.17 = bf16[80,3200]{1,0:T(8,128)(2,1)} collective-permute-done((bf16[80,3200]{1,0:T(8,128)(2,1)}, bf16[80,3200]{1,0:T(8,128)(2,1)}, u32[]{:S(2)}, u32[]{:S(2)}) %collective-permute-start.17) | collective-permute-done | bytes 512032 | tf_op jit(solution)/shard_map/ppermute | solution.py:158
  70.5 8.2 %collective-permute-done.18 = bf16[80,3200]{1,0:T(8,128)(2,1)} collective-permute-done((bf16[80,3200]{1,0:T(8,128)(2,1)}, bf16[80,3200]{1,0:T(8,128)(2,1)}, u32[]{:S(2)}, u32[]{:S(2)}) %collective-permute-start.18) | collective-permute-done | bytes 512032 | tf_op jit(solution)/shard_map/ppermute | solution.py:158
  81.6 4.1 scatter_custom_fusion
  92.5 8.3 %collective-permute-done.20 = bf16[80,3200]{1,0:T(8,128)(2,1)} collective-permute-done((bf16[80,3200]{1,0:T(8,128)(2,1)}, bf16[80,3200]{1,0:T(8,128)(2,1)}, u32[]{:S(2)}, u32[]{:S(2)}) %collective-permute-start.20) | collective-permute-done | bytes 512032 | tf_op jit(solution)/shard_map/ppermute | solution.py:158
  104.0 36.9 %conditional.11 = (bf16[640,13056]{1,0:T(8,128)(2,1)}) conditional(s32[]{:T(128)} %convert_element_type.353, (bf16[80,3328]{1,0:T(8,128)(2,1)}, bf16[80,3328]{1,0:T(8,128)(2,1)}, bf16[80,3328]{1,0:T(8,128)(2,1)}, bf16[80,3328]{1,0:T(8,128)(2,1)}, bf16[80,3328]{1,0:T(8,128)(2,1)}, /*index=5*/bf16[80,3328]{1,0:T(8,128)(2,1)}, ...), branch_computations={%region_2.3_spmd, %region_3.4_spmd} | conditional | flops 66846720 | bytes 73072728 | solution.py:260
  134.0 6.7 %pad_maximum_fusion.1 = bf16[640,13056]{1,0:T(8,128)(2,1)} fusion(bf16[640,3200]{1,0:T(8,128)(2,1)S(1)} %get-tuple-element.593, bf16[640,3328]{1,0:T(8,128)(2,1)S(1)} %get-tuple-element.591, bf16[640,3200]{1,0:T(8,128)(2,1)S(1)} %get-tuple-element.592, bf16[640,3328]{1,0:T(8,128)(2,1)S(1)} %get-tuple-element.590), kind=kLoop, calls=%fused_computation.39 | loop fusion | flops 66846720 | bytes 33423360 | tf_op jit(solution)/shard_map/cond/branch_1_fun/concatenate | solution.py:256
  160.2 17.0 %multiply_convert_fusion.1 = (bf16[256,5120]{1,0:T(8,128)(2,1)}, f32[256,5120]{1,0:T(8,128)}, f32[256,5120]{1,0:T(8,128)}) fusion(f32[5120]{0:T(1024)S(1)} %add.409, bf16[256,640]{1,0:T(8,128)(2,1)S(1)} %fusion.54, bf16[640,13056]{1,0:T(8,128)(2,1)} %get-tuple-element.665), kind=kOutput, calls=%fused_computation.98 | convolution fusion | flops 1764229120 | bytes 20008960 | tf_op jit(solution)/shard_map/dot_general | solution.py:297
  177.2 7.3 %convert_reduce_fusion = (f32[5120]{0:T(1024)S(1)}, bf16[256,5120]{1,0:T(8,128)(2,1)S(1)}) fusion(f32[256,5120]{1,0:T(8,128)} %get-tuple-element.585, f32[256,5120]{1,0:T(8,128)} %get-tuple-element.641, bf16[640,256]{1,0:T(8,128)(2,1)S(1)} %copy-done.33, bf16[640,13056]{1,0:T(8,128)(2,1)S(1)} %bitcast.105), kind=kOutput, calls=%fused_computation.93 | convolution fusion | flops 1698688000 | bytes 20008960 | tf_op jit(solution)/shard_map/dot_general | solution.py:342
  193.2 4.5 fusion.56
  197.7 4.0 multiply_reduce_fusion
  213.0 3.1 fusion.32
  231.2 45.0 %conditional.12 = (f32[640,6528]{1,0:T(8,128)}, bf16[640,6528]{1,0:T(8,128)(2,1)}) conditional(s32[]{:T(128)} %convert_element_type.353, (bf16[256,640]{1,0:T(8,128)(2,1)}, bf16[256,5120]{1,0:T(8,128)(2,1)}, bf16[256,640]{0,1:T(8,128)(2,1)S(1)}, bf16[256,5120]{1,0:T(8,128)(2,1)}, bf16[256,640]{1,0:T(8,128)(2,1)}, ...), branch_computations={%region_22.24_spmd, %region_23.25_spmd} | conditional | flops 4219371520 | bytes 174311600
  231.3 4.5 fusion.160
  239.4 4.9 slice.302
  247.1 19.1 %concatenate.76 = f32[640,6528]{1,0:T(8,128)} concatenate(f32[640,16]{1,0:T(8,128)S(1)} %copy-done.22, f32[640,112]{1,0:T(8,128)S(1)} %broadcast.329, f32[640,1920]{1,0:T(8,128)} %fusion.160, f32[640,640]{1,0:T(8,128)} %fusion.161, f32[640,3840]{1,0:T(8,128)} %slice.302), dimensions={1} | concatenate | bytes 33423360 | tf_op jit(solution)/shard_map/cond/branch_1_fun/concatenate | solution.py:395
  266.2 3.6 fusion.163
  271.9 4.1 maximum_maximum_fusion.1
  276.5 13.3 %collective-permute-done.28 = bf16[640,6528]{1,0:T(8,128)(2,1)} collective-permute-done((bf16[640,6528]{1,0:T(8,128)(2,1)}, bf16[640,6528]{1,0:T(8,128)(2,1)}, u32[]{:S(2)}, u32[]{:S(2)}) %collective-permute-start.28) | collective-permute-done | bytes 8355872 | tf_op jit(solution)/shard_map/ppermute | solution.py:419
  289.8 8.9 %fusion.147 = (bf16[640,6528]{1,0:T(8,128)(2,1)S(1)}, f32[640,6528]{1,0:T(8,128)S(1)}) fusion(f32[640,6528]{1,0:T(8,128)} %get-tuple-element.396, bf16[640,6528]{1,0:T(8,128)(2,1)} %collective-permute-done.28), kind=kLoop, calls=%fused_computation.368 | loop fusion | flops 12533760 | bytes 50135040 | tf_op jit(solution)/shard_map/convert.3
  302.9 4.7 collective-permute-done.47
  309.4 4.6 collective-permute-done.38
  320.8 4.1 collective-permute-done.57
  324.9 3.7 collective-permute-done.39
  335.4 4.1 collective-permute-done.58
  349.2 3.2 collective-permute-done.59
  364.4 3.1 collective-permute-done.42
  375.9 3.9 collective-permute-done.43
  397.0 4.5 collective-permute-done.63
  401.5 3.8 collective-permute-done.45
  415.2 5.2 conditional.13
  415.2 3.9 pad_maximum_fusion.7
  420.4 5.0 reshape.453
  425.4 3.4 copy.217
  428.9 4.4 gather_fusion.1
  433.2 3.3 fusion.25
  436.5 42.5 %all_to_all.20 = bf16[80,8,5,160]{3,0,2,1:T(8,128)(2,1)} all-to-all(bf16[80,8,5,160]{3,0,2,1:T(8,128)(2,1)S(1)} %bitcast.106), channel_id=1, replica_groups=mesh['dp'=4,'fsdp'=8] {'fsdp'}, dimensions={1} | all-to-all | bytes 2048000 | tf_op jit(solution)/shard_map/all_to_all | solution.py:447
  479.0 3.7 copy.218
  488.5 20.3 %conditional.14 = (bf16[640,5,320]{0,2,1:T(8,128)(2,1)}) conditional(s32[]{:T(128)} %convert_element_type.353, (bf16[640,5,160]{0,2,1:T(8,128)(2,1)}, bf16[640,5,160]{0,2,1:T(8,128)(2,1)S(1)}) %tuple.78, (bf16[640,5,160]{0,2,1:T(8,128)(2,1)S(1)}, bf16[640,5,160]{0,2,1:T(8,128)(2,1)}) %tuple.79), branch_computations={%region_28.30_spmd, %region_29.31_spmd} | conditional | flops 4096000 | bytes 12288008 | solution.py:451
  488.9 4.7 copy.222
  493.5 3.5 copy.221
  497.1 6.0 pad_maximum_fusion.3
  503.1 5.6 copy.242
  508.8 8.1 %fusion.164 = f32[5,320,640]{2,1,0:T(8,128)S(1)} fusion(bf16[640,5,320]{0,2,1:T(8,128)(2,1)} %get-tuple-element.541, f32[5,640,640]{2,1,0:T(8,128)} %param.40), kind=kOutput, calls=%fused_computation.383 | convolution fusion | flops 3932160000 | bytes 14336000 | tf_op jit(solution)/shard_map/kdi,dkc->kic/dot_general | solution.py:457
  516.9 11.6 %broadcast_select_fusion = (f32[5,640,320]{1,2,0:T(8,128)}, f32[5,640,320]{1,2,0:T(8,128)}, f32[5,640,320]{1,2,0:T(8,128)}) fusion(pred[5]{0:T(512)(128)(4,1)S(1)} %dynamic_slice.39, f32[5,640,320]{1,2,0:T(8,128)S(1)} %copy-done.19, f32[5,640,320]{1,2,0:T(8,128)} %param.38, f32[5,320,640]{2,1,0:T(8,128)S(1)} %fusion.164, f32[5,320,320]{2,1,0:T(8,128)S(1)} %copy-done), kind=kOutput, calls=%fused_computation.141 | convolution fusion | flops 1974272000 | bytes 26624004 | tf_op jit(solution)/shard_map/kic,kcj->kij/dot_general | solution.py:458
  528.5 9.8 %fusion.17 = f32[5,640,320]{1,2,0:T(8,128)S(1)} fusion(f32[5,320,320]{2,1,0:T(8,128)S(1)} %copy-done, f32[5,640,320]{1,2,0:T(8,128)} %get-tuple-element.648, f32[5,640,320]{1,2,0:T(8,128)} %param.38, f32[5,640,320]{1,2,0:T(8,128)S(1)} %copy-done.19), kind=kOutput, calls=%fused_computation.118 | convolution fusion | flops 1976320000 | bytes 18432000 | tf_op jit(solution)/shard_map/kij,klj->kil/dot_general | solution.py:462
  538.3 8.6 %fusion.165 = bf16[5,320,640]{2,1,0:T(8,128)(2,1)S(1)} fusion(f32[5,640,320]{1,2,0:T(8,128)S(1)} %fusion.17, f32[5,640,640]{2,1,0:T(8,128)S(1)} %bitcast.103), kind=kOutput, calls=%fused_computation.384 | convolution fusion | flops 3932160000 | bytes 14336000 | tf_op jit(solution)/shard_map/kdi,kil->dkl/dot_general | solution.py:463
  549.6 3.9 copy.225
  553.5 4.6 all-to-all-start.1
  558.1 5.9 fusion.2
  565.7 31.3 %all-to-all-done.1 = bf16[8,80,5,160]{3,1,2,0:T(8,128)(2,1)} async-done(((bf16[8,80,5,160]{3,1,2,0:T(8,128)(2,1)}), bf16[8,80,5,160]{3,1,2,0:T(8,128)(2,1)}, u32[]{:S(2)}, u32[]{:S(2)}) %all-to-all-start.1) | async-done | bytes 1024032 | tf_op jit(solution)/shard_map/all_to_all | solution.py:467
  608.8 3.6 collective-permute-done.70
  613.2 3.6 collective-permute-done.71
  619.3 3.5 copy.216
  624.1 7.9 %conditional.15 = (bf16[8,80,5,320]{3,1,2,0:T(8,128)(2,1)}) conditional(s32[]{:T(128)} %convert_element_type.353, (bf16[8,80,5,160]{3,1,2,0:T(8,128)(2,1)}, bf16[8,80,5,160]{3,1,2,0:T(8,128)(2,1)}) %tuple.80, (bf16[8,80,5,160]{3,1,2,0:T(8,128)(2,1)}, bf16[8,80,5,160]{3,1,2,0:T(8,128)(2,1)}) %tuple.81), branch_computations={%region_30.32_spmd, %region_31.33_spmd} | conditional | flops 4096000 | bytes 12288008 | solution.py:475
  632.0 4.3 gather_fusion.2
  638.4 3.7 copy.231
  642.2 5.5 mul.324
  647.7 6.5 fusion.146
  (420 shorter events, 239.3 us)
Async XLA Ops:
  11.9 15.3 %collective-permute-start = (bf16[80,3328]{1,0:T(8,128)(2,1)S(1)}, bf16[80,3328]{1,0:T(8,128)(2,1)}, u32[]{:S(2)}, u32[]{:S(2)}) collective-permute-start(bf16[80,3328]{1,0:T(8,128)(2,1)S(1)} %get-tuple-element.625), channel_id=1, source_target_pairs={{0,1},{1,3},{3,5},{5,7},{7,6},{6,4},{4,2},{2,0},{8,9},{9,11},{11,1... | collective-permute-start | bytes 1597448 | tf_op jit(solution)/shard_map/ppermute | solution.py:158
  17.0 13.1 %collective-permute-start.14 = (bf16[80,3200]{1,0:T(8,128)(2,1)S(1)}, bf16[80,3200]{1,0:T(8,128)(2,1)S(1)}, u32[]{:S(2)}, u32[]{:S(2)}) collective-permute-start(bf16[80,3200]{1,0:T(8,128)(2,1)S(1)} %get-tuple-element.623), channel_id=1, source_target_pairs={{0,2},{1,0},{3,1},{5,3},{7,5},{6,7},{4,6},{2,4},{8,10},{9,8},{11,9... | collective-permute-start | bytes 1536008 | tf_op jit(solution)/shard_map/ppermute | solution.py:158
  27.2 13.6 %collective-permute-start.2 = (bf16[80,3328]{1,0:T(8,128)(2,1)}, bf16[80,3328]{1,0:T(8,128)(2,1)}, u32[]{:S(2)}, u32[]{:S(2)}) collective-permute-start(bf16[80,3328]{1,0:T(8,128)(2,1)} %collective-permute-done), channel_id=1, source_target_pairs={{0,1},{1,3},{3,5},{5,7},{7,6},{6,4},{4,2},{2,0},{8,9},{9,11},{11,1... | collective-permute-start | bytes 1597448 | tf_op jit(solution)/shard_map/ppermute | solution.py:158
  30.9 12.4 %collective-permute-start.15 = (bf16[80,3200]{1,0:T(8,128)(2,1)S(1)}, bf16[80,3200]{1,0:T(8,128)(2,1)}, u32[]{:S(2)}, u32[]{:S(2)}) collective-permute-start(bf16[80,3200]{1,0:T(8,128)(2,1)S(1)} %collective-permute-done.14), channel_id=1, source_target_pairs={{0,2},{1,0},{3,1},{5,3},{7,5},{6,7},{4,6},{2,4},{8,10},{9,8},{11,9... | collective-permute-start | bytes 1536008 | tf_op jit(solution)/shard_map/ppermute | solution.py:158
  40.8 15.1 %collective-permute-start.4 = (bf16[80,3328]{1,0:T(8,128)(2,1)}, bf16[80,3328]{1,0:T(8,128)(2,1)}, u32[]{:S(2)}, u32[]{:S(2)}) collective-permute-start(bf16[80,3328]{1,0:T(8,128)(2,1)} %collective-permute-done.2), channel_id=1, source_target_pairs={{0,1},{1,3},{3,5},{5,7},{7,6},{6,4},{4,2},{2,0},{8,9},{9,11},{11,1... | collective-permute-start | bytes 1597448 | tf_op jit(solution)/shard_map/ppermute | solution.py:158
  43.2 11.8 %collective-permute-start.16 = (bf16[80,3200]{1,0:T(8,128)(2,1)}, bf16[80,3200]{1,0:T(8,128)(2,1)}, u32[]{:S(2)}, u32[]{:S(2)}) collective-permute-start(bf16[80,3200]{1,0:T(8,128)(2,1)} %collective-permute-done.15), channel_id=1, source_target_pairs={{0,2},{1,0},{3,1},{5,3},{7,5},{6,7},{4,6},{2,4},{8,10},{9,8},{11,9... | collective-permute-start | bytes 1536008 | tf_op jit(solution)/shard_map/ppermute | solution.py:158
  55.1 11.8 %collective-permute-start.17 = (bf16[80,3200]{1,0:T(8,128)(2,1)}, bf16[80,3200]{1,0:T(8,128)(2,1)}, u32[]{:S(2)}, u32[]{:S(2)}) collective-permute-start(bf16[80,3200]{1,0:T(8,128)(2,1)} %collective-permute-done.16), channel_id=1, source_target_pairs={{0,2},{1,0},{3,1},{5,3},{7,5},{6,7},{4,6},{2,4},{8,10},{9,8},{11,9... | collective-permute-start | bytes 1536008 | tf_op jit(solution)/shard_map/ppermute | solution.py:158
  55.9 12.3 %collective-permute-start.6 = (bf16[80,3328]{1,0:T(8,128)(2,1)}, bf16[80,3328]{1,0:T(8,128)(2,1)}, u32[]{:S(2)}, u32[]{:S(2)}) collective-permute-start(bf16[80,3328]{1,0:T(8,128)(2,1)} %collective-permute-done.4), channel_id=1, source_target_pairs={{0,1},{1,3},{3,5},{5,7},{7,6},{6,4},{4,2},{2,0},{8,9},{9,11},{11,1... | collective-permute-start | bytes 1597448 | tf_op jit(solution)/shard_map/ppermute | solution.py:158
  57.8 12.0 %collective-permute-start.27 = (bf16[80,3200]{1,0:T(8,128)(2,1)}, bf16[80,3200]{1,0:T(8,128)(2,1)}, u32[]{:S(2)}, u32[]{:S(2)}) collective-permute-start(bf16[80,3200]{1,0:T(8,128)(2,1)} %copy-done.30), channel_id=1, source_target_pairs={{0,8},{8,0},{16,24},{24,16},{1,9},{9,1},{17,25},{25,17},{2,10},{10... | collective-permute-start | bytes 1536008 | tf_op jit(solution)/shard_map/ppermute | solution.py:161
  57.9 12.1 %collective-permute-start.1 = (bf16[80,3328]{1,0:T(8,128)(2,1)}, bf16[80,3328]{1,0:T(8,128)(2,1)}, u32[]{:S(2)}, u32[]{:S(2)}) collective-permute-start(bf16[80,3328]{1,0:T(8,128)(2,1)} %collective-permute-done), channel_id=1, source_target_pairs={{0,8},{8,0},{16,24},{24,16},{1,9},{9,1},{17,25},{25,17},{2,10},{10... | collective-permute-start | bytes 1597448 | tf_op jit(solution)/shard_map/ppermute | solution.py:161
  58.4 12.1 %collective-permute-start.26 = (bf16[80,3200]{1,0:T(8,128)(2,1)}, bf16[80,3200]{1,0:T(8,128)(2,1)}, u32[]{:S(2)}, u32[]{:S(2)}) collective-permute-start(bf16[80,3200]{1,0:T(8,128)(2,1)} %collective-permute-done.15), channel_id=1, source_target_pairs={{0,8},{8,0},{16,24},{24,16},{1,9},{9,1},{17,25},{25,17},{2,10},{10... | collective-permute-start | bytes 1536008 | tf_op jit(solution)/shard_map/ppermute | solution.py:161
  66.9 11.8 %collective-permute-start.18 = (bf16[80,3200]{1,0:T(8,128)(2,1)}, bf16[80,3200]{1,0:T(8,128)(2,1)}, u32[]{:S(2)}, u32[]{:S(2)}) collective-permute-start(bf16[80,3200]{1,0:T(8,128)(2,1)} %collective-permute-done.17), channel_id=1, source_target_pairs={{0,2},{1,0},{3,1},{5,3},{7,5},{6,7},{4,6},{2,4},{8,10},{9,8},{11,9... | collective-permute-start | bytes 1536008 | tf_op jit(solution)/shard_map/ppermute | solution.py:158
  68.1 12.3 %collective-permute-start.8 = (bf16[80,3328]{1,0:T(8,128)(2,1)}, bf16[80,3328]{1,0:T(8,128)(2,1)}, u32[]{:S(2)}, u32[]{:S(2)}) collective-permute-start(bf16[80,3328]{1,0:T(8,128)(2,1)} %collective-permute-done.6), channel_id=1, source_target_pairs={{0,1},{1,3},{3,5},{5,7},{7,6},{6,4},{4,2},{2,0},{8,9},{9,11},{11,1... | collective-permute-start | bytes 1597448 | tf_op jit(solution)/shard_map/ppermute | solution.py:158
  69.9 15.9 %collective-permute-start.3 = (bf16[80,3328]{1,0:T(8,128)(2,1)}, bf16[80,3328]{1,0:T(8,128)(2,1)}, u32[]{:S(2)}, u32[]{:S(2)}) collective-permute-start(bf16[80,3328]{1,0:T(8,128)(2,1)} %collective-permute-done.2), channel_id=1, source_target_pairs={{0,8},{8,0},{16,24},{24,16},{1,9},{9,1},{17,25},{25,17},{2,10},{10... | collective-permute-start | bytes 1597448 | tf_op jit(solution)/shard_map/ppermute | solution.py:161
  69.9 15.9 %collective-permute-start.25 = (bf16[80,3200]{1,0:T(8,128)(2,1)}, bf16[80,3200]{1,0:T(8,128)(2,1)}, u32[]{:S(2)}, u32[]{:S(2)}) collective-permute-start(bf16[80,3200]{1,0:T(8,128)(2,1)} %collective-permute-done.16), channel_id=1, source_target_pairs={{0,8},{8,0},{16,24},{24,16},{1,9},{9,1},{17,25},{25,17},{2,10},{10... | collective-permute-start | bytes 1536008 | tf_op jit(solution)/shard_map/ppermute | solution.py:161
  70.4 15.9 %collective-permute-start.5 = (bf16[80,3328]{1,0:T(8,128)(2,1)}, bf16[80,3328]{1,0:T(8,128)(2,1)}, u32[]{:S(2)}, u32[]{:S(2)}) collective-permute-start(bf16[80,3328]{1,0:T(8,128)(2,1)} %collective-permute-done.4), channel_id=1, source_target_pairs={{0,8},{8,0},{16,24},{24,16},{1,9},{9,1},{17,25},{25,17},{2,10},{10... | collective-permute-start | bytes 1597448 | tf_op jit(solution)/shard_map/ppermute | solution.py:161
  78.7 9.4 %collective-permute-start.19 = (bf16[80,3200]{1,0:T(8,128)(2,1)}, bf16[80,3200]{1,0:T(8,128)(2,1)}, u32[]{:S(2)}, u32[]{:S(2)}) collective-permute-start(bf16[80,3200]{1,0:T(8,128)(2,1)} %collective-permute-done.18), channel_id=1, source_target_pairs={{0,2},{1,0},{3,1},{5,3},{7,5},{6,7},{4,6},{2,4},{8,10},{9,8},{11,9... | collective-permute-start | bytes 1536008 | tf_op jit(solution)/shard_map/ppermute | solution.py:158
  80.4 9.6 %collective-permute-start.10 = (bf16[80,3328]{1,0:T(8,128)(2,1)}, bf16[80,3328]{1,0:T(8,128)(2,1)}, u32[]{:S(2)}, u32[]{:S(2)}) collective-permute-start(bf16[80,3328]{1,0:T(8,128)(2,1)} %collective-permute-done.8), channel_id=1, source_target_pairs={{0,1},{1,3},{3,5},{5,7},{7,6},{6,4},{4,2},{2,0},{8,9},{9,11},{11,1... | collective-permute-start | bytes 1597448 | tf_op jit(solution)/shard_map/ppermute | solution.py:158
  85.8 6.0 collective-permute-start.24
  85.8 6.0 collective-permute-start.7
  86.3 6.0 collective-permute-start.23
  88.1 12.6 %collective-permute-start.20 = (bf16[80,3200]{1,0:T(8,128)(2,1)}, bf16[80,3200]{1,0:T(8,128)(2,1)}, u32[]{:S(2)}, u32[]{:S(2)}) collective-permute-start(bf16[80,3200]{1,0:T(8,128)(2,1)} %collective-permute-done.19), channel_id=1, source_target_pairs={{0,2},{1,0},{3,1},{5,3},{7,5},{6,7},{4,6},{2,4},{8,10},{9,8},{11,9... | collective-permute-start | bytes 1536008 | tf_op jit(solution)/shard_map/ppermute | solution.py:158
  90.0 11.7 %collective-permute-start.12 = (bf16[80,3328]{1,0:T(8,128)(2,1)}, bf16[80,3328]{1,0:T(8,128)(2,1)}, u32[]{:S(2)}, u32[]{:S(2)}) collective-permute-start(bf16[80,3328]{1,0:T(8,128)(2,1)} %collective-permute-done.10), channel_id=1, source_target_pairs={{0,1},{1,3},{3,5},{5,7},{7,6},{6,4},{4,2},{2,0},{8,9},{9,11},{11,1... | collective-permute-start | bytes 1597448 | tf_op jit(solution)/shard_map/ppermute | solution.py:158
  91.8 12.2 %collective-permute-start.9 = (bf16[80,3328]{1,0:T(8,128)(2,1)}, bf16[80,3328]{1,0:T(8,128)(2,1)}, u32[]{:S(2)}, u32[]{:S(2)}) collective-permute-start(bf16[80,3328]{1,0:T(8,128)(2,1)} %collective-permute-done.8), channel_id=1, source_target_pairs={{0,8},{8,0},{16,24},{24,16},{1,9},{9,1},{17,25},{25,17},{2,10},{10... | collective-permute-start | bytes 1597448 | tf_op jit(solution)/shard_map/ppermute | solution.py:161
  91.9 12.1 %collective-permute-start.22 = (bf16[80,3200]{1,0:T(8,128)(2,1)}, bf16[80,3200]{1,0:T(8,128)(2,1)}, u32[]{:S(2)}, u32[]{:S(2)}) collective-permute-start(bf16[80,3200]{1,0:T(8,128)(2,1)} %collective-permute-done.19), channel_id=1, source_target_pairs={{0,8},{8,0},{16,24},{24,16},{1,9},{9,1},{17,25},{25,17},{2,10},{10... | collective-permute-start | bytes 1536008 | tf_op jit(solution)/shard_map/ppermute | solution.py:161
  92.4 11.6 %collective-permute-start.11 = (bf16[80,3328]{1,0:T(8,128)(2,1)}, bf16[80,3328]{1,0:T(8,128)(2,1)}, u32[]{:S(2)}, u32[]{:S(2)}) collective-permute-start(bf16[80,3328]{1,0:T(8,128)(2,1)} %collective-permute-done.10), channel_id=1, source_target_pairs={{0,8},{8,0},{16,24},{24,16},{1,9},{9,1},{17,25},{25,17},{2,10},{10... | collective-permute-start | bytes 1597448 | tf_op jit(solution)/shard_map/ppermute | solution.py:161
  276.2 13.5 %collective-permute-start.28 = (bf16[640,6528]{1,0:T(8,128)(2,1)}, bf16[640,6528]{1,0:T(8,128)(2,1)}, u32[]{:S(2)}, u32[]{:S(2)}) collective-permute-start(bf16[640,6528]{1,0:T(8,128)(2,1)} %get-tuple-element.397), channel_id=1, source_target_pairs={{0,8},{8,0},{16,24},{24,16},{1,9},{9,1},{17,25},{25,17},{2,10},{10... | collective-permute-start | bytes 25067528 | tf_op jit(solution)/shard_map/ppermute | solution.py:419
  298.7 8.9 %collective-permute-start.47 = (bf16[80,1536]{1,0:T(8,128)(2,1)S(1)}, bf16[80,1536]{1,0:T(8,128)(2,1)S(1)}, u32[]{:S(2)}, u32[]{:S(2)}) collective-permute-start(bf16[80,1536]{1,0:T(8,128)(2,1)S(1)} %slice.339), channel_id=1, source_target_pairs={{0,1},{1,3},{3,5},{5,7},{7,6},{6,4},{4,2},{2,0},{8,9},{9,11},{11,1... | collective-permute-start | bytes 737288 | tf_op jit(solution)/shard_map/ppermute | solution.py:178
  300.1 9.3 %collective-permute-start.56 = (bf16[80,1664]{1,0:T(8,128)(2,1)S(1)}, bf16[80,1664]{1,0:T(8,128)(2,1)S(1)}, u32[]{:S(2)}, u32[]{:S(2)}) collective-permute-start(bf16[80,1664]{1,0:T(8,128)(2,1)S(1)} %get-tuple-element.618), channel_id=1, source_target_pairs={{0,2},{1,0},{3,1},{5,3},{7,5},{6,7},{4,6},{2,4},{8,10},{9,8},{11,9... | collective-permute-start | bytes 798728 | tf_op jit(solution)/shard_map/ppermute | solution.py:178
  300.9 13.1 %collective-permute-start.38 = (bf16[80,1664]{1,0:T(8,128)(2,1)S(1)}, bf16[80,1664]{1,0:T(8,128)(2,1)S(1)}, u32[]{:S(2)}, u32[]{:S(2)}) collective-permute-start(bf16[80,1664]{1,0:T(8,128)(2,1)S(1)} %get-tuple-element.619), channel_id=1, source_target_pairs={{0,2},{1,0},{3,1},{5,3},{7,5},{6,7},{4,6},{2,4},{8,10},{9,8},{11,9... | collective-permute-start | bytes 798728 | tf_op jit(solution)/shard_map/ppermute | solution.py:178
  302.1 11.9 %collective-permute-start.29 = (bf16[80,1664]{1,0:T(8,128)(2,1)S(1)}, bf16[80,1664]{1,0:T(8,128)(2,1)S(1)}, u32[]{:S(2)}, u32[]{:S(2)}) collective-permute-start(bf16[80,1664]{1,0:T(8,128)(2,1)S(1)} %get-tuple-element.620), channel_id=1, source_target_pairs={{0,1},{1,3},{3,5},{5,7},{7,6},{6,4},{4,2},{2,0},{8,9},{9,11},{11,1... | collective-permute-start | bytes 798728 | tf_op jit(solution)/shard_map/ppermute | solution.py:178
  307.6 10.8 %collective-permute-start.48 = (bf16[80,1536]{1,0:T(8,128)(2,1)S(1)}, bf16[80,1536]{1,0:T(8,128)(2,1)S(1)}, u32[]{:S(2)}, u32[]{:S(2)}) collective-permute-start(bf16[80,1536]{1,0:T(8,128)(2,1)S(1)} %fusion.107), channel_id=1, source_target_pairs={{0,1},{1,3},{3,5},{5,7},{7,6},{6,4},{4,2},{2,0},{8,9},{9,11},{11,1... | collective-permute-start | bytes 737288 | tf_op jit(solution)/shard_map/ppermute | solution.py:178
  315.6 9.3 %collective-permute-start.57 = (bf16[80,1664]{1,0:T(8,128)(2,1)S(1)}, bf16[80,1664]{1,0:T(8,128)(2,1)S(1)}, u32[]{:S(2)}, u32[]{:S(2)}) collective-permute-start(bf16[80,1664]{1,0:T(8,128)(2,1)S(1)} %get-tuple-element.615), channel_id=1, source_target_pairs={{0,2},{1,0},{3,1},{5,3},{7,5},{6,7},{4,6},{2,4},{8,10},{9,8},{11,9... | collective-permute-start | bytes 798728 | tf_op jit(solution)/shard_map/ppermute | solution.py:178
  316.3 12.3 %collective-permute-start.39 = (bf16[80,1664]{1,0:T(8,128)(2,1)S(1)}, bf16[80,1664]{1,0:T(8,128)(2,1)S(1)}, u32[]{:S(2)}, u32[]{:S(2)}) collective-permute-start(bf16[80,1664]{1,0:T(8,128)(2,1)S(1)} %get-tuple-element.616), channel_id=1, source_target_pairs={{0,2},{1,0},{3,1},{5,3},{7,5},{6,7},{4,6},{2,4},{8,10},{9,8},{11,9... | collective-permute-start | bytes 798728 | tf_op jit(solution)/shard_map/ppermute | solution.py:178
  317.7 10.9 %collective-permute-start.30 = (bf16[80,1664]{1,0:T(8,128)(2,1)S(1)}, bf16[80,1664]{1,0:T(8,128)(2,1)S(1)}, u32[]{:S(2)}, u32[]{:S(2)}) collective-permute-start(bf16[80,1664]{1,0:T(8,128)(2,1)S(1)} %get-tuple-element.617), channel_id=1, source_target_pairs={{0,1},{1,3},{3,5},{5,7},{7,6},{6,4},{4,2},{2,0},{8,9},{9,11},{11,1... | collective-permute-start | bytes 798728 | tf_op jit(solution)/shard_map/ppermute | solution.py:178
  319.5 13.5 %collective-permute-start.49 = (bf16[80,1536]{1,0:T(8,128)(2,1)S(1)}, bf16[80,1536]{1,0:T(8,128)(2,1)S(1)}, u32[]{:S(2)}, u32[]{:S(2)}) collective-permute-start(bf16[80,1536]{1,0:T(8,128)(2,1)S(1)} %fusion.106), channel_id=1, source_target_pairs={{0,1},{1,3},{3,5},{5,7},{7,6},{6,4},{4,2},{2,0},{8,9},{9,11},{11,1... | collective-permute-start | bytes 737288 | tf_op jit(solution)/shard_map/ppermute | solution.py:178
  330.2 9.3 %collective-permute-start.58 = (bf16[80,1664]{1,0:T(8,128)(2,1)S(1)}, bf16[80,1664]{1,0:T(8,128)(2,1)S(1)}, u32[]{:S(2)}, u32[]{:S(2)}) collective-permute-start(bf16[80,1664]{1,0:T(8,128)(2,1)S(1)} %get-tuple-element.612), channel_id=1, source_target_pairs={{0,2},{1,0},{3,1},{5,3},{7,5},{6,7},{4,6},{2,4},{8,10},{9,8},{11,9... | collective-permute-start | bytes 798728 | tf_op jit(solution)/shard_map/ppermute | solution.py:178
  330.9 11.4 %collective-permute-start.40 = (bf16[80,1664]{1,0:T(8,128)(2,1)S(1)}, bf16[80,1664]{1,0:T(8,128)(2,1)S(1)}, u32[]{:S(2)}, u32[]{:S(2)}) collective-permute-start(bf16[80,1664]{1,0:T(8,128)(2,1)S(1)} %get-tuple-element.613), channel_id=1, source_target_pairs={{0,2},{1,0},{3,1},{5,3},{7,5},{6,7},{4,6},{2,4},{8,10},{9,8},{11,9... | collective-permute-start | bytes 798728 | tf_op jit(solution)/shard_map/ppermute | solution.py:178
  332.2 10.2 %collective-permute-start.31 = (bf16[80,1664]{1,0:T(8,128)(2,1)S(1)}, bf16[80,1664]{1,0:T(8,128)(2,1)S(1)}, u32[]{:S(2)}, u32[]{:S(2)}) collective-permute-start(bf16[80,1664]{1,0:T(8,128)(2,1)S(1)} %get-tuple-element.614), channel_id=1, source_target_pairs={{0,1},{1,3},{3,5},{5,7},{7,6},{6,4},{4,2},{2,0},{8,9},{9,11},{11,1... | collective-permute-start | bytes 798728 | tf_op jit(solution)/shard_map/ppermute | solution.py:178
  334.1 12.7 %collective-permute-start.50 = (bf16[80,1536]{1,0:T(8,128)(2,1)S(1)}, bf16[80,1536]{1,0:T(8,128)(2,1)S(1)}, u32[]{:S(2)}, u32[]{:S(2)}) collective-permute-start(bf16[80,1536]{1,0:T(8,128)(2,1)S(1)} %fusion.105), channel_id=1, source_target_pairs={{0,1},{1,3},{3,5},{5,7},{7,6},{6,4},{4,2},{2,0},{8,9},{9,11},{11,1... | collective-permute-start | bytes 737288 | tf_op jit(solution)/shard_map/ppermute | solution.py:178
  343.9 8.5 %collective-permute-start.59 = (bf16[80,1664]{1,0:T(8,128)(2,1)S(1)}, bf16[80,1664]{1,0:T(8,128)(2,1)S(1)}, u32[]{:S(2)}, u32[]{:S(2)}) collective-permute-start(bf16[80,1664]{1,0:T(8,128)(2,1)S(1)} %get-tuple-element.609), channel_id=1, source_target_pairs={{0,2},{1,0},{3,1},{5,3},{7,5},{6,7},{4,6},{2,4},{8,10},{9,8},{11,9... | collective-permute-start | bytes 798728 | tf_op jit(solution)/shard_map/ppermute | solution.py:178
  344.7 10.6 %collective-permute-start.41 = (bf16[80,1664]{1,0:T(8,128)(2,1)S(1)}, bf16[80,1664]{1,0:T(8,128)(2,1)S(1)}, u32[]{:S(2)}, u32[]{:S(2)}) collective-permute-start(bf16[80,1664]{1,0:T(8,128)(2,1)S(1)} %get-tuple-element.610), channel_id=1, source_target_pairs={{0,2},{1,0},{3,1},{5,3},{7,5},{6,7},{4,6},{2,4},{8,10},{9,8},{11,9... | collective-permute-start | bytes 798728 | tf_op jit(solution)/shard_map/ppermute | solution.py:178
  345.8 9.4 %collective-permute-start.32 = (bf16[80,1664]{1,0:T(8,128)(2,1)S(1)}, bf16[80,1664]{1,0:T(8,128)(2,1)S(1)}, u32[]{:S(2)}, u32[]{:S(2)}) collective-permute-start(bf16[80,1664]{1,0:T(8,128)(2,1)S(1)} %get-tuple-element.611), channel_id=1, source_target_pairs={{0,1},{1,3},{3,5},{5,7},{7,6},{6,4},{4,2},{2,0},{8,9},{9,11},{11,1... | collective-permute-start | bytes 798728 | tf_op jit(solution)/shard_map/ppermute | solution.py:178
  347.8 11.8 %collective-permute-start.51 = (bf16[80,1536]{1,0:T(8,128)(2,1)S(1)}, bf16[80,1536]{1,0:T(8,128)(2,1)S(1)}, u32[]{:S(2)}, u32[]{:S(2)}) collective-permute-start(bf16[80,1536]{1,0:T(8,128)(2,1)S(1)} %fusion.104), channel_id=1, source_target_pairs={{0,1},{1,3},{3,5},{5,7},{7,6},{6,4},{4,2},{2,0},{8,9},{9,11},{11,1... | collective-permute-start | bytes 737288 | tf_op jit(solution)/shard_map/ppermute | solution.py:178
  356.8 7.6 %collective-permute-start.60 = (bf16[80,1664]{1,0:T(8,128)(2,1)S(1)}, bf16[80,1664]{1,0:T(8,128)(2,1)S(1)}, u32[]{:S(2)}, u32[]{:S(2)}) collective-permute-start(bf16[80,1664]{1,0:T(8,128)(2,1)S(1)} %get-tuple-element.606), channel_id=1, source_target_pairs={{0,2},{1,0},{3,1},{5,3},{7,5},{6,7},{4,6},{2,4},{8,10},{9,8},{11,9... | collective-permute-start | bytes 798728 | tf_op jit(solution)/shard_map/ppermute | solution.py:178
  357.6 9.9 %collective-permute-start.42 = (bf16[80,1664]{1,0:T(8,128)(2,1)S(1)}, bf16[80,1664]{1,0:T(8,128)(2,1)S(1)}, u32[]{:S(2)}, u32[]{:S(2)}) collective-permute-start(bf16[80,1664]{1,0:T(8,128)(2,1)S(1)} %get-tuple-element.607), channel_id=1, source_target_pairs={{0,2},{1,0},{3,1},{5,3},{7,5},{6,7},{4,6},{2,4},{8,10},{9,8},{11,9... | collective-permute-start | bytes 798728 | tf_op jit(solution)/shard_map/ppermute | solution.py:178
  358.6 8.9 %collective-permute-start.33 = (bf16[80,1664]{1,0:T(8,128)(2,1)S(1)}, bf16[80,1664]{1,0:T(8,128)(2,1)S(1)}, u32[]{:S(2)}, u32[]{:S(2)}) collective-permute-start(bf16[80,1664]{1,0:T(8,128)(2,1)S(1)} %get-tuple-element.608), channel_id=1, source_target_pairs={{0,1},{1,3},{3,5},{5,7},{7,6},{6,4},{4,2},{2,0},{8,9},{9,11},{11,1... | collective-permute-start | bytes 798728 | tf_op jit(solution)/shard_map/ppermute | solution.py:178
  360.7 11.2 %collective-permute-start.52 = (bf16[80,1536]{1,0:T(8,128)(2,1)S(1)}, bf16[80,1536]{1,0:T(8,128)(2,1)S(1)}, u32[]{:S(2)}, u32[]{:S(2)}) collective-permute-start(bf16[80,1536]{1,0:T(8,128)(2,1)S(1)} %fusion.103), channel_id=1, source_target_pairs={{0,1},{1,3},{3,5},{5,7},{7,6},{6,4},{4,2},{2,0},{8,9},{9,11},{11,1... | collective-permute-start | bytes 737288 | tf_op jit(solution)/shard_map/ppermute | solution.py:178
  369.1 6.8 %collective-permute-start.61 = (bf16[80,1664]{1,0:T(8,128)(2,1)S(1)}, bf16[80,1664]{1,0:T(8,128)(2,1)S(1)}, u32[]{:S(2)}, u32[]{:S(2)}) collective-permute-start(bf16[80,1664]{1,0:T(8,128)(2,1)S(1)} %get-tuple-element.603), channel_id=1, source_target_pairs={{0,2},{1,0},{3,1},{5,3},{7,5},{6,7},{4,6},{2,4},{8,10},{9,8},{11,9... | collective-permute-start | bytes 798728 | tf_op jit(solution)/shard_map/ppermute | solution.py:178
  369.9 9.9 %collective-permute-start.43 = (bf16[80,1664]{1,0:T(8,128)(2,1)S(1)}, bf16[80,1664]{1,0:T(8,128)(2,1)S(1)}, u32[]{:S(2)}, u32[]{:S(2)}) collective-permute-start(bf16[80,1664]{1,0:T(8,128)(2,1)S(1)} %get-tuple-element.604), channel_id=1, source_target_pairs={{0,2},{1,0},{3,1},{5,3},{7,5},{6,7},{4,6},{2,4},{8,10},{9,8},{11,9... | collective-permute-start | bytes 798728 | tf_op jit(solution)/shard_map/ppermute | solution.py:178
  370.9 8.9 %collective-permute-start.34 = (bf16[80,1664]{1,0:T(8,128)(2,1)S(1)}, bf16[80,1664]{1,0:T(8,128)(2,1)S(1)}, u32[]{:S(2)}, u32[]{:S(2)}) collective-permute-start(bf16[80,1664]{1,0:T(8,128)(2,1)S(1)} %get-tuple-element.605), channel_id=1, source_target_pairs={{0,1},{1,3},{3,5},{5,7},{7,6},{6,4},{4,2},{2,0},{8,9},{9,11},{11,1... | collective-permute-start | bytes 798728 | tf_op jit(solution)/shard_map/ppermute | solution.py:178
  373.0 11.2 %collective-permute-start.53 = (bf16[80,1536]{1,0:T(8,128)(2,1)S(1)}, bf16[80,1536]{1,0:T(8,128)(2,1)S(1)}, u32[]{:S(2)}, u32[]{:S(2)}) collective-permute-start(bf16[80,1536]{1,0:T(8,128)(2,1)S(1)} %fusion.102), channel_id=1, source_target_pairs={{0,1},{1,3},{3,5},{5,7},{7,6},{6,4},{4,2},{2,0},{8,9},{9,11},{11,1... | collective-permute-start | bytes 737288 | tf_op jit(solution)/shard_map/ppermute | solution.py:178
  381.3 6.5 collective-permute-start.62
  382.1 8.5 %collective-permute-start.44 = (bf16[80,1664]{1,0:T(8,128)(2,1)S(1)}, bf16[80,1664]{1,0:T(8,128)(2,1)S(1)}, u32[]{:S(2)}, u32[]{:S(2)}) collective-permute-start(bf16[80,1664]{1,0:T(8,128)(2,1)S(1)} %get-tuple-element.601), channel_id=1, source_target_pairs={{0,2},{1,0},{3,1},{5,3},{7,5},{6,7},{4,6},{2,4},{8,10},{9,8},{11,9... | collective-permute-start | bytes 798728 | tf_op jit(solution)/shard_map/ppermute | solution.py:178
  383.2 7.5 %collective-permute-start.35 = (bf16[80,1664]{1,0:T(8,128)(2,1)S(1)}, bf16[80,1664]{1,0:T(8,128)(2,1)S(1)}, u32[]{:S(2)}, u32[]{:S(2)}) collective-permute-start(bf16[80,1664]{1,0:T(8,128)(2,1)S(1)} %get-tuple-element.602), channel_id=1, source_target_pairs={{0,1},{1,3},{3,5},{5,7},{7,6},{6,4},{4,2},{2,0},{8,9},{9,11},{11,1... | collective-permute-start | bytes 798728 | tf_op jit(solution)/shard_map/ppermute | solution.py:178
  385.2 10.5 %collective-permute-start.54 = (bf16[80,1536]{1,0:T(8,128)(2,1)S(1)}, bf16[80,1536]{1,0:T(8,128)(2,1)S(1)}, u32[]{:S(2)}, u32[]{:S(2)}) collective-permute-start(bf16[80,1536]{1,0:T(8,128)(2,1)S(1)} %fusion.121), channel_id=1, source_target_pairs={{0,16},{8,24},{16,0},{24,8},{1,17},{9,25},{17,1},{25,9},{2,18},{10... | collective-permute-start | bytes 737288 | tf_op jit(solution)/shard_map/ppermute | solution.py:181
  392.2 9.3 %collective-permute-start.63 = (bf16[80,1664]{1,0:T(8,128)(2,1)S(1)}, bf16[80,1664]{1,0:T(8,128)(2,1)S(1)}, u32[]{:S(2)}, u32[]{:S(2)}) collective-permute-start(bf16[80,1664]{1,0:T(8,128)(2,1)S(1)} %get-tuple-element.597), channel_id=1, source_target_pairs={{0,16},{8,24},{16,0},{24,8},{1,17},{9,25},{17,1},{25,9},{2,18},{10... | collective-permute-start | bytes 798728 | tf_op jit(solution)/shard_map/ppermute | solution.py:181
  393.8 11.6 %collective-permute-start.45 = (bf16[80,1664]{1,0:T(8,128)(2,1)S(1)}, bf16[80,1664]{1,0:T(8,128)(2,1)S(1)}, u32[]{:S(2)}, u32[]{:S(2)}) collective-permute-start(bf16[80,1664]{1,0:T(8,128)(2,1)S(1)} %get-tuple-element.598), channel_id=1, source_target_pairs={{0,16},{8,24},{16,0},{24,8},{1,17},{9,25},{17,1},{25,9},{2,18},{10... | collective-permute-start | bytes 798728 | tf_op jit(solution)/shard_map/ppermute | solution.py:181
  394.3 13.9 %collective-permute-start.36 = (bf16[80,1664]{1,0:T(8,128)(2,1)S(1)}, bf16[80,1664]{1,0:T(8,128)(2,1)S(1)}, u32[]{:S(2)}, u32[]{:S(2)}) collective-permute-start(bf16[80,1664]{1,0:T(8,128)(2,1)S(1)} %get-tuple-element.599), channel_id=1, source_target_pairs={{0,16},{8,24},{16,0},{24,8},{1,17},{9,25},{17,1},{25,9},{2,18},{10... | collective-permute-start | bytes 798728 | tf_op jit(solution)/shard_map/ppermute | solution.py:181
  396.9 16.6 %collective-permute-start.55 = (f32[80,1536]{1,0:T(8,128)S(1)}, f32[80,1536]{1,0:T(8,128)S(1)}, u32[]{:S(2)}, u32[]{:S(2)}) collective-permute-start(f32[80,1536]{1,0:T(8,128)S(1)} %convert_add_fusion.5), channel_id=1, source_target_pairs={{0,8},{8,0},{16,24},{24,16},{1,9},{9,1},{17,25},{25,17},{2,10},{10... | collective-permute-start | bytes 1474568 | tf_op jit(solution)/shard_map/ppermute | solution.py:184
  410.4 4.0 collective-permute-start.64
  553.5 43.5 %all-to-all-start.1 = ((bf16[8,80,5,160]{3,1,2,0:T(8,128)(2,1)}), bf16[8,80,5,160]{3,1,2,0:T(8,128)(2,1)}, u32[]{:S(2)}, u32[]{:S(2)}) async-start(bf16[8,80,5,160]{3,1,2,0:T(8,128)(2,1)} %copy.225), calls=%async_computation.1 | async-start | bytes 3276800 | tf_op jit(solution)/shard_map/all_to_all | solution.py:467
  597.1 27.0 %collective-permute-start.66 = (bf16[8,80,5,160]{3,1,2,0:T(8,128)(2,1)}, bf16[8,80,5,160]{3,1,2,0:T(8,128)(2,1)}, u32[]{:S(2)}, u32[]{:S(2)}) collective-permute-start(bf16[8,80,5,160]{3,1,2,0:T(8,128)(2,1)} %all-to-all-done.1), channel_id=1, source_target_pairs={{0,8},{8,0},{16,24},{24,16},{1,9},{9,1},{17,25},{25,17},{2,10},{10... | collective-permute-start | bytes 3072008 | tf_op jit(solution)/shard_map/ppermute | solution.py:474
  612.4 4.5 collective-permute-start.71
  (67 other events, 1531.6 us)

commit v4 on v3

--- a/solution.py
+++ b/solution.py
@@ -444,9 +444,10 @@
         outgoing = jnp.where(in_use[None, :, None], outgoing, 0.0).reshape(
             row_count, devices, owned_slots, quarter
         )
+        outgoing = jnp.transpose(outgoing, (2, 0, 1, 3)).astype(jnp.bfloat16)
         incoming = lax.all_to_all(
-            outgoing.astype(jnp.bfloat16), "fsdp", split_axis=1, concat_axis=0, tiled=True
-        ).reshape(row_count * devices, owned_slots, quarter)
+            outgoing, "fsdp", split_axis=2, concat_axis=1, tiled=True
+        ).reshape(owned_slots, row_count * devices, quarter)
         incoming_other = lax.ppermute(incoming, "dp", core_pairs)
         incoming = lax.cond(
             core == 0,
@@ -454,21 +455,21 @@
             lambda: jnp.concatenate([incoming_other, incoming], axis=2),
         ).astype(jnp.float32)
         my_use = lax.dynamic_slice_in_dim(in_use, lax.axis_index("fsdp") * owned_slots, owned_slots)
-        eigen_turned = jnp.einsum("kdi,dkc->kic", left_bases, incoming, precision=OPT_PRECISION)
+        eigen_turned = jnp.einsum("kdi,kdc->kic", left_bases, incoming, precision=OPT_PRECISION)
         eigen_turned = jnp.einsum("kic,kcj->kij", eigen_turned, right_bases, precision=OPT_PRECISION)
         first_new = BETA_FIRST * first_moment + (1.0 - BETA_FIRST) * eigen_turned
         second_new = BETA_SECOND * second_moment + (1.0 - BETA_SECOND) * eigen_turned * eigen_turned
         direction = adam_direction(first_new, second_new)
         rotated_gradient = jnp.einsum("kij,klj->kil", direction, right_bases, precision=OPT_PRECISION)
         rotated_gradient = jnp.einsum(
-            "kdi,kil->dkl", left_bases, rotated_gradient, precision=OPT_PRECISION
+            "kdi,kil->kdl", left_bases, rotated_gradient, precision=OPT_PRECISION
         )
         going = lax.dynamic_slice_in_dim(rotated_gradient, core * quarter, quarter, axis=2)
         returned = lax.all_to_all(
-            going.reshape(devices, row_count, owned_slots, quarter).astype(jnp.bfloat16),
+            going.reshape(owned_slots, devices, row_count, quarter).astype(jnp.bfloat16),
             "fsdp",
-            split_axis=0,
-            concat_axis=0,
+            split_axis=1,
+            concat_axis=1,
             tiled=True,
         )
         returned_other = lax.ppermute(returned, "dp", core_pairs)
@@ -476,10 +477,9 @@
             core == 0,
             lambda: jnp.concatenate([returned, returned_other], axis=3),
             lambda: jnp.concatenate([returned_other, returned], axis=3),
-        )
-        owner_of = block_slots // owned_slots
-        slot_in = block_slots % owned_slots
-        update = returned_full[owner_of, :, slot_in, :].astype(jnp.float32)
+        ).reshape(owned_slots * devices, row_count, block_width)
+        slot_row = (block_slots % owned_slots) * devices + block_slots // owned_slots
+        update = jnp.take(returned_full, slot_row, axis=0).astype(jnp.float32)
         update = jnp.transpose(update, (1, 0, 2)).reshape(row_count, block_count * block_width)
         new_master = master - RATE_MATRIX * update
         new_copy = new_master.astype(jnp.bfloat16)

time: 665 us -> 652 us (0.980)
  local copies, waits for them, and re-layouts: 169 us -> 157 us
    cond x37 -> x35, local copies, waits for them, and re-layouts: 35.9 us -> 28.6 us
    another operation x18 -> x16, local copies, waits for them, and re-layouts: 15.3 us -> 8.48 us
where the time goes in v4:
time: 652 us; the launch traced here: 642 us
  waiting for transfers between devices  181 us (28%)
  local copies, waits for them, and re-layouts  157 us (24%)
  matrix products  113 us (17%)
  other arithmetic  83.1 us (13%)
  starting transfers between devices  61.2 us (9%)
  blocking collectives  42.5 us (7%)
    ppermute x14, waiting for transfers between devices, all_gather(): piece = lax.ppermute(piece, 'fsdp', pairs)  61.8 us
    ppermute x28, waiting for transfers between devices, reduce_scatter(): got = lax.ppermute(acc.astype(jnp.bfloat16), 'fsdp', pairs)  45.8 us
    all_to_all x1, blocking collectives, local(): lax.all_to_all(outgoing, 'fsdp', split_axis=2, concat_axis=1, tiled=True)  42.5 us
    all_to_all x1, waiting for transfers between devices, local(): lax.all_to_all(going.reshape(owned_slots, devices, row_count, quarter).as...  31.3 us
    ppermute x28, starting transfers between devices, reduce_scatter(): got = lax.ppermute(acc.astype(jnp.bfloat16), 'fsdp', pairs)  29.1 us
    cond x35, local copies, waits for them, and re-layouts  28.6 us
    concatenate x1, local copies, waits for them, and re-layouts, build(): jnp.concatenate([small_rel, jnp.zeros((model_width, lead - small_cols), j...  19.1 us
    dot_general x1, matrix products, local(): jnp.dot(normed_two_rel, weights[:, 4 * model_width:4 * model_width + hidd...  16.9 us
  transfers between devices with their start and end apart: 73, of which 40 were waited for; matrix products, arithmetic and copies ran while one was open for 8% of the time, Pallas kernels for 0%

profile of v4, /device:TPU:0, one launch (start us, length us, event | category | flops | bytes accessed | tf_op | source)
XLA Modules:
  0.0 641.7 jit_solution(4758134768177860745)
XLA Ops:
  1.6 3.7 convert_element_type.358
  5.4 4.5 concatenate.90
  11.9 3.0 collective-permute-start
  17.0 10.1 %collective-permute-done = bf16[80,3328]{1,0:T(8,128)(2,1)} collective-permute-done((bf16[80,3328]{1,0:T(8,128)(2,1)S(1)}, bf16[80,3328]{1,0:T(8,128)(2,1)}, u32[]{:S(2)}, u32[]{:S(2)}) %collective-permute-start) | collective-permute-done | bytes 532512 | tf_op jit(solution)/shard_map/ppermute | solution.py:158
  31.2 9.5 %collective-permute-done.2 = bf16[80,3328]{1,0:T(8,128)(2,1)} collective-permute-done((bf16[80,3328]{1,0:T(8,128)(2,1)}, bf16[80,3328]{1,0:T(8,128)(2,1)}, u32[]{:S(2)}, u32[]{:S(2)}) %collective-permute-start.2) | collective-permute-done | bytes 532512 | tf_op jit(solution)/shard_map/ppermute | solution.py:158
  45.2 9.8 %collective-permute-done.16 = bf16[80,3200]{1,0:T(8,128)(2,1)} collective-permute-done((bf16[80,3200]{1,0:T(8,128)(2,1)}, bf16[80,3200]{1,0:T(8,128)(2,1)}, u32[]{:S(2)}, u32[]{:S(2)}) %collective-permute-start.16) | collective-permute-done | bytes 512032 | tf_op jit(solution)/shard_map/ppermute | solution.py:158
  58.4 8.5 %collective-permute-done.17 = bf16[80,3200]{1,0:T(8,128)(2,1)} collective-permute-done((bf16[80,3200]{1,0:T(8,128)(2,1)}, bf16[80,3200]{1,0:T(8,128)(2,1)}, u32[]{:S(2)}, u32[]{:S(2)}) %collective-permute-start.17) | collective-permute-done | bytes 512032 | tf_op jit(solution)/shard_map/ppermute | solution.py:158
  70.5 8.2 %collective-permute-done.18 = bf16[80,3200]{1,0:T(8,128)(2,1)} collective-permute-done((bf16[80,3200]{1,0:T(8,128)(2,1)}, bf16[80,3200]{1,0:T(8,128)(2,1)}, u32[]{:S(2)}, u32[]{:S(2)}) %collective-permute-start.18) | collective-permute-done | bytes 512032 | tf_op jit(solution)/shard_map/ppermute | solution.py:158
  81.6 4.1 scatter_custom_fusion
  92.5 8.3 %collective-permute-done.20 = bf16[80,3200]{1,0:T(8,128)(2,1)} collective-permute-done((bf16[80,3200]{1,0:T(8,128)(2,1)}, bf16[80,3200]{1,0:T(8,128)(2,1)}, u32[]{:S(2)}, u32[]{:S(2)}) %collective-permute-start.20) | collective-permute-done | bytes 512032 | tf_op jit(solution)/shard_map/ppermute | solution.py:158
  104.0 36.8 %conditional.11 = (bf16[640,13056]{1,0:T(8,128)(2,1)}) conditional(s32[]{:T(128)} %convert_element_type.356, (bf16[80,3328]{1,0:T(8,128)(2,1)}, bf16[80,3328]{1,0:T(8,128)(2,1)}, bf16[80,3328]{1,0:T(8,128)(2,1)}, bf16[80,3328]{1,0:T(8,128)(2,1)}, bf16[80,3328]{1,0:T(8,128)(2,1)}, /*index=5*/bf16[80,3328]{1,0:T(8,128)(2,1)}, ...), branch_computations={%region_2.3_spmd, %region_3.4_spmd} | conditional | flops 66846720 | bytes 73072728 | solution.py:260
  134.0 6.7 %pad_maximum_fusion.1 = bf16[640,13056]{1,0:T(8,128)(2,1)} fusion(bf16[640,3200]{1,0:T(8,128)(2,1)S(1)} %get-tuple-element.594, bf16[640,3328]{1,0:T(8,128)(2,1)S(1)} %get-tuple-element.592, bf16[640,3200]{1,0:T(8,128)(2,1)S(1)} %get-tuple-element.593, bf16[640,3328]{1,0:T(8,128)(2,1)S(1)} %get-tuple-element.591), kind=kLoop, calls=%fused_computation.39 | loop fusion | flops 66846720 | bytes 33423360 | tf_op jit(solution)/shard_map/cond/branch_1_fun/concatenate | solution.py:256
  160.2 16.9 %multiply_convert_fusion.1 = (bf16[256,5120]{1,0:T(8,128)(2,1)}, f32[256,5120]{1,0:T(8,128)}, f32[256,5120]{1,0:T(8,128)}) fusion(f32[5120]{0:T(1024)S(1)} %add.408, bf16[256,640]{1,0:T(8,128)(2,1)S(1)} %fusion.54, bf16[640,13056]{1,0:T(8,128)(2,1)} %get-tuple-element.662), kind=kOutput, calls=%fused_computation.98 | convolution fusion | flops 1764229120 | bytes 20008960 | tf_op jit(solution)/shard_map/dot_general | solution.py:297
  177.1 7.3 %convert_reduce_fusion = (f32[5120]{0:T(1024)S(1)}, bf16[256,5120]{1,0:T(8,128)(2,1)S(1)}) fusion(f32[256,5120]{1,0:T(8,128)} %get-tuple-element.586, f32[256,5120]{1,0:T(8,128)} %get-tuple-element.642, bf16[640,256]{1,0:T(8,128)(2,1)S(1)} %copy-done.33, bf16[640,13056]{1,0:T(8,128)(2,1)S(1)} %bitcast.109), kind=kOutput, calls=%fused_computation.93 | convolution fusion | flops 1698688000 | bytes 20008960 | tf_op jit(solution)/shard_map/dot_general | solution.py:342
  193.2 4.5 fusion.56
  197.6 4.0 multiply_reduce_fusion
  212.9 3.1 fusion.32
  231.2 45.2 %conditional.12 = (f32[640,6528]{1,0:T(8,128)}, bf16[640,6528]{1,0:T(8,128)(2,1)}) conditional(s32[]{:T(128)} %convert_element_type.356, (bf16[256,640]{1,0:T(8,128)(2,1)}, bf16[256,5120]{1,0:T(8,128)(2,1)}, bf16[256,640]{0,1:T(8,128)(2,1)S(1)}, bf16[256,5120]{1,0:T(8,128)(2,1)}, bf16[256,640]{1,0:T(8,128)(2,1)}, ...), branch_computations={%region_22.24_spmd, %region_23.25_spmd} | conditional | flops 4219371520 | bytes 174311600
  231.2 4.5 fusion.157
  239.3 4.9 slice.302
  247.0 19.1 %concatenate.74 = f32[640,6528]{1,0:T(8,128)} concatenate(f32[640,16]{1,0:T(8,128)S(1)} %copy-done.22, f32[640,112]{1,0:T(8,128)S(1)} %broadcast.336, f32[640,1920]{1,0:T(8,128)} %fusion.157, f32[640,640]{1,0:T(8,128)} %fusion.158, f32[640,3840]{1,0:T(8,128)} %slice.302), dimensions={1} | concatenate | bytes 33423360 | tf_op jit(solution)/shard_map/cond/branch_1_fun/concatenate | solution.py:395
  266.1 3.6 fusion.160
  271.8 4.1 maximum_maximum_fusion.1
  276.6 13.3 %collective-permute-done.28 = bf16[640,6528]{1,0:T(8,128)(2,1)} collective-permute-done((bf16[640,6528]{1,0:T(8,128)(2,1)}, bf16[640,6528]{1,0:T(8,128)(2,1)}, u32[]{:S(2)}, u32[]{:S(2)}) %collective-permute-start.28) | collective-permute-done | bytes 8355872 | tf_op jit(solution)/shard_map/ppermute | solution.py:419
  289.9 8.9 %fusion.144 = (bf16[640,6528]{1,0:T(8,128)(2,1)S(1)}, f32[640,6528]{1,0:T(8,128)S(1)}) fusion(f32[640,6528]{1,0:T(8,128)} %get-tuple-element.397, bf16[640,6528]{1,0:T(8,128)(2,1)} %collective-permute-done.28), kind=kLoop, calls=%fused_computation.366 | loop fusion | flops 12533760 | bytes 50135040 | tf_op jit(solution)/shard_map/convert.3
  303.0 4.7 collective-permute-done.47
  309.5 4.6 collective-permute-done.38
  320.9 4.1 collective-permute-done.57
  325.0 3.7 collective-permute-done.39
  335.5 4.1 collective-permute-done.58
  339.6 2.9 collective-permute-done.40
  349.3 3.2 collective-permute-done.59
  364.6 3.1 collective-permute-done.42
  376.0 3.9 collective-permute-done.43
  397.1 4.5 collective-permute-done.63
  401.7 3.8 collective-permute-done.45
  415.4 5.2 conditional.13
  415.4 3.9 pad_maximum_fusion.7
  420.6 5.0 reshape.456
  425.6 3.4 copy.215
  429.1 4.4 gather_fusion.1
  433.5 3.3 fusion.25
  436.7 42.5 %all_to_all.20 = bf16[5,80,8,160]{3,1,0,2:T(8,128)(2,1)} all-to-all(bf16[5,80,8,160]{3,1,0,2:T(8,128)(2,1)S(1)} %bitcast.112), channel_id=1, replica_groups=mesh['dp'=4,'fsdp'=8] {'fsdp'}, dimensions={2} | all-to-all | bytes 2048000 | tf_op jit(solution)/shard_map/all_to_all | solution.py:448
  479.2 3.7 copy.216
  482.9 2.9 reshape.398
  488.7 10.1 %conditional.14 = (bf16[5,640,320]{2,1,0:T(8,128)(2,1)}) conditional(s32[]{:T(128)} %convert_element_type.356, (bf16[5,640,160]{1,2,0:T(8,128)(2,1)}, bf16[5,640,160]{1,2,0:T(8,128)(2,1)S(1)}) %tuple.80, (bf16[5,640,160]{1,2,0:T(8,128)(2,1)S(1)}, bf16[5,640,160]{1,2,0:T(8,128)(2,1)}) %tuple.81), branch_computations={%region_28.30_spmd, %region_29.31_spmd} | conditional | flops 4096000 | bytes 8192008 | solution.py:452
  488.8 3.4 copy.220
  494.5 4.2 pad_maximum_fusion.3
  498.7 8.3 %fusion.161 = f32[5,320,640]{2,1,0:T(8,128)S(1)} fusion(bf16[5,640,320]{2,1,0:T(8,128)(2,1)} %get-tuple-element.663, f32[5,640,640]{2,1,0:T(8,128)} %param.40), kind=kOutput, calls=%fused_computation.381 | convolution fusion | flops 3932160000 | bytes 14336000 | tf_op jit(solution)/shard_map/kdi,kdc->kic/dot_general | solution.py:458
  507.1 11.6 %broadcast_select_fusion = (f32[5,640,320]{1,2,0:T(8,128)}, f32[5,640,320]{1,2,0:T(8,128)}, f32[5,640,320]{1,2,0:T(8,128)}) fusion(pred[5]{0:T(512)(128)(4,1)S(1)} %dynamic_slice.39, f32[5,640,320]{1,2,0:T(8,128)S(1)} %copy-done.19, f32[5,640,320]{1,2,0:T(8,128)} %param.38, f32[5,320,640]{2,1,0:T(8,128)S(1)} %fusion.161, f32[5,320,320]{2,1,0:T(8,128)S(1)} %copy-done), kind=kOutput, calls=%fused_computation.141 | convolution fusion | flops 1974272000 | bytes 26624004 | tf_op jit(solution)/shard_map/kic,kcj->kij/dot_general | solution.py:459
  518.6 9.8 %fusion.17 = f32[5,640,320]{1,2,0:T(8,128)S(1)} fusion(f32[5,320,320]{2,1,0:T(8,128)S(1)} %copy-done, f32[5,640,320]{1,2,0:T(8,128)} %get-tuple-element.649, f32[5,640,320]{1,2,0:T(8,128)} %param.38, f32[5,640,320]{1,2,0:T(8,128)S(1)} %copy-done.19), kind=kOutput, calls=%fused_computation.118 | convolution fusion | flops 1976320000 | bytes 18432000 | tf_op jit(solution)/shard_map/kij,klj->kil/dot_general | solution.py:463
  528.4 8.6 %fusion.162 = bf16[5,320,640]{2,1,0:T(8,128)(2,1)S(1)} fusion(f32[5,640,320]{1,2,0:T(8,128)S(1)} %fusion.17, f32[5,640,640]{2,1,0:T(8,128)S(1)} %bitcast.107), kind=kOutput, calls=%fused_computation.382 | convolution fusion | flops 3932160000 | bytes 14336000 | tf_op jit(solution)/shard_map/kdi,kil->kdl/dot_general | solution.py:464
  539.7 3.9 copy.223
  543.6 4.6 all-to-all-start.1
  548.2 5.9 fusion.2
  555.8 31.3 %all-to-all-done.1 = bf16[5,8,80,160]{3,2,0,1:T(8,128)(2,1)} async-done(((bf16[5,8,80,160]{3,2,0,1:T(8,128)(2,1)}), bf16[5,8,80,160]{3,2,0,1:T(8,128)(2,1)}, u32[]{:S(2)}, u32[]{:S(2)}) %all-to-all-start.1) | async-done | bytes 1024032 | tf_op jit(solution)/shard_map/all_to_all | solution.py:468
  598.9 3.6 collective-permute-done.70
  603.3 3.6 collective-permute-done.71
  609.4 3.5 copy.214
  614.2 4.6 conditional.15
  618.8 4.2 gather_fusion.2
  625.5 3.7 copy.228
  629.2 5.5 mul.332
  634.7 6.5 %fusion.143 = (bf16[80,12800]{1,0:T(8,128)(2,1)}, f32[80,12800]{1,0:T(8,128)}) fusion(f32[80,12800]{1,0:T(8,128)} %param.33, f32[80,12800]{1,0:T(8,128)} %mul.332), kind=kLoop, calls=%fused_computation.365 | loop fusion | flops 2048000 | bytes 14336000 | tf_op jit(solution)/shard_map/convert_element_type | solution.py:485
  (418 shorter events, 233.2 us)
Async XLA Ops:
  11.9 15.3 %collective-permute-start = (bf16[80,3328]{1,0:T(8,128)(2,1)S(1)}, bf16[80,3328]{1,0:T(8,128)(2,1)}, u32[]{:S(2)}, u32[]{:S(2)}) collective-permute-start(bf16[80,3328]{1,0:T(8,128)(2,1)S(1)} %get-tuple-element.626), channel_id=1, source_target_pairs={{0,1},{1,3},{3,5},{5,7},{7,6},{6,4},{4,2},{2,0},{8,9},{9,11},{11,1... | collective-permute-start | bytes 1597448 | tf_op jit(solution)/shard_map/ppermute | solution.py:158
  17.0 13.1 %collective-permute-start.14 = (bf16[80,3200]{1,0:T(8,128)(2,1)S(1)}, bf16[80,3200]{1,0:T(8,128)(2,1)S(1)}, u32[]{:S(2)}, u32[]{:S(2)}) collective-permute-start(bf16[80,3200]{1,0:T(8,128)(2,1)S(1)} %get-tuple-element.624), channel_id=1, source_target_pairs={{0,2},{1,0},{3,1},{5,3},{7,5},{6,7},{4,6},{2,4},{8,10},{9,8},{11,9... | collective-permute-start | bytes 1536008 | tf_op jit(solution)/shard_map/ppermute | solution.py:158
  27.2 13.6 %collective-permute-start.2 = (bf16[80,3328]{1,0:T(8,128)(2,1)}, bf16[80,3328]{1,0:T(8,128)(2,1)}, u32[]{:S(2)}, u32[]{:S(2)}) collective-permute-start(bf16[80,3328]{1,0:T(8,128)(2,1)} %collective-permute-done), channel_id=1, source_target_pairs={{0,1},{1,3},{3,5},{5,7},{7,6},{6,4},{4,2},{2,0},{8,9},{9,11},{11,1... | collective-permute-start | bytes 1597448 | tf_op jit(solution)/shard_map/ppermute | solution.py:158
  30.9 12.4 %collective-permute-start.15 = (bf16[80,3200]{1,0:T(8,128)(2,1)S(1)}, bf16[80,3200]{1,0:T(8,128)(2,1)}, u32[]{:S(2)}, u32[]{:S(2)}) collective-permute-start(bf16[80,3200]{1,0:T(8,128)(2,1)S(1)} %collective-permute-done.14), channel_id=1, source_target_pairs={{0,2},{1,0},{3,1},{5,3},{7,5},{6,7},{4,6},{2,4},{8,10},{9,8},{11,9... | collective-permute-start | bytes 1536008 | tf_op jit(solution)/shard_map/ppermute | solution.py:158
  40.8 15.1 %collective-permute-start.4 = (bf16[80,3328]{1,0:T(8,128)(2,1)}, bf16[80,3328]{1,0:T(8,128)(2,1)}, u32[]{:S(2)}, u32[]{:S(2)}) collective-permute-start(bf16[80,3328]{1,0:T(8,128)(2,1)} %collective-permute-done.2), channel_id=1, source_target_pairs={{0,1},{1,3},{3,5},{5,7},{7,6},{6,4},{4,2},{2,0},{8,9},{9,11},{11,1... | collective-permute-start | bytes 1597448 | tf_op jit(solution)/shard_map/ppermute | solution.py:158
  43.2 11.8 %collective-permute-start.16 = (bf16[80,3200]{1,0:T(8,128)(2,1)}, bf16[80,3200]{1,0:T(8,128)(2,1)}, u32[]{:S(2)}, u32[]{:S(2)}) collective-permute-start(bf16[80,3200]{1,0:T(8,128)(2,1)} %collective-permute-done.15), channel_id=1, source_target_pairs={{0,2},{1,0},{3,1},{5,3},{7,5},{6,7},{4,6},{2,4},{8,10},{9,8},{11,9... | collective-permute-start | bytes 1536008 | tf_op jit(solution)/shard_map/ppermute | solution.py:158
  55.1 11.8 %collective-permute-start.17 = (bf16[80,3200]{1,0:T(8,128)(2,1)}, bf16[80,3200]{1,0:T(8,128)(2,1)}, u32[]{:S(2)}, u32[]{:S(2)}) collective-permute-start(bf16[80,3200]{1,0:T(8,128)(2,1)} %collective-permute-done.16), channel_id=1, source_target_pairs={{0,2},{1,0},{3,1},{5,3},{7,5},{6,7},{4,6},{2,4},{8,10},{9,8},{11,9... | collective-permute-start | bytes 1536008 | tf_op jit(solution)/shard_map/ppermute | solution.py:158
  55.9 12.3 %collective-permute-start.6 = (bf16[80,3328]{1,0:T(8,128)(2,1)}, bf16[80,3328]{1,0:T(8,128)(2,1)}, u32[]{:S(2)}, u32[]{:S(2)}) collective-permute-start(bf16[80,3328]{1,0:T(8,128)(2,1)} %collective-permute-done.4), channel_id=1, source_target_pairs={{0,1},{1,3},{3,5},{5,7},{7,6},{6,4},{4,2},{2,0},{8,9},{9,11},{11,1... | collective-permute-start | bytes 1597448 | tf_op jit(solution)/shard_map/ppermute | solution.py:158
  57.8 12.0 %collective-permute-start.27 = (bf16[80,3200]{1,0:T(8,128)(2,1)}, bf16[80,3200]{1,0:T(8,128)(2,1)}, u32[]{:S(2)}, u32[]{:S(2)}) collective-permute-start(bf16[80,3200]{1,0:T(8,128)(2,1)} %copy-done.30), channel_id=1, source_target_pairs={{0,8},{8,0},{16,24},{24,16},{1,9},{9,1},{17,25},{25,17},{2,10},{10... | collective-permute-start | bytes 1536008 | tf_op jit(solution)/shard_map/ppermute | solution.py:161
  57.9 12.1 %collective-permute-start.1 = (bf16[80,3328]{1,0:T(8,128)(2,1)}, bf16[80,3328]{1,0:T(8,128)(2,1)}, u32[]{:S(2)}, u32[]{:S(2)}) collective-permute-start(bf16[80,3328]{1,0:T(8,128)(2,1)} %collective-permute-done), channel_id=1, source_target_pairs={{0,8},{8,0},{16,24},{24,16},{1,9},{9,1},{17,25},{25,17},{2,10},{10... | collective-permute-start | bytes 1597448 | tf_op jit(solution)/shard_map/ppermute | solution.py:161
  58.4 12.1 %collective-permute-start.26 = (bf16[80,3200]{1,0:T(8,128)(2,1)}, bf16[80,3200]{1,0:T(8,128)(2,1)}, u32[]{:S(2)}, u32[]{:S(2)}) collective-permute-start(bf16[80,3200]{1,0:T(8,128)(2,1)} %collective-permute-done.15), channel_id=1, source_target_pairs={{0,8},{8,0},{16,24},{24,16},{1,9},{9,1},{17,25},{25,17},{2,10},{10... | collective-permute-start | bytes 1536008 | tf_op jit(solution)/shard_map/ppermute | solution.py:161
  66.9 11.8 %collective-permute-start.18 = (bf16[80,3200]{1,0:T(8,128)(2,1)}, bf16[80,3200]{1,0:T(8,128)(2,1)}, u32[]{:S(2)}, u32[]{:S(2)}) collective-permute-start(bf16[80,3200]{1,0:T(8,128)(2,1)} %collective-permute-done.17), channel_id=1, source_target_pairs={{0,2},{1,0},{3,1},{5,3},{7,5},{6,7},{4,6},{2,4},{8,10},{9,8},{11,9... | collective-permute-start | bytes 1536008 | tf_op jit(solution)/shard_map/ppermute | solution.py:158
  68.1 12.3 %collective-permute-start.8 = (bf16[80,3328]{1,0:T(8,128)(2,1)}, bf16[80,3328]{1,0:T(8,128)(2,1)}, u32[]{:S(2)}, u32[]{:S(2)}) collective-permute-start(bf16[80,3328]{1,0:T(8,128)(2,1)} %collective-permute-done.6), channel_id=1, source_target_pairs={{0,1},{1,3},{3,5},{5,7},{7,6},{6,4},{4,2},{2,0},{8,9},{9,11},{11,1... | collective-permute-start | bytes 1597448 | tf_op jit(solution)/shard_map/ppermute | solution.py:158
  69.9 15.9 %collective-permute-start.3 = (bf16[80,3328]{1,0:T(8,128)(2,1)}, bf16[80,3328]{1,0:T(8,128)(2,1)}, u32[]{:S(2)}, u32[]{:S(2)}) collective-permute-start(bf16[80,3328]{1,0:T(8,128)(2,1)} %collective-permute-done.2), channel_id=1, source_target_pairs={{0,8},{8,0},{16,24},{24,16},{1,9},{9,1},{17,25},{25,17},{2,10},{10... | collective-permute-start | bytes 1597448 | tf_op jit(solution)/shard_map/ppermute | solution.py:161
  69.9 15.9 %collective-permute-start.25 = (bf16[80,3200]{1,0:T(8,128)(2,1)}, bf16[80,3200]{1,0:T(8,128)(2,1)}, u32[]{:S(2)}, u32[]{:S(2)}) collective-permute-start(bf16[80,3200]{1,0:T(8,128)(2,1)} %collective-permute-done.16), channel_id=1, source_target_pairs={{0,8},{8,0},{16,24},{24,16},{1,9},{9,1},{17,25},{25,17},{2,10},{10... | collective-permute-start | bytes 1536008 | tf_op jit(solution)/shard_map/ppermute | solution.py:161
  70.4 15.9 %collective-permute-start.5 = (bf16[80,3328]{1,0:T(8,128)(2,1)}, bf16[80,3328]{1,0:T(8,128)(2,1)}, u32[]{:S(2)}, u32[]{:S(2)}) collective-permute-start(bf16[80,3328]{1,0:T(8,128)(2,1)} %collective-permute-done.4), channel_id=1, source_target_pairs={{0,8},{8,0},{16,24},{24,16},{1,9},{9,1},{17,25},{25,17},{2,10},{10... | collective-permute-start | bytes 1597448 | tf_op jit(solution)/shard_map/ppermute | solution.py:161
  78.7 9.4 %collective-permute-start.19 = (bf16[80,3200]{1,0:T(8,128)(2,1)}, bf16[80,3200]{1,0:T(8,128)(2,1)}, u32[]{:S(2)}, u32[]{:S(2)}) collective-permute-start(bf16[80,3200]{1,0:T(8,128)(2,1)} %collective-permute-done.18), channel_id=1, source_target_pairs={{0,2},{1,0},{3,1},{5,3},{7,5},{6,7},{4,6},{2,4},{8,10},{9,8},{11,9... | collective-permute-start | bytes 1536008 | tf_op jit(solution)/shard_map/ppermute | solution.py:158
  80.4 9.6 %collective-permute-start.10 = (bf16[80,3328]{1,0:T(8,128)(2,1)}, bf16[80,3328]{1,0:T(8,128)(2,1)}, u32[]{:S(2)}, u32[]{:S(2)}) collective-permute-start(bf16[80,3328]{1,0:T(8,128)(2,1)} %collective-permute-done.8), channel_id=1, source_target_pairs={{0,1},{1,3},{3,5},{5,7},{7,6},{6,4},{4,2},{2,0},{8,9},{9,11},{11,1... | collective-permute-start | bytes 1597448 | tf_op jit(solution)/shard_map/ppermute | solution.py:158
  85.8 6.0 collective-permute-start.24
  85.8 6.0 collective-permute-start.7
  86.3 6.0 collective-permute-start.23
  88.1 12.6 %collective-permute-start.20 = (bf16[80,3200]{1,0:T(8,128)(2,1)}, bf16[80,3200]{1,0:T(8,128)(2,1)}, u32[]{:S(2)}, u32[]{:S(2)}) collective-permute-start(bf16[80,3200]{1,0:T(8,128)(2,1)} %collective-permute-done.19), channel_id=1, source_target_pairs={{0,2},{1,0},{3,1},{5,3},{7,5},{6,7},{4,6},{2,4},{8,10},{9,8},{11,9... | collective-permute-start | bytes 1536008 | tf_op jit(solution)/shard_map/ppermute | solution.py:158
  90.0 11.7 %collective-permute-start.12 = (bf16[80,3328]{1,0:T(8,128)(2,1)}, bf16[80,3328]{1,0:T(8,128)(2,1)}, u32[]{:S(2)}, u32[]{:S(2)}) collective-permute-start(bf16[80,3328]{1,0:T(8,128)(2,1)} %collective-permute-done.10), channel_id=1, source_target_pairs={{0,1},{1,3},{3,5},{5,7},{7,6},{6,4},{4,2},{2,0},{8,9},{9,11},{11,1... | collective-permute-start | bytes 1597448 | tf_op jit(solution)/shard_map/ppermute | solution.py:158
  91.8 12.2 %collective-permute-start.9 = (bf16[80,3328]{1,0:T(8,128)(2,1)}, bf16[80,3328]{1,0:T(8,128)(2,1)}, u32[]{:S(2)}, u32[]{:S(2)}) collective-permute-start(bf16[80,3328]{1,0:T(8,128)(2,1)} %collective-permute-done.8), channel_id=1, source_target_pairs={{0,8},{8,0},{16,24},{24,16},{1,9},{9,1},{17,25},{25,17},{2,10},{10... | collective-permute-start | bytes 1597448 | tf_op jit(solution)/shard_map/ppermute | solution.py:161
  91.9 12.1 %collective-permute-start.22 = (bf16[80,3200]{1,0:T(8,128)(2,1)}, bf16[80,3200]{1,0:T(8,128)(2,1)}, u32[]{:S(2)}, u32[]{:S(2)}) collective-permute-start(bf16[80,3200]{1,0:T(8,128)(2,1)} %collective-permute-done.19), channel_id=1, source_target_pairs={{0,8},{8,0},{16,24},{24,16},{1,9},{9,1},{17,25},{25,17},{2,10},{10... | collective-permute-start | bytes 1536008 | tf_op jit(solution)/shard_map/ppermute | solution.py:161
  92.4 11.6 %collective-permute-start.11 = (bf16[80,3328]{1,0:T(8,128)(2,1)}, bf16[80,3328]{1,0:T(8,128)(2,1)}, u32[]{:S(2)}, u32[]{:S(2)}) collective-permute-start(bf16[80,3328]{1,0:T(8,128)(2,1)} %collective-permute-done.10), channel_id=1, source_target_pairs={{0,8},{8,0},{16,24},{24,16},{1,9},{9,1},{17,25},{25,17},{2,10},{10... | collective-permute-start | bytes 1597448 | tf_op jit(solution)/shard_map/ppermute | solution.py:161
  276.4 13.5 %collective-permute-start.28 = (bf16[640,6528]{1,0:T(8,128)(2,1)}, bf16[640,6528]{1,0:T(8,128)(2,1)}, u32[]{:S(2)}, u32[]{:S(2)}) collective-permute-start(bf16[640,6528]{1,0:T(8,128)(2,1)} %get-tuple-element.398), channel_id=1, source_target_pairs={{0,8},{8,0},{16,24},{24,16},{1,9},{9,1},{17,25},{25,17},{2,10},{10... | collective-permute-start | bytes 25067528 | tf_op jit(solution)/shard_map/ppermute | solution.py:419
  298.8 8.9 %collective-permute-start.47 = (bf16[80,1536]{1,0:T(8,128)(2,1)S(1)}, bf16[80,1536]{1,0:T(8,128)(2,1)S(1)}, u32[]{:S(2)}, u32[]{:S(2)}) collective-permute-start(bf16[80,1536]{1,0:T(8,128)(2,1)S(1)} %slice.339), channel_id=1, source_target_pairs={{0,1},{1,3},{3,5},{5,7},{7,6},{6,4},{4,2},{2,0},{8,9},{9,11},{11,1... | collective-permute-start | bytes 737288 | tf_op jit(solution)/shard_map/ppermute | solution.py:178
  300.2 9.3 %collective-permute-start.56 = (bf16[80,1664]{1,0:T(8,128)(2,1)S(1)}, bf16[80,1664]{1,0:T(8,128)(2,1)S(1)}, u32[]{:S(2)}, u32[]{:S(2)}) collective-permute-start(bf16[80,1664]{1,0:T(8,128)(2,1)S(1)} %get-tuple-element.619), channel_id=1, source_target_pairs={{0,2},{1,0},{3,1},{5,3},{7,5},{6,7},{4,6},{2,4},{8,10},{9,8},{11,9... | collective-permute-start | bytes 798728 | tf_op jit(solution)/shard_map/ppermute | solution.py:178
  301.0 13.1 %collective-permute-start.38 = (bf16[80,1664]{1,0:T(8,128)(2,1)S(1)}, bf16[80,1664]{1,0:T(8,128)(2,1)S(1)}, u32[]{:S(2)}, u32[]{:S(2)}) collective-permute-start(bf16[80,1664]{1,0:T(8,128)(2,1)S(1)} %get-tuple-element.620), channel_id=1, source_target_pairs={{0,2},{1,0},{3,1},{5,3},{7,5},{6,7},{4,6},{2,4},{8,10},{9,8},{11,9... | collective-permute-start | bytes 798728 | tf_op jit(solution)/shard_map/ppermute | solution.py:178
  302.2 11.9 %collective-permute-start.29 = (bf16[80,1664]{1,0:T(8,128)(2,1)S(1)}, bf16[80,1664]{1,0:T(8,128)(2,1)S(1)}, u32[]{:S(2)}, u32[]{:S(2)}) collective-permute-start(bf16[80,1664]{1,0:T(8,128)(2,1)S(1)} %get-tuple-element.621), channel_id=1, source_target_pairs={{0,1},{1,3},{3,5},{5,7},{7,6},{6,4},{4,2},{2,0},{8,9},{9,11},{11,1... | collective-permute-start | bytes 798728 | tf_op jit(solution)/shard_map/ppermute | solution.py:178
  307.7 10.8 %collective-permute-start.48 = (bf16[80,1536]{1,0:T(8,128)(2,1)S(1)}, bf16[80,1536]{1,0:T(8,128)(2,1)S(1)}, u32[]{:S(2)}, u32[]{:S(2)}) collective-permute-start(bf16[80,1536]{1,0:T(8,128)(2,1)S(1)} %fusion.107), channel_id=1, source_target_pairs={{0,1},{1,3},{3,5},{5,7},{7,6},{6,4},{4,2},{2,0},{8,9},{9,11},{11,1... | collective-permute-start | bytes 737288 | tf_op jit(solution)/shard_map/ppermute | solution.py:178
  315.7 9.3 %collective-permute-start.57 = (bf16[80,1664]{1,0:T(8,128)(2,1)S(1)}, bf16[80,1664]{1,0:T(8,128)(2,1)S(1)}, u32[]{:S(2)}, u32[]{:S(2)}) collective-permute-start(bf16[80,1664]{1,0:T(8,128)(2,1)S(1)} %get-tuple-element.616), channel_id=1, source_target_pairs={{0,2},{1,0},{3,1},{5,3},{7,5},{6,7},{4,6},{2,4},{8,10},{9,8},{11,9... | collective-permute-start | bytes 798728 | tf_op jit(solution)/shard_map/ppermute | solution.py:178
  316.5 12.3 %collective-permute-start.39 = (bf16[80,1664]{1,0:T(8,128)(2,1)S(1)}, bf16[80,1664]{1,0:T(8,128)(2,1)S(1)}, u32[]{:S(2)}, u32[]{:S(2)}) collective-permute-start(bf16[80,1664]{1,0:T(8,128)(2,1)S(1)} %get-tuple-element.617), channel_id=1, source_target_pairs={{0,2},{1,0},{3,1},{5,3},{7,5},{6,7},{4,6},{2,4},{8,10},{9,8},{11,9... | collective-permute-start | bytes 798728 | tf_op jit(solution)/shard_map/ppermute | solution.py:178
  317.8 10.9 %collective-permute-start.30 = (bf16[80,1664]{1,0:T(8,128)(2,1)S(1)}, bf16[80,1664]{1,0:T(8,128)(2,1)S(1)}, u32[]{:S(2)}, u32[]{:S(2)}) collective-permute-start(bf16[80,1664]{1,0:T(8,128)(2,1)S(1)} %get-tuple-element.618), channel_id=1, source_target_pairs={{0,1},{1,3},{3,5},{5,7},{7,6},{6,4},{4,2},{2,0},{8,9},{9,11},{11,1... | collective-permute-start | bytes 798728 | tf_op jit(solution)/shard_map/ppermute | solution.py:178
  319.6 13.5 %collective-permute-start.49 = (bf16[80,1536]{1,0:T(8,128)(2,1)S(1)}, bf16[80,1536]{1,0:T(8,128)(2,1)S(1)}, u32[]{:S(2)}, u32[]{:S(2)}) collective-permute-start(bf16[80,1536]{1,0:T(8,128)(2,1)S(1)} %fusion.106), channel_id=1, source_target_pairs={{0,1},{1,3},{3,5},{5,7},{7,6},{6,4},{4,2},{2,0},{8,9},{9,11},{11,1... | collective-permute-start | bytes 737288 | tf_op jit(solution)/shard_map/ppermute | solution.py:178
  330.3 9.3 %collective-permute-start.58 = (bf16[80,1664]{1,0:T(8,128)(2,1)S(1)}, bf16[80,1664]{1,0:T(8,128)(2,1)S(1)}, u32[]{:S(2)}, u32[]{:S(2)}) collective-permute-start(bf16[80,1664]{1,0:T(8,128)(2,1)S(1)} %get-tuple-element.613), channel_id=1, source_target_pairs={{0,2},{1,0},{3,1},{5,3},{7,5},{6,7},{4,6},{2,4},{8,10},{9,8},{11,9... | collective-permute-start | bytes 798728 | tf_op jit(solution)/shard_map/ppermute | solution.py:178
  331.1 11.4 %collective-permute-start.40 = (bf16[80,1664]{1,0:T(8,128)(2,1)S(1)}, bf16[80,1664]{1,0:T(8,128)(2,1)S(1)}, u32[]{:S(2)}, u32[]{:S(2)}) collective-permute-start(bf16[80,1664]{1,0:T(8,128)(2,1)S(1)} %get-tuple-element.614), channel_id=1, source_target_pairs={{0,2},{1,0},{3,1},{5,3},{7,5},{6,7},{4,6},{2,4},{8,10},{9,8},{11,9... | collective-permute-start | bytes 798728 | tf_op jit(solution)/shard_map/ppermute | solution.py:178
  332.3 10.2 %collective-permute-start.31 = (bf16[80,1664]{1,0:T(8,128)(2,1)S(1)}, bf16[80,1664]{1,0:T(8,128)(2,1)S(1)}, u32[]{:S(2)}, u32[]{:S(2)}) collective-permute-start(bf16[80,1664]{1,0:T(8,128)(2,1)S(1)} %get-tuple-element.615), channel_id=1, source_target_pairs={{0,1},{1,3},{3,5},{5,7},{7,6},{6,4},{4,2},{2,0},{8,9},{9,11},{11,1... | collective-permute-start | bytes 798728 | tf_op jit(solution)/shard_map/ppermute | solution.py:178
  334.2 12.7 %collective-permute-start.50 = (bf16[80,1536]{1,0:T(8,128)(2,1)S(1)}, bf16[80,1536]{1,0:T(8,128)(2,1)S(1)}, u32[]{:S(2)}, u32[]{:S(2)}) collective-permute-start(bf16[80,1536]{1,0:T(8,128)(2,1)S(1)} %fusion.105), channel_id=1, source_target_pairs={{0,1},{1,3},{3,5},{5,7},{7,6},{6,4},{4,2},{2,0},{8,9},{9,11},{11,1... | collective-permute-start | bytes 737288 | tf_op jit(solution)/shard_map/ppermute | solution.py:178
  344.0 8.5 %collective-permute-start.59 = (bf16[80,1664]{1,0:T(8,128)(2,1)S(1)}, bf16[80,1664]{1,0:T(8,128)(2,1)S(1)}, u32[]{:S(2)}, u32[]{:S(2)}) collective-permute-start(bf16[80,1664]{1,0:T(8,128)(2,1)S(1)} %get-tuple-element.610), channel_id=1, source_target_pairs={{0,2},{1,0},{3,1},{5,3},{7,5},{6,7},{4,6},{2,4},{8,10},{9,8},{11,9... | collective-permute-start | bytes 798728 | tf_op jit(solution)/shard_map/ppermute | solution.py:178
  344.8 10.6 %collective-permute-start.41 = (bf16[80,1664]{1,0:T(8,128)(2,1)S(1)}, bf16[80,1664]{1,0:T(8,128)(2,1)S(1)}, u32[]{:S(2)}, u32[]{:S(2)}) collective-permute-start(bf16[80,1664]{1,0:T(8,128)(2,1)S(1)} %get-tuple-element.611), channel_id=1, source_target_pairs={{0,2},{1,0},{3,1},{5,3},{7,5},{6,7},{4,6},{2,4},{8,10},{9,8},{11,9... | collective-permute-start | bytes 798728 | tf_op jit(solution)/shard_map/ppermute | solution.py:178
  346.0 9.4 %collective-permute-start.32 = (bf16[80,1664]{1,0:T(8,128)(2,1)S(1)}, bf16[80,1664]{1,0:T(8,128)(2,1)S(1)}, u32[]{:S(2)}, u32[]{:S(2)}) collective-permute-start(bf16[80,1664]{1,0:T(8,128)(2,1)S(1)} %get-tuple-element.612), channel_id=1, source_target_pairs={{0,1},{1,3},{3,5},{5,7},{7,6},{6,4},{4,2},{2,0},{8,9},{9,11},{11,1... | collective-permute-start | bytes 798728 | tf_op jit(solution)/shard_map/ppermute | solution.py:178
  347.9 11.8 %collective-permute-start.51 = (bf16[80,1536]{1,0:T(8,128)(2,1)S(1)}, bf16[80,1536]{1,0:T(8,128)(2,1)S(1)}, u32[]{:S(2)}, u32[]{:S(2)}) collective-permute-start(bf16[80,1536]{1,0:T(8,128)(2,1)S(1)} %fusion.104), channel_id=1, source_target_pairs={{0,1},{1,3},{3,5},{5,7},{7,6},{6,4},{4,2},{2,0},{8,9},{9,11},{11,1... | collective-permute-start | bytes 737288 | tf_op jit(solution)/shard_map/ppermute | solution.py:178
  356.9 7.6 %collective-permute-start.60 = (bf16[80,1664]{1,0:T(8,128)(2,1)S(1)}, bf16[80,1664]{1,0:T(8,128)(2,1)S(1)}, u32[]{:S(2)}, u32[]{:S(2)}) collective-permute-start(bf16[80,1664]{1,0:T(8,128)(2,1)S(1)} %get-tuple-element.607), channel_id=1, source_target_pairs={{0,2},{1,0},{3,1},{5,3},{7,5},{6,7},{4,6},{2,4},{8,10},{9,8},{11,9... | collective-permute-start | bytes 798728 | tf_op jit(solution)/shard_map/ppermute | solution.py:178
  357.7 9.9 %collective-permute-start.42 = (bf16[80,1664]{1,0:T(8,128)(2,1)S(1)}, bf16[80,1664]{1,0:T(8,128)(2,1)S(1)}, u32[]{:S(2)}, u32[]{:S(2)}) collective-permute-start(bf16[80,1664]{1,0:T(8,128)(2,1)S(1)} %get-tuple-element.608), channel_id=1, source_target_pairs={{0,2},{1,0},{3,1},{5,3},{7,5},{6,7},{4,6},{2,4},{8,10},{9,8},{11,9... | collective-permute-start | bytes 798728 | tf_op jit(solution)/shard_map/ppermute | solution.py:178
  358.7 8.9 %collective-permute-start.33 = (bf16[80,1664]{1,0:T(8,128)(2,1)S(1)}, bf16[80,1664]{1,0:T(8,128)(2,1)S(1)}, u32[]{:S(2)}, u32[]{:S(2)}) collective-permute-start(bf16[80,1664]{1,0:T(8,128)(2,1)S(1)} %get-tuple-element.609), channel_id=1, source_target_pairs={{0,1},{1,3},{3,5},{5,7},{7,6},{6,4},{4,2},{2,0},{8,9},{9,11},{11,1... | collective-permute-start | bytes 798728 | tf_op jit(solution)/shard_map/ppermute | solution.py:178
  360.8 11.2 %collective-permute-start.52 = (bf16[80,1536]{1,0:T(8,128)(2,1)S(1)}, bf16[80,1536]{1,0:T(8,128)(2,1)S(1)}, u32[]{:S(2)}, u32[]{:S(2)}) collective-permute-start(bf16[80,1536]{1,0:T(8,128)(2,1)S(1)} %fusion.103), channel_id=1, source_target_pairs={{0,1},{1,3},{3,5},{5,7},{7,6},{6,4},{4,2},{2,0},{8,9},{9,11},{11,1... | collective-permute-start | bytes 737288 | tf_op jit(solution)/shard_map/ppermute | solution.py:178
  369.2 6.8 %collective-permute-start.61 = (bf16[80,1664]{1,0:T(8,128)(2,1)S(1)}, bf16[80,1664]{1,0:T(8,128)(2,1)S(1)}, u32[]{:S(2)}, u32[]{:S(2)}) collective-permute-start(bf16[80,1664]{1,0:T(8,128)(2,1)S(1)} %get-tuple-element.604), channel_id=1, source_target_pairs={{0,2},{1,0},{3,1},{5,3},{7,5},{6,7},{4,6},{2,4},{8,10},{9,8},{11,9... | collective-permute-start | bytes 798728 | tf_op jit(solution)/shard_map/ppermute | solution.py:178
  370.0 9.9 %collective-permute-start.43 = (bf16[80,1664]{1,0:T(8,128)(2,1)S(1)}, bf16[80,1664]{1,0:T(8,128)(2,1)S(1)}, u32[]{:S(2)}, u32[]{:S(2)}) collective-permute-start(bf16[80,1664]{1,0:T(8,128)(2,1)S(1)} %get-tuple-element.605), channel_id=1, source_target_pairs={{0,2},{1,0},{3,1},{5,3},{7,5},{6,7},{4,6},{2,4},{8,10},{9,8},{11,9... | collective-permute-start | bytes 798728 | tf_op jit(solution)/shard_map/ppermute | solution.py:178
  371.0 8.9 %collective-permute-start.34 = (bf16[80,1664]{1,0:T(8,128)(2,1)S(1)}, bf16[80,1664]{1,0:T(8,128)(2,1)S(1)}, u32[]{:S(2)}, u32[]{:S(2)}) collective-permute-start(bf16[80,1664]{1,0:T(8,128)(2,1)S(1)} %get-tuple-element.606), channel_id=1, source_target_pairs={{0,1},{1,3},{3,5},{5,7},{7,6},{6,4},{4,2},{2,0},{8,9},{9,11},{11,1... | collective-permute-start | bytes 798728 | tf_op jit(solution)/shard_map/ppermute | solution.py:178
  373.1 11.2 %collective-permute-start.53 = (bf16[80,1536]{1,0:T(8,128)(2,1)S(1)}, bf16[80,1536]{1,0:T(8,128)(2,1)S(1)}, u32[]{:S(2)}, u32[]{:S(2)}) collective-permute-start(bf16[80,1536]{1,0:T(8,128)(2,1)S(1)} %fusion.102), channel_id=1, source_target_pairs={{0,1},{1,3},{3,5},{5,7},{7,6},{6,4},{4,2},{2,0},{8,9},{9,11},{11,1... | collective-permute-start | bytes 737288 | tf_op jit(solution)/shard_map/ppermute | solution.py:178
  381.5 6.5 %collective-permute-start.62 = (bf16[80,1664]{1,0:T(8,128)(2,1)S(1)}, bf16[80,1664]{1,0:T(8,128)(2,1)S(1)}, u32[]{:S(2)}, u32[]{:S(2)}) collective-permute-start(bf16[80,1664]{1,0:T(8,128)(2,1)S(1)} %get-tuple-element.601), channel_id=1, source_target_pairs={{0,2},{1,0},{3,1},{5,3},{7,5},{6,7},{4,6},{2,4},{8,10},{9,8},{11,9... | collective-permute-start | bytes 798728 | tf_op jit(solution)/shard_map/ppermute | solution.py:178
  382.3 8.5 %collective-permute-start.44 = (bf16[80,1664]{1,0:T(8,128)(2,1)S(1)}, bf16[80,1664]{1,0:T(8,128)(2,1)S(1)}, u32[]{:S(2)}, u32[]{:S(2)}) collective-permute-start(bf16[80,1664]{1,0:T(8,128)(2,1)S(1)} %get-tuple-element.602), channel_id=1, source_target_pairs={{0,2},{1,0},{3,1},{5,3},{7,5},{6,7},{4,6},{2,4},{8,10},{9,8},{11,9... | collective-permute-start | bytes 798728 | tf_op jit(solution)/shard_map/ppermute | solution.py:178
  383.3 7.5 %collective-permute-start.35 = (bf16[80,1664]{1,0:T(8,128)(2,1)S(1)}, bf16[80,1664]{1,0:T(8,128)(2,1)S(1)}, u32[]{:S(2)}, u32[]{:S(2)}) collective-permute-start(bf16[80,1664]{1,0:T(8,128)(2,1)S(1)} %get-tuple-element.603), channel_id=1, source_target_pairs={{0,1},{1,3},{3,5},{5,7},{7,6},{6,4},{4,2},{2,0},{8,9},{9,11},{11,1... | collective-permute-start | bytes 798728 | tf_op jit(solution)/shard_map/ppermute | solution.py:178
  385.4 10.5 %collective-permute-start.54 = (bf16[80,1536]{1,0:T(8,128)(2,1)S(1)}, bf16[80,1536]{1,0:T(8,128)(2,1)S(1)}, u32[]{:S(2)}, u32[]{:S(2)}) collective-permute-start(bf16[80,1536]{1,0:T(8,128)(2,1)S(1)} %fusion.121), channel_id=1, source_target_pairs={{0,16},{8,24},{16,0},{24,8},{1,17},{9,25},{17,1},{25,9},{2,18},{10... | collective-permute-start | bytes 737288 | tf_op jit(solution)/shard_map/ppermute | solution.py:181
  392.3 9.3 %collective-permute-start.63 = (bf16[80,1664]{1,0:T(8,128)(2,1)S(1)}, bf16[80,1664]{1,0:T(8,128)(2,1)S(1)}, u32[]{:S(2)}, u32[]{:S(2)}) collective-permute-start(bf16[80,1664]{1,0:T(8,128)(2,1)S(1)} %get-tuple-element.598), channel_id=1, source_target_pairs={{0,16},{8,24},{16,0},{24,8},{1,17},{9,25},{17,1},{25,9},{2,18},{10... | collective-permute-start | bytes 798728 | tf_op jit(solution)/shard_map/ppermute | solution.py:181
  393.9 11.6 %collective-permute-start.45 = (bf16[80,1664]{1,0:T(8,128)(2,1)S(1)}, bf16[80,1664]{1,0:T(8,128)(2,1)S(1)}, u32[]{:S(2)}, u32[]{:S(2)}) collective-permute-start(bf16[80,1664]{1,0:T(8,128)(2,1)S(1)} %get-tuple-element.599), channel_id=1, source_target_pairs={{0,16},{8,24},{16,0},{24,8},{1,17},{9,25},{17,1},{25,9},{2,18},{10... | collective-permute-start | bytes 798728 | tf_op jit(solution)/shard_map/ppermute | solution.py:181
  394.4 13.9 %collective-permute-start.36 = (bf16[80,1664]{1,0:T(8,128)(2,1)S(1)}, bf16[80,1664]{1,0:T(8,128)(2,1)S(1)}, u32[]{:S(2)}, u32[]{:S(2)}) collective-permute-start(bf16[80,1664]{1,0:T(8,128)(2,1)S(1)} %get-tuple-element.600), channel_id=1, source_target_pairs={{0,16},{8,24},{16,0},{24,8},{1,17},{9,25},{17,1},{25,9},{2,18},{10... | collective-permute-start | bytes 798728 | tf_op jit(solution)/shard_map/ppermute | solution.py:181
  397.0 16.7 %collective-permute-start.55 = (f32[80,1536]{1,0:T(8,128)S(1)}, f32[80,1536]{1,0:T(8,128)S(1)}, u32[]{:S(2)}, u32[]{:S(2)}) collective-permute-start(f32[80,1536]{1,0:T(8,128)S(1)} %convert_add_fusion.5), channel_id=1, source_target_pairs={{0,8},{8,0},{16,24},{24,16},{1,9},{9,1},{17,25},{25,17},{2,10},{10... | collective-permute-start | bytes 1474568 | tf_op jit(solution)/shard_map/ppermute | solution.py:184
  410.5 4.1 collective-permute-start.64
  543.6 43.5 %all-to-all-start.1 = ((bf16[5,8,80,160]{3,2,0,1:T(8,128)(2,1)}), bf16[5,8,80,160]{3,2,0,1:T(8,128)(2,1)}, u32[]{:S(2)}, u32[]{:S(2)}) async-start(bf16[5,8,80,160]{3,2,0,1:T(8,128)(2,1)} %copy.223), calls=%async_computation.1 | async-start | bytes 3276800 | tf_op jit(solution)/shard_map/all_to_all | solution.py:468
  587.2 27.0 %collective-permute-start.66 = (bf16[5,8,80,160]{3,2,0,1:T(8,128)(2,1)}, bf16[5,8,80,160]{3,2,0,1:T(8,128)(2,1)}, u32[]{:S(2)}, u32[]{:S(2)}) collective-permute-start(bf16[5,8,80,160]{3,2,0,1:T(8,128)(2,1)} %all-to-all-done.1), channel_id=1, source_target_pairs={{0,8},{8,0},{16,24},{24,16},{1,9},{9,1},{17,25},{25,17},{2,10},{10... | collective-permute-start | bytes 3072008 | tf_op jit(solution)/shard_map/ppermute | solution.py:475
  602.5 4.5 collective-permute-start.71
  (67 other events, 1521.9 us)

commit v5 on v4

--- a/solution.py
+++ b/solution.py
@@ -257,7 +257,7 @@
                 [jnp.concatenate(chain, axis=0) for chain in first + second], axis=1
             )
 
-        full = lax.cond(core == 0, lambda: assemble(mine, other), lambda: assemble(other, mine))
+        full = jnp.where(core == 0, assemble(mine, other), assemble(other, mine))
         weights = full[:, lead : lead + weight_cols]
         params = jnp.take(full[:, :small_cols].astype(jnp.float32), natural_of, axis=0)
 

time: 652 us -> 641 us (0.983)
  local copies, waits for them, and re-layouts: 157 us -> 148 us
    cond x35 -> x1, local copies, waits for them, and re-layouts: 28.6 us -> 1.3 us
    unnamed x102 -> x138, local copies, waits for them, and re-layouts: 8.35 us -> 31.5 us
    select_n x0 -> x1, other arithmetic: none -> 13.3 us  [local(): full = jnp.where(core == 0, assemble(mine, other), assemble(other, mine))]
    concatenate x1 -> x0, other arithmetic: 6.69 us -> none  [assemble(): jnp.concatenate([jnp.concatenate(chain, axis=0) for chain in first + seco...]
  transfers between devices with their start and end apart: 73 -> 73, of which waited for: 40 -> 45; matrix products, arithmetic and copies ran while one was open for 8% -> 10% of each run, Pallas kernels for 0% -> 0%
where the time goes in v5:
time: 641 us; the launch traced here: 634 us
  waiting for transfers between devices  177 us (28%)
  local copies, waits for them, and re-layouts  148 us (23%)
  matrix products  112 us (17%)
  other arithmetic  88.8 us (14%)
  starting transfers between devices  61 us (10%)
  blocking collectives  42.8 us (7%)
    ppermute x14, waiting for transfers between devices, all_gather(): piece = lax.ppermute(piece, 'fsdp', pairs)  56.5 us
    ppermute x28, waiting for transfers between devices, reduce_scatter(): got = lax.ppermute(acc.astype(jnp.bfloat16), 'fsdp', pairs)  45.5 us
    all_to_all x1, blocking collectives, local(): lax.all_to_all(outgoing, 'fsdp', split_axis=2, concat_axis=1, tiled=True)  42.8 us
    unnamed x138, local copies, waits for them, and re-layouts  31.5 us
    all_to_all x1, waiting for transfers between devices, local(): lax.all_to_all(going.reshape(owned_slots, devices, row_count, quarter).as...  31.3 us
    ppermute x28, starting transfers between devices, reduce_scatter(): got = lax.ppermute(acc.astype(jnp.bfloat16), 'fsdp', pairs)  28.9 us
    concatenate x1, local copies, waits for them, and re-layouts, build(): jnp.concatenate([small_rel, jnp.zeros((model_width, lead - small_cols), j...  19.1 us
    dot_general x1, matrix products, local(): jnp.dot(normed_two_rel, weights[:, 4 * model_width:4 * model_width + hidd...  17.3 us
  transfers between devices with their start and end apart: 73, of which 45 were waited for; matrix products, arithmetic and copies ran while one was open for 10% of the time, Pallas kernels for 0%

profile of v5, /device:TPU:0, one launch (start us, length us, event | category | flops | bytes accessed | tf_op | source)
XLA Modules:
  0.0 634.2 jit_solution(9792792552462256871)
XLA Ops:
  1.6 3.7 convert_element_type.356
  5.4 4.5 concatenate.82
  20.0 4.1 scatter_custom_fusion
  34.4 6.0 collective-permute-done.8
  46.8 5.7 collective-permute-done.9
  59.1 5.3 collective-permute-done.10
  65.8 3.3 collective-permute-done.3
  71.4 3.5 collective-permute-done.11
  75.8 5.6 collective-permute-done.4
  85.6 5.0 collective-permute-done.5
  94.0 5.7 collective-permute-done.13
  103.9 5.3 collective-permute-done.6
  115.3 13.3 %maximum_select_fusion = bf16[640,13056]{1,0:T(8,128)(2,1)S(1)} fusion(bf16[640,3200]{1,0:T(8,128)(2,1)} %copy-done.17, bf16[640,3328]{1,0:T(8,128)(2,1)S(1)} %constant_dynamic-update-slice_fusion.16, bf16[640,3200]{1,0:T(8,128)(2,1)} %copy-done.19, bf16[640,3328]{1,0:T(8,128)(2,1)} %constant_dynamic-update-slice_fusion, pred[]{:T(512)S(6)} %eq.25), kind=kLoop, calls=%fused_computation.14 | loop fusion | flops 142049280 | bytes 33423360 | tf_op jit(solution)/shard_map/jit(_where)/select_n | solution.py:260
  128.6 5.8 copy-done.5
  152.7 17.3 %multiply_convert_fusion.1 = (bf16[256,5120]{1,0:T(8,128)(2,1)}, f32[256,5120]{1,0:T(8,128)}, f32[256,5120]{1,0:T(8,128)}) fusion(f32[5120]{0:T(1024)S(1)} %add.408, bf16[256,640]{1,0:T(8,128)(2,1)S(1)} %fusion.54, bf16[640,13056]{1,0:T(8,128)(2,1)} %copy-done.5), kind=kOutput, calls=%fused_computation.33 | convolution fusion | flops 1764229120 | bytes 20008960 | tf_op jit(solution)/shard_map/dot_general | solution.py:297
  170.1 6.8 %convert_reduce_fusion = (f32[5120]{0:T(1024)S(1)}, bf16[256,5120]{1,0:T(8,128)(2,1)S(1)}) fusion(f32[256,5120]{1,0:T(8,128)} %get-tuple-element.391, f32[256,5120]{1,0:T(8,128)} %get-tuple-element.441, bf16[640,256]{1,0:T(8,128)(2,1)S(1)} %copy-done.31, bf16[640,13056]{1,0:T(8,128)(2,1)S(1)} %bitcast.109), kind=kOutput, calls=%fused_computation.28 | convolution fusion | flops 1698688000 | bytes 20008960 | tf_op jit(solution)/shard_map/dot_general | solution.py:342
  185.7 4.5 fusion.56
  190.2 4.0 multiply_reduce_fusion
  205.5 3.1 fusion.32
  223.7 45.1 %conditional.10 = (f32[640,6528]{1,0:T(8,128)}, bf16[640,6528]{1,0:T(8,128)(2,1)}) conditional(s32[]{:T(128)} %convert_element_type.387, (bf16[256,640]{1,0:T(8,128)(2,1)}, bf16[256,5120]{1,0:T(8,128)(2,1)}, bf16[256,640]{0,1:T(8,128)(2,1)S(1)}, bf16[256,5120]{1,0:T(8,128)(2,1)}, bf16[256,640]{1,0:T(8,128)(2,1)}, ...), branch_computations={%region_20.22_spmd, %region_21.23_spmd} | conditional | flops 4219371520 | bytes 174311600
  223.7 4.5 fusion.157
  231.8 4.9 slice.302
  239.5 19.1 %concatenate.60 = f32[640,6528]{1,0:T(8,128)} concatenate(f32[640,16]{1,0:T(8,128)S(1)} %copy-done.23, f32[640,112]{1,0:T(8,128)S(1)} %broadcast.336, f32[640,1920]{1,0:T(8,128)} %fusion.157, f32[640,640]{1,0:T(8,128)} %fusion.158, f32[640,3840]{1,0:T(8,128)} %slice.302), dimensions={1} | concatenate | bytes 33423360 | tf_op jit(solution)/shard_map/cond/branch_1_fun/concatenate | solution.py:395
  258.6 3.6 fusion.160
  264.3 4.1 maximum_maximum_fusion.1
  269.0 13.3 %collective-permute-done.28 = bf16[640,6528]{1,0:T(8,128)(2,1)} collective-permute-done((bf16[640,6528]{1,0:T(8,128)(2,1)}, bf16[640,6528]{1,0:T(8,128)(2,1)}, u32[]{:S(2)}, u32[]{:S(2)}) %collective-permute-start.28) | collective-permute-done | bytes 8355872 | tf_op jit(solution)/shard_map/ppermute | solution.py:419
  282.3 8.9 %fusion.144 = (bf16[640,6528]{1,0:T(8,128)(2,1)S(1)}, f32[640,6528]{1,0:T(8,128)S(1)}) fusion(f32[640,6528]{1,0:T(8,128)} %get-tuple-element.202, bf16[640,6528]{1,0:T(8,128)(2,1)} %collective-permute-done.28), kind=kLoop, calls=%fused_computation.331 | loop fusion | flops 12533760 | bytes 50135040 | tf_op jit(solution)/shard_map/convert.3
  295.5 4.7 collective-permute-done.47
  301.9 4.6 collective-permute-done.38
  313.3 4.1 collective-permute-done.57
  317.3 3.7 collective-permute-done.39
  327.9 4.1 collective-permute-done.58
  341.6 3.2 collective-permute-done.59
  356.9 3.1 collective-permute-done.42
  368.3 3.9 collective-permute-done.43
  389.6 4.4 collective-permute-done.63
  394.0 3.8 collective-permute-done.45
  407.7 5.2 conditional.11
  407.7 3.9 pad_maximum_fusion.5
  412.8 5.0 reshape.456
  417.9 3.4 copy.215
  421.3 4.4 gather_fusion.1
  425.7 3.3 fusion.25
  429.0 42.8 %all_to_all.20 = bf16[5,80,8,160]{3,1,0,2:T(8,128)(2,1)} all-to-all(bf16[5,80,8,160]{3,1,0,2:T(8,128)(2,1)S(1)} %bitcast.112), channel_id=1, replica_groups=mesh['dp'=4,'fsdp'=8] {'fsdp'}, dimensions={2} | all-to-all | bytes 2048000 | tf_op jit(solution)/shard_map/all_to_all | solution.py:448
  471.7 3.7 copy.216
  481.2 10.1 %conditional.12 = (bf16[5,640,320]{2,1,0:T(8,128)(2,1)}) conditional(s32[]{:T(128)} %convert_element_type.387, (bf16[5,640,160]{1,2,0:T(8,128)(2,1)}, bf16[5,640,160]{1,2,0:T(8,128)(2,1)S(1)}) %tuple.72, (bf16[5,640,160]{1,2,0:T(8,128)(2,1)S(1)}, bf16[5,640,160]{1,2,0:T(8,128)(2,1)}) %tuple.73), branch_computations={%region_26.28_spmd, %region_27.29_spmd} | conditional | flops 4096000 | bytes 8192008 | solution.py:452
  481.4 3.4 copy.220
  487.0 4.2 pad_maximum_fusion.1
  491.3 8.3 %fusion.161 = f32[5,320,640]{2,1,0:T(8,128)S(1)} fusion(bf16[5,640,320]{2,1,0:T(8,128)(2,1)} %get-tuple-element.461, f32[5,640,640]{2,1,0:T(8,128)} %param.38), kind=kOutput, calls=%fused_computation.346 | convolution fusion | flops 3932160000 | bytes 14336000 | tf_op jit(solution)/shard_map/kdi,kdc->kic/dot_general | solution.py:458
  499.6 11.6 %broadcast_select_fusion = (f32[5,640,320]{1,2,0:T(8,128)}, f32[5,640,320]{1,2,0:T(8,128)}, f32[5,640,320]{1,2,0:T(8,128)}) fusion(pred[5]{0:T(512)(128)(4,1)S(1)} %dynamic_slice.39, f32[5,640,320]{1,2,0:T(8,128)S(1)} %copy-done.20, f32[5,640,320]{1,2,0:T(8,128)} %param.36, f32[5,320,640]{2,1,0:T(8,128)S(1)} %fusion.161, f32[5,320,320]{2,1,0:T(8,128)S(1)} %copy-done), kind=kOutput, calls=%fused_computation.76 | convolution fusion | flops 1974272000 | bytes 26624004 | tf_op jit(solution)/shard_map/kic,kcj->kij/dot_general | solution.py:459
  511.2 9.8 %fusion.17 = f32[5,640,320]{1,2,0:T(8,128)S(1)} fusion(f32[5,320,320]{2,1,0:T(8,128)S(1)} %copy-done, f32[5,640,320]{1,2,0:T(8,128)} %get-tuple-element.448, f32[5,640,320]{1,2,0:T(8,128)} %param.36, f32[5,640,320]{1,2,0:T(8,128)S(1)} %copy-done.20), kind=kOutput, calls=%fused_computation.53 | convolution fusion | flops 1976320000 | bytes 18432000 | tf_op jit(solution)/shard_map/kij,klj->kil/dot_general | solution.py:463
  521.0 8.6 %fusion.162 = bf16[5,320,640]{2,1,0:T(8,128)(2,1)S(1)} fusion(f32[5,640,320]{1,2,0:T(8,128)S(1)} %fusion.17, f32[5,640,640]{2,1,0:T(8,128)S(1)} %bitcast.107), kind=kOutput, calls=%fused_computation.347 | convolution fusion | flops 3932160000 | bytes 14336000 | tf_op jit(solution)/shard_map/kdi,kil->kdl/dot_general | solution.py:464
  532.3 3.9 copy.223
  536.2 4.6 all-to-all-start.1
  540.8 5.9 fusion.2
  548.4 31.3 %all-to-all-done.1 = bf16[5,8,80,160]{3,2,0,1:T(8,128)(2,1)} async-done(((bf16[5,8,80,160]{3,2,0,1:T(8,128)(2,1)}), bf16[5,8,80,160]{3,2,0,1:T(8,128)(2,1)}, u32[]{:S(2)}, u32[]{:S(2)}) %all-to-all-start.1) | async-done | bytes 1024032 | tf_op jit(solution)/shard_map/all_to_all | solution.py:468
  591.4 3.6 collective-permute-done.70
  595.8 3.6 collective-permute-done.71
  601.9 3.5 copy.214
  606.7 4.6 conditional.13
  611.3 4.2 gather_fusion.2
  618.0 3.7 copy.228
  621.7 5.5 mul.332
  627.2 6.5 %fusion.143 = (bf16[80,12800]{1,0:T(8,128)(2,1)}, f32[80,12800]{1,0:T(8,128)}) fusion(f32[80,12800]{1,0:T(8,128)} %param.31, f32[80,12800]{1,0:T(8,128)} %mul.332), kind=kLoop, calls=%fused_computation.330 | loop fusion | flops 2048000 | bytes 14336000 | tf_op jit(solution)/shard_map/convert_element_type | solution.py:485
  (419 shorter events, 231.1 us)
Async XLA Ops:
  12.3 15.0 %collective-permute-start.7 = (bf16[80,3200]{1,0:T(8,128)(2,1)}, bf16[80,3200]{1,0:T(8,128)(2,1)}, u32[]{:S(2)}, u32[]{:S(2)}) collective-permute-start(bf16[80,3200]{1,0:T(8,128)(2,1)} %get-tuple-element.395), channel_id=1, source_target_pairs={{0,2},{1,0},{3,1},{5,3},{7,5},{6,7},{4,6},{2,4},{8,10},{9,8},{11,9... | collective-permute-start | bytes 1536008 | tf_op jit(solution)/shard_map/ppermute | solution.py:158
  17.8 13.9 %collective-permute-start = (bf16[80,3328]{1,0:T(8,128)(2,1)}, bf16[80,3328]{1,0:T(8,128)(2,1)}, u32[]{:S(2)}, u32[]{:S(2)}) collective-permute-start(bf16[80,3328]{1,0:T(8,128)(2,1)} %get-tuple-element.393), channel_id=1, source_target_pairs={{0,1},{1,3},{3,5},{5,7},{7,6},{6,4},{4,2},{2,0},{8,9},{9,11},{11,1... | collective-permute-start | bytes 1597448 | tf_op jit(solution)/shard_map/ppermute | solution.py:158
  27.3 13.1 %collective-permute-start.8 = (bf16[80,3200]{1,0:T(8,128)(2,1)}, bf16[80,3200]{1,0:T(8,128)(2,1)}, u32[]{:S(2)}, u32[]{:S(2)}) collective-permute-start(bf16[80,3200]{1,0:T(8,128)(2,1)} %collective-permute-done.7), channel_id=1, source_target_pairs={{0,2},{1,0},{3,1},{5,3},{7,5},{6,7},{4,6},{2,4},{8,10},{9,8},{11,9... | collective-permute-start | bytes 1536008 | tf_op jit(solution)/shard_map/ppermute | solution.py:158
  31.7 12.9 %collective-permute-start.1 = (bf16[80,3328]{1,0:T(8,128)(2,1)}, bf16[80,3328]{1,0:T(8,128)(2,1)S(1)}, u32[]{:S(2)}, u32[]{:S(2)}) collective-permute-start(bf16[80,3328]{1,0:T(8,128)(2,1)} %collective-permute-done), channel_id=1, source_target_pairs={{0,1},{1,3},{3,5},{5,7},{7,6},{6,4},{4,2},{2,0},{8,9},{9,11},{11,1... | collective-permute-start | bytes 1597448 | tf_op jit(solution)/shard_map/ppermute | solution.py:158
  32.0 81.2 %collective-permute-start.27 = (bf16[80,3200]{1,0:T(8,128)(2,1)}, bf16[80,3200]{1,0:T(8,128)(2,1)S(1)}, u32[]{:S(2)}, u32[]{:S(2)}) collective-permute-start(bf16[80,3200]{1,0:T(8,128)(2,1)} %collective-permute-done.7), channel_id=1, source_target_pairs={{0,8},{8,0},{16,24},{24,16},{1,9},{9,1},{17,25},{25,17},{2,10},{10... | collective-permute-start | bytes 1536008 | tf_op jit(solution)/shard_map/ppermute | solution.py:161
  32.0 14.0 %collective-permute-start.14 = (bf16[80,3328]{1,0:T(8,128)(2,1)}, bf16[80,3328]{1,0:T(8,128)(2,1)S(1)}, u32[]{:S(2)}, u32[]{:S(2)}) collective-permute-start(bf16[80,3328]{1,0:T(8,128)(2,1)} %collective-permute-done), channel_id=1, source_target_pairs={{0,8},{8,0},{16,24},{24,16},{1,9},{9,1},{17,25},{25,17},{2,10},{10... | collective-permute-start | bytes 1597448 | tf_op jit(solution)/shard_map/ppermute | solution.py:161
  40.4 12.2 %collective-permute-start.9 = (bf16[80,3200]{1,0:T(8,128)(2,1)}, bf16[80,3200]{1,0:T(8,128)(2,1)S(1)}, u32[]{:S(2)}, u32[]{:S(2)}) collective-permute-start(bf16[80,3200]{1,0:T(8,128)(2,1)} %collective-permute-done.8), channel_id=1, source_target_pairs={{0,2},{1,0},{3,1},{5,3},{7,5},{6,7},{4,6},{2,4},{8,10},{9,8},{11,9... | collective-permute-start | bytes 1536008 | tf_op jit(solution)/shard_map/ppermute | solution.py:158
  41.9 71.2 %collective-permute-start.26 = (bf16[80,3200]{1,0:T(8,128)(2,1)}, bf16[80,3200]{1,0:T(8,128)(2,1)S(1)}, u32[]{:S(2)}, u32[]{:S(2)}) collective-permute-start(bf16[80,3200]{1,0:T(8,128)(2,1)} %collective-permute-done.8), channel_id=1, source_target_pairs={{0,8},{8,0},{16,24},{24,16},{1,9},{9,1},{17,25},{25,17},{2,10},{10... | collective-permute-start | bytes 1536008 | tf_op jit(solution)/shard_map/ppermute | solution.py:161
  44.6 12.3 %collective-permute-start.2 = (bf16[80,3328]{1,0:T(8,128)(2,1)S(1)}, bf16[80,3328]{1,0:T(8,128)(2,1)S(1)}, u32[]{:S(2)}, u32[]{:S(2)}) collective-permute-start(bf16[80,3328]{1,0:T(8,128)(2,1)S(1)} %collective-permute-done.1), channel_id=1, source_target_pairs={{0,1},{1,3},{3,5},{5,7},{7,6},{6,4},{4,2},{2,0},{8,9},{9,11},{11,1... | collective-permute-start | bytes 1597448 | tf_op jit(solution)/shard_map/ppermute | solution.py:158
  46.0 12.3 %collective-permute-start.15 = (bf16[80,3328]{1,0:T(8,128)(2,1)S(1)}, bf16[80,3328]{1,0:T(8,128)(2,1)S(1)}, u32[]{:S(2)}, u32[]{:S(2)}) collective-permute-start(bf16[80,3328]{1,0:T(8,128)(2,1)S(1)} %collective-permute-done.1), channel_id=1, source_target_pairs={{0,8},{8,0},{16,24},{24,16},{1,9},{9,1},{17,25},{25,17},{2,10},{10... | collective-permute-start | bytes 1597448 | tf_op jit(solution)/shard_map/ppermute | solution.py:161
  52.6 11.8 %collective-permute-start.10 = (bf16[80,3200]{1,0:T(8,128)(2,1)S(1)}, bf16[80,3200]{1,0:T(8,128)(2,1)S(1)}, u32[]{:S(2)}, u32[]{:S(2)}) collective-permute-start(bf16[80,3200]{1,0:T(8,128)(2,1)S(1)} %collective-permute-done.9), channel_id=1, source_target_pairs={{0,2},{1,0},{3,1},{5,3},{7,5},{6,7},{4,6},{2,4},{8,10},{9,8},{11,9... | collective-permute-start | bytes 1536008 | tf_op jit(solution)/shard_map/ppermute | solution.py:158
  56.9 12.3 %collective-permute-start.3 = (bf16[80,3328]{1,0:T(8,128)(2,1)S(1)}, bf16[80,3328]{1,0:T(8,128)(2,1)S(1)}, u32[]{:S(2)}, u32[]{:S(2)}) collective-permute-start(bf16[80,3328]{1,0:T(8,128)(2,1)S(1)} %collective-permute-done.2), channel_id=1, source_target_pairs={{0,1},{1,3},{3,5},{5,7},{7,6},{6,4},{4,2},{2,0},{8,9},{9,11},{11,1... | collective-permute-start | bytes 1597448 | tf_op jit(solution)/shard_map/ppermute | solution.py:158
  58.2 12.3 %collective-permute-start.16 = (bf16[80,3328]{1,0:T(8,128)(2,1)S(1)}, bf16[80,3328]{1,0:T(8,128)(2,1)S(1)}, u32[]{:S(2)}, u32[]{:S(2)}) collective-permute-start(bf16[80,3328]{1,0:T(8,128)(2,1)S(1)} %collective-permute-done.2), channel_id=1, source_target_pairs={{0,8},{8,0},{16,24},{24,16},{1,9},{9,1},{17,25},{25,17},{2,10},{10... | collective-permute-start | bytes 1597448 | tf_op jit(solution)/shard_map/ppermute | solution.py:161
  64.4 10.5 %collective-permute-start.11 = (bf16[80,3200]{1,0:T(8,128)(2,1)S(1)}, bf16[80,3200]{1,0:T(8,128)(2,1)S(1)}, u32[]{:S(2)}, u32[]{:S(2)}) collective-permute-start(bf16[80,3200]{1,0:T(8,128)(2,1)S(1)} %collective-permute-done.10), channel_id=1, source_target_pairs={{0,2},{1,0},{3,1},{5,3},{7,5},{6,7},{4,6},{2,4},{8,10},{9,8},{11,9... | collective-permute-start | bytes 1536008 | tf_op jit(solution)/shard_map/ppermute | solution.py:158
  69.1 12.3 %collective-permute-start.4 = (bf16[80,3328]{1,0:T(8,128)(2,1)S(1)}, bf16[80,3328]{1,0:T(8,128)(2,1)S(1)}, u32[]{:S(2)}, u32[]{:S(2)}) collective-permute-start(bf16[80,3328]{1,0:T(8,128)(2,1)S(1)} %collective-permute-done.3), channel_id=1, source_target_pairs={{0,1},{1,3},{3,5},{5,7},{7,6},{6,4},{4,2},{2,0},{8,9},{9,11},{11,1... | collective-permute-start | bytes 1597448 | tf_op jit(solution)/shard_map/ppermute | solution.py:158
  70.5 12.3 %collective-permute-start.17 = (bf16[80,3328]{1,0:T(8,128)(2,1)S(1)}, bf16[80,3328]{1,0:T(8,128)(2,1)S(1)}, u32[]{:S(2)}, u32[]{:S(2)}) collective-permute-start(bf16[80,3328]{1,0:T(8,128)(2,1)S(1)} %collective-permute-done.3), channel_id=1, source_target_pairs={{0,8},{8,0},{16,24},{24,16},{1,9},{9,1},{17,25},{25,17},{2,10},{10... | collective-permute-start | bytes 1597448 | tf_op jit(solution)/shard_map/ppermute | solution.py:161
  74.9 10.8 %collective-permute-start.12 = (bf16[80,3200]{1,0:T(8,128)(2,1)S(1)}, bf16[80,3200]{1,0:T(8,128)(2,1)S(1)}, u32[]{:S(2)}, u32[]{:S(2)}) collective-permute-start(bf16[80,3200]{1,0:T(8,128)(2,1)S(1)} %collective-permute-done.11), channel_id=1, source_target_pairs={{0,2},{1,0},{3,1},{5,3},{7,5},{6,7},{4,6},{2,4},{8,10},{9,8},{11,9... | collective-permute-start | bytes 1536008 | tf_op jit(solution)/shard_map/ppermute | solution.py:158
  81.4 9.3 %collective-permute-start.5 = (bf16[80,3328]{1,0:T(8,128)(2,1)S(1)}, bf16[80,3328]{1,0:T(8,128)(2,1)S(1)}, u32[]{:S(2)}, u32[]{:S(2)}) collective-permute-start(bf16[80,3328]{1,0:T(8,128)(2,1)S(1)} %collective-permute-done.4), channel_id=1, source_target_pairs={{0,1},{1,3},{3,5},{5,7},{7,6},{6,4},{4,2},{2,0},{8,9},{9,11},{11,1... | collective-permute-start | bytes 1597448 | tf_op jit(solution)/shard_map/ppermute | solution.py:158
  82.8 10.3 %collective-permute-start.18 = (bf16[80,3328]{1,0:T(8,128)(2,1)S(1)}, bf16[80,3328]{1,0:T(8,128)(2,1)S(1)}, u32[]{:S(2)}, u32[]{:S(2)}) collective-permute-start(bf16[80,3328]{1,0:T(8,128)(2,1)S(1)} %collective-permute-done.4), channel_id=1, source_target_pairs={{0,8},{8,0},{16,24},{24,16},{1,9},{9,1},{17,25},{25,17},{2,10},{10... | collective-permute-start | bytes 1597448 | tf_op jit(solution)/shard_map/ppermute | solution.py:161
  85.6 27.4 %collective-permute-start.25 = (bf16[80,3200]{1,0:T(8,128)(2,1)S(1)}, bf16[80,3200]{1,0:T(8,128)(2,1)S(1)}, u32[]{:S(2)}, u32[]{:S(2)}) collective-permute-start(bf16[80,3200]{1,0:T(8,128)(2,1)S(1)} %collective-permute-done.9), channel_id=1, source_target_pairs={{0,8},{8,0},{16,24},{24,16},{1,9},{9,1},{17,25},{25,17},{2,10},{10... | collective-permute-start | bytes 1536008 | tf_op jit(solution)/shard_map/ppermute | solution.py:161
  90.7 9.0 %collective-permute-start.13 = (bf16[80,3200]{1,0:T(8,128)(2,1)S(1)}, bf16[80,3200]{1,0:T(8,128)(2,1)S(1)}, u32[]{:S(2)}, u32[]{:S(2)}) collective-permute-start(bf16[80,3200]{1,0:T(8,128)(2,1)S(1)} %collective-permute-done.12), channel_id=1, source_target_pairs={{0,2},{1,0},{3,1},{5,3},{7,5},{6,7},{4,6},{2,4},{8,10},{9,8},{11,9... | collective-permute-start | bytes 1536008 | tf_op jit(solution)/shard_map/ppermute | solution.py:158
  93.2 10.6 %collective-permute-start.19 = (bf16[80,3328]{1,0:T(8,128)(2,1)S(1)}, bf16[80,3328]{1,0:T(8,128)(2,1)S(1)}, u32[]{:S(2)}, u32[]{:S(2)}) collective-permute-start(bf16[80,3328]{1,0:T(8,128)(2,1)S(1)} %collective-permute-done.5), channel_id=1, source_target_pairs={{0,8},{8,0},{16,24},{24,16},{1,9},{9,1},{17,25},{25,17},{2,10},{10... | collective-permute-start | bytes 1597448 | tf_op jit(solution)/shard_map/ppermute | solution.py:161
  99.7 9.5 %collective-permute-start.6 = (bf16[80,3328]{1,0:T(8,128)(2,1)S(1)}, bf16[80,3328]{1,0:T(8,128)(2,1)S(1)}, u32[]{:S(2)}, u32[]{:S(2)}) collective-permute-start(bf16[80,3328]{1,0:T(8,128)(2,1)S(1)} %collective-permute-done.5), channel_id=1, source_target_pairs={{0,1},{1,3},{3,5},{5,7},{7,6},{6,4},{4,2},{2,0},{8,9},{9,11},{11,1... | collective-permute-start | bytes 1597448 | tf_op jit(solution)/shard_map/ppermute | solution.py:158
  103.8 6.3 collective-permute-start.21
  268.8 13.5 %collective-permute-start.28 = (bf16[640,6528]{1,0:T(8,128)(2,1)}, bf16[640,6528]{1,0:T(8,128)(2,1)}, u32[]{:S(2)}, u32[]{:S(2)}) collective-permute-start(bf16[640,6528]{1,0:T(8,128)(2,1)} %get-tuple-element.203), channel_id=1, source_target_pairs={{0,8},{8,0},{16,24},{24,16},{1,9},{9,1},{17,25},{25,17},{2,10},{10... | collective-permute-start | bytes 25067528 | tf_op jit(solution)/shard_map/ppermute | solution.py:419
  291.2 8.9 %collective-permute-start.47 = (bf16[80,1536]{1,0:T(8,128)(2,1)S(1)}, bf16[80,1536]{1,0:T(8,128)(2,1)S(1)}, u32[]{:S(2)}, u32[]{:S(2)}) collective-permute-start(bf16[80,1536]{1,0:T(8,128)(2,1)S(1)} %slice.339), channel_id=1, source_target_pairs={{0,1},{1,3},{3,5},{5,7},{7,6},{6,4},{4,2},{2,0},{8,9},{9,11},{11,1... | collective-permute-start | bytes 737288 | tf_op jit(solution)/shard_map/ppermute | solution.py:178
  292.6 9.3 %collective-permute-start.56 = (bf16[80,1664]{1,0:T(8,128)(2,1)S(1)}, bf16[80,1664]{1,0:T(8,128)(2,1)S(1)}, u32[]{:S(2)}, u32[]{:S(2)}) collective-permute-start(bf16[80,1664]{1,0:T(8,128)(2,1)S(1)} %get-tuple-element.420), channel_id=1, source_target_pairs={{0,2},{1,0},{3,1},{5,3},{7,5},{6,7},{4,6},{2,4},{8,10},{9,8},{11,9... | collective-permute-start | bytes 798728 | tf_op jit(solution)/shard_map/ppermute | solution.py:178
  293.4 13.0 %collective-permute-start.38 = (bf16[80,1664]{1,0:T(8,128)(2,1)S(1)}, bf16[80,1664]{1,0:T(8,128)(2,1)S(1)}, u32[]{:S(2)}, u32[]{:S(2)}) collective-permute-start(bf16[80,1664]{1,0:T(8,128)(2,1)S(1)} %get-tuple-element.421), channel_id=1, source_target_pairs={{0,2},{1,0},{3,1},{5,3},{7,5},{6,7},{4,6},{2,4},{8,10},{9,8},{11,9... | collective-permute-start | bytes 798728 | tf_op jit(solution)/shard_map/ppermute | solution.py:178
  295.0 11.5 %collective-permute-start.29 = (bf16[80,1664]{1,0:T(8,128)(2,1)S(1)}, bf16[80,1664]{1,0:T(8,128)(2,1)S(1)}, u32[]{:S(2)}, u32[]{:S(2)}) collective-permute-start(bf16[80,1664]{1,0:T(8,128)(2,1)S(1)} %get-tuple-element.422), channel_id=1, source_target_pairs={{0,1},{1,3},{3,5},{5,7},{7,6},{6,4},{4,2},{2,0},{8,9},{9,11},{11,1... | collective-permute-start | bytes 798728 | tf_op jit(solution)/shard_map/ppermute | solution.py:178
  300.2 10.9 %collective-permute-start.48 = (bf16[80,1536]{1,0:T(8,128)(2,1)S(1)}, bf16[80,1536]{1,0:T(8,128)(2,1)S(1)}, u32[]{:S(2)}, u32[]{:S(2)}) collective-permute-start(bf16[80,1536]{1,0:T(8,128)(2,1)S(1)} %fusion.107), channel_id=1, source_target_pairs={{0,1},{1,3},{3,5},{5,7},{7,6},{6,4},{4,2},{2,0},{8,9},{9,11},{11,1... | collective-permute-start | bytes 737288 | tf_op jit(solution)/shard_map/ppermute | solution.py:178
  308.0 9.3 %collective-permute-start.57 = (bf16[80,1664]{1,0:T(8,128)(2,1)S(1)}, bf16[80,1664]{1,0:T(8,128)(2,1)S(1)}, u32[]{:S(2)}, u32[]{:S(2)}) collective-permute-start(bf16[80,1664]{1,0:T(8,128)(2,1)S(1)} %get-tuple-element.417), channel_id=1, source_target_pairs={{0,2},{1,0},{3,1},{5,3},{7,5},{6,7},{4,6},{2,4},{8,10},{9,8},{11,9... | collective-permute-start | bytes 798728 | tf_op jit(solution)/shard_map/ppermute | solution.py:178
  309.0 12.1 %collective-permute-start.39 = (bf16[80,1664]{1,0:T(8,128)(2,1)S(1)}, bf16[80,1664]{1,0:T(8,128)(2,1)S(1)}, u32[]{:S(2)}, u32[]{:S(2)}) collective-permute-start(bf16[80,1664]{1,0:T(8,128)(2,1)S(1)} %get-tuple-element.418), channel_id=1, source_target_pairs={{0,2},{1,0},{3,1},{5,3},{7,5},{6,7},{4,6},{2,4},{8,10},{9,8},{11,9... | collective-permute-start | bytes 798728 | tf_op jit(solution)/shard_map/ppermute | solution.py:178
  310.6 10.5 %collective-permute-start.30 = (bf16[80,1664]{1,0:T(8,128)(2,1)S(1)}, bf16[80,1664]{1,0:T(8,128)(2,1)S(1)}, u32[]{:S(2)}, u32[]{:S(2)}) collective-permute-start(bf16[80,1664]{1,0:T(8,128)(2,1)S(1)} %get-tuple-element.419), channel_id=1, source_target_pairs={{0,1},{1,3},{3,5},{5,7},{7,6},{6,4},{4,2},{2,0},{8,9},{9,11},{11,1... | collective-permute-start | bytes 798728 | tf_op jit(solution)/shard_map/ppermute | solution.py:178
  312.1 13.4 %collective-permute-start.49 = (bf16[80,1536]{1,0:T(8,128)(2,1)S(1)}, bf16[80,1536]{1,0:T(8,128)(2,1)S(1)}, u32[]{:S(2)}, u32[]{:S(2)}) collective-permute-start(bf16[80,1536]{1,0:T(8,128)(2,1)S(1)} %fusion.106), channel_id=1, source_target_pairs={{0,1},{1,3},{3,5},{5,7},{7,6},{6,4},{4,2},{2,0},{8,9},{9,11},{11,1... | collective-permute-start | bytes 737288 | tf_op jit(solution)/shard_map/ppermute | solution.py:178
  322.6 9.3 %collective-permute-start.58 = (bf16[80,1664]{1,0:T(8,128)(2,1)S(1)}, bf16[80,1664]{1,0:T(8,128)(2,1)S(1)}, u32[]{:S(2)}, u32[]{:S(2)}) collective-permute-start(bf16[80,1664]{1,0:T(8,128)(2,1)S(1)} %get-tuple-element.414), channel_id=1, source_target_pairs={{0,2},{1,0},{3,1},{5,3},{7,5},{6,7},{4,6},{2,4},{8,10},{9,8},{11,9... | collective-permute-start | bytes 798728 | tf_op jit(solution)/shard_map/ppermute | solution.py:178
  323.5 11.3 %collective-permute-start.40 = (bf16[80,1664]{1,0:T(8,128)(2,1)S(1)}, bf16[80,1664]{1,0:T(8,128)(2,1)S(1)}, u32[]{:S(2)}, u32[]{:S(2)}) collective-permute-start(bf16[80,1664]{1,0:T(8,128)(2,1)S(1)} %get-tuple-element.415), channel_id=1, source_target_pairs={{0,2},{1,0},{3,1},{5,3},{7,5},{6,7},{4,6},{2,4},{8,10},{9,8},{11,9... | collective-permute-start | bytes 798728 | tf_op jit(solution)/shard_map/ppermute | solution.py:178
  325.1 9.7 %collective-permute-start.31 = (bf16[80,1664]{1,0:T(8,128)(2,1)S(1)}, bf16[80,1664]{1,0:T(8,128)(2,1)S(1)}, u32[]{:S(2)}, u32[]{:S(2)}) collective-permute-start(bf16[80,1664]{1,0:T(8,128)(2,1)S(1)} %get-tuple-element.416), channel_id=1, source_target_pairs={{0,1},{1,3},{3,5},{5,7},{7,6},{6,4},{4,2},{2,0},{8,9},{9,11},{11,1... | collective-permute-start | bytes 798728 | tf_op jit(solution)/shard_map/ppermute | solution.py:178
  326.6 12.6 %collective-permute-start.50 = (bf16[80,1536]{1,0:T(8,128)(2,1)S(1)}, bf16[80,1536]{1,0:T(8,128)(2,1)S(1)}, u32[]{:S(2)}, u32[]{:S(2)}) collective-permute-start(bf16[80,1536]{1,0:T(8,128)(2,1)S(1)} %fusion.105), channel_id=1, source_target_pairs={{0,1},{1,3},{3,5},{5,7},{7,6},{6,4},{4,2},{2,0},{8,9},{9,11},{11,1... | collective-permute-start | bytes 737288 | tf_op jit(solution)/shard_map/ppermute | solution.py:178
  336.4 8.5 %collective-permute-start.59 = (bf16[80,1664]{1,0:T(8,128)(2,1)S(1)}, bf16[80,1664]{1,0:T(8,128)(2,1)S(1)}, u32[]{:S(2)}, u32[]{:S(2)}) collective-permute-start(bf16[80,1664]{1,0:T(8,128)(2,1)S(1)} %get-tuple-element.411), channel_id=1, source_target_pairs={{0,2},{1,0},{3,1},{5,3},{7,5},{6,7},{4,6},{2,4},{8,10},{9,8},{11,9... | collective-permute-start | bytes 798728 | tf_op jit(solution)/shard_map/ppermute | solution.py:178
  337.2 10.6 %collective-permute-start.41 = (bf16[80,1664]{1,0:T(8,128)(2,1)S(1)}, bf16[80,1664]{1,0:T(8,128)(2,1)S(1)}, u32[]{:S(2)}, u32[]{:S(2)}) collective-permute-start(bf16[80,1664]{1,0:T(8,128)(2,1)S(1)} %get-tuple-element.412), channel_id=1, source_target_pairs={{0,2},{1,0},{3,1},{5,3},{7,5},{6,7},{4,6},{2,4},{8,10},{9,8},{11,9... | collective-permute-start | bytes 798728 | tf_op jit(solution)/shard_map/ppermute | solution.py:178
  338.7 9.0 %collective-permute-start.32 = (bf16[80,1664]{1,0:T(8,128)(2,1)S(1)}, bf16[80,1664]{1,0:T(8,128)(2,1)S(1)}, u32[]{:S(2)}, u32[]{:S(2)}) collective-permute-start(bf16[80,1664]{1,0:T(8,128)(2,1)S(1)} %get-tuple-element.413), channel_id=1, source_target_pairs={{0,1},{1,3},{3,5},{5,7},{7,6},{6,4},{4,2},{2,0},{8,9},{9,11},{11,1... | collective-permute-start | bytes 798728 | tf_op jit(solution)/shard_map/ppermute | solution.py:178
  340.3 11.7 %collective-permute-start.51 = (bf16[80,1536]{1,0:T(8,128)(2,1)S(1)}, bf16[80,1536]{1,0:T(8,128)(2,1)S(1)}, u32[]{:S(2)}, u32[]{:S(2)}) collective-permute-start(bf16[80,1536]{1,0:T(8,128)(2,1)S(1)} %fusion.104), channel_id=1, source_target_pairs={{0,1},{1,3},{3,5},{5,7},{7,6},{6,4},{4,2},{2,0},{8,9},{9,11},{11,1... | collective-permute-start | bytes 737288 | tf_op jit(solution)/shard_map/ppermute | solution.py:178
  349.3 7.6 %collective-permute-start.60 = (bf16[80,1664]{1,0:T(8,128)(2,1)S(1)}, bf16[80,1664]{1,0:T(8,128)(2,1)S(1)}, u32[]{:S(2)}, u32[]{:S(2)}) collective-permute-start(bf16[80,1664]{1,0:T(8,128)(2,1)S(1)} %get-tuple-element.408), channel_id=1, source_target_pairs={{0,2},{1,0},{3,1},{5,3},{7,5},{6,7},{4,6},{2,4},{8,10},{9,8},{11,9... | collective-permute-start | bytes 798728 | tf_op jit(solution)/shard_map/ppermute | solution.py:178
  349.9 10.1 %collective-permute-start.42 = (bf16[80,1664]{1,0:T(8,128)(2,1)S(1)}, bf16[80,1664]{1,0:T(8,128)(2,1)S(1)}, u32[]{:S(2)}, u32[]{:S(2)}) collective-permute-start(bf16[80,1664]{1,0:T(8,128)(2,1)S(1)} %get-tuple-element.409), channel_id=1, source_target_pairs={{0,2},{1,0},{3,1},{5,3},{7,5},{6,7},{4,6},{2,4},{8,10},{9,8},{11,9... | collective-permute-start | bytes 798728 | tf_op jit(solution)/shard_map/ppermute | solution.py:178
  351.6 8.5 %collective-permute-start.33 = (bf16[80,1664]{1,0:T(8,128)(2,1)S(1)}, bf16[80,1664]{1,0:T(8,128)(2,1)S(1)}, u32[]{:S(2)}, u32[]{:S(2)}) collective-permute-start(bf16[80,1664]{1,0:T(8,128)(2,1)S(1)} %get-tuple-element.410), channel_id=1, source_target_pairs={{0,1},{1,3},{3,5},{5,7},{7,6},{6,4},{4,2},{2,0},{8,9},{9,11},{11,1... | collective-permute-start | bytes 798728 | tf_op jit(solution)/shard_map/ppermute | solution.py:178
  353.1 11.2 %collective-permute-start.52 = (bf16[80,1536]{1,0:T(8,128)(2,1)S(1)}, bf16[80,1536]{1,0:T(8,128)(2,1)S(1)}, u32[]{:S(2)}, u32[]{:S(2)}) collective-permute-start(bf16[80,1536]{1,0:T(8,128)(2,1)S(1)} %fusion.103), channel_id=1, source_target_pairs={{0,1},{1,3},{3,5},{5,7},{7,6},{6,4},{4,2},{2,0},{8,9},{9,11},{11,1... | collective-permute-start | bytes 737288 | tf_op jit(solution)/shard_map/ppermute | solution.py:178
  361.5 6.8 %collective-permute-start.61 = (bf16[80,1664]{1,0:T(8,128)(2,1)S(1)}, bf16[80,1664]{1,0:T(8,128)(2,1)S(1)}, u32[]{:S(2)}, u32[]{:S(2)}) collective-permute-start(bf16[80,1664]{1,0:T(8,128)(2,1)S(1)} %get-tuple-element.405), channel_id=1, source_target_pairs={{0,2},{1,0},{3,1},{5,3},{7,5},{6,7},{4,6},{2,4},{8,10},{9,8},{11,9... | collective-permute-start | bytes 798728 | tf_op jit(solution)/shard_map/ppermute | solution.py:178
  362.2 10.1 %collective-permute-start.43 = (bf16[80,1664]{1,0:T(8,128)(2,1)S(1)}, bf16[80,1664]{1,0:T(8,128)(2,1)S(1)}, u32[]{:S(2)}, u32[]{:S(2)}) collective-permute-start(bf16[80,1664]{1,0:T(8,128)(2,1)S(1)} %get-tuple-element.406), channel_id=1, source_target_pairs={{0,2},{1,0},{3,1},{5,3},{7,5},{6,7},{4,6},{2,4},{8,10},{9,8},{11,9... | collective-permute-start | bytes 798728 | tf_op jit(solution)/shard_map/ppermute | solution.py:178
  363.8 8.5 %collective-permute-start.34 = (bf16[80,1664]{1,0:T(8,128)(2,1)S(1)}, bf16[80,1664]{1,0:T(8,128)(2,1)S(1)}, u32[]{:S(2)}, u32[]{:S(2)}) collective-permute-start(bf16[80,1664]{1,0:T(8,128)(2,1)S(1)} %get-tuple-element.407), channel_id=1, source_target_pairs={{0,1},{1,3},{3,5},{5,7},{7,6},{6,4},{4,2},{2,0},{8,9},{9,11},{11,1... | collective-permute-start | bytes 798728 | tf_op jit(solution)/shard_map/ppermute | solution.py:178
  365.3 11.2 %collective-permute-start.53 = (bf16[80,1536]{1,0:T(8,128)(2,1)S(1)}, bf16[80,1536]{1,0:T(8,128)(2,1)S(1)}, u32[]{:S(2)}, u32[]{:S(2)}) collective-permute-start(bf16[80,1536]{1,0:T(8,128)(2,1)S(1)} %fusion.102), channel_id=1, source_target_pairs={{0,1},{1,3},{3,5},{5,7},{7,6},{6,4},{4,2},{2,0},{8,9},{9,11},{11,1... | collective-permute-start | bytes 737288 | tf_op jit(solution)/shard_map/ppermute | solution.py:178
  373.8 6.5 %collective-permute-start.62 = (bf16[80,1664]{1,0:T(8,128)(2,1)S(1)}, bf16[80,1664]{1,0:T(8,128)(2,1)S(1)}, u32[]{:S(2)}, u32[]{:S(2)}) collective-permute-start(bf16[80,1664]{1,0:T(8,128)(2,1)S(1)} %get-tuple-element.402), channel_id=1, source_target_pairs={{0,2},{1,0},{3,1},{5,3},{7,5},{6,7},{4,6},{2,4},{8,10},{9,8},{11,9... | collective-permute-start | bytes 798728 | tf_op jit(solution)/shard_map/ppermute | solution.py:178
  374.5 8.7 %collective-permute-start.44 = (bf16[80,1664]{1,0:T(8,128)(2,1)S(1)}, bf16[80,1664]{1,0:T(8,128)(2,1)S(1)}, u32[]{:S(2)}, u32[]{:S(2)}) collective-permute-start(bf16[80,1664]{1,0:T(8,128)(2,1)S(1)} %get-tuple-element.403), channel_id=1, source_target_pairs={{0,2},{1,0},{3,1},{5,3},{7,5},{6,7},{4,6},{2,4},{8,10},{9,8},{11,9... | collective-permute-start | bytes 798728 | tf_op jit(solution)/shard_map/ppermute | solution.py:178
  376.1 7.1 %collective-permute-start.35 = (bf16[80,1664]{1,0:T(8,128)(2,1)S(1)}, bf16[80,1664]{1,0:T(8,128)(2,1)S(1)}, u32[]{:S(2)}, u32[]{:S(2)}) collective-permute-start(bf16[80,1664]{1,0:T(8,128)(2,1)S(1)} %get-tuple-element.404), channel_id=1, source_target_pairs={{0,1},{1,3},{3,5},{5,7},{7,6},{6,4},{4,2},{2,0},{8,9},{9,11},{11,1... | collective-permute-start | bytes 798728 | tf_op jit(solution)/shard_map/ppermute | solution.py:178
  377.6 10.8 %collective-permute-start.54 = (bf16[80,1536]{1,0:T(8,128)(2,1)S(1)}, bf16[80,1536]{1,0:T(8,128)(2,1)S(1)}, u32[]{:S(2)}, u32[]{:S(2)}) collective-permute-start(bf16[80,1536]{1,0:T(8,128)(2,1)S(1)} %fusion.121), channel_id=1, source_target_pairs={{0,16},{8,24},{16,0},{24,8},{1,17},{9,25},{17,1},{25,9},{2,18},{10... | collective-permute-start | bytes 737288 | tf_op jit(solution)/shard_map/ppermute | solution.py:181
  384.7 9.3 %collective-permute-start.63 = (bf16[80,1664]{1,0:T(8,128)(2,1)S(1)}, bf16[80,1664]{1,0:T(8,128)(2,1)S(1)}, u32[]{:S(2)}, u32[]{:S(2)}) collective-permute-start(bf16[80,1664]{1,0:T(8,128)(2,1)S(1)} %get-tuple-element.399), channel_id=1, source_target_pairs={{0,16},{8,24},{16,0},{24,8},{1,17},{9,25},{17,1},{25,9},{2,18},{10... | collective-permute-start | bytes 798728 | tf_op jit(solution)/shard_map/ppermute | solution.py:181
  386.3 11.5 %collective-permute-start.45 = (bf16[80,1664]{1,0:T(8,128)(2,1)S(1)}, bf16[80,1664]{1,0:T(8,128)(2,1)S(1)}, u32[]{:S(2)}, u32[]{:S(2)}) collective-permute-start(bf16[80,1664]{1,0:T(8,128)(2,1)S(1)} %get-tuple-element.400), channel_id=1, source_target_pairs={{0,16},{8,24},{16,0},{24,8},{1,17},{9,25},{17,1},{25,9},{2,18},{10... | collective-permute-start | bytes 798728 | tf_op jit(solution)/shard_map/ppermute | solution.py:181
  386.8 13.9 %collective-permute-start.36 = (bf16[80,1664]{1,0:T(8,128)(2,1)S(1)}, bf16[80,1664]{1,0:T(8,128)(2,1)S(1)}, u32[]{:S(2)}, u32[]{:S(2)}) collective-permute-start(bf16[80,1664]{1,0:T(8,128)(2,1)S(1)} %get-tuple-element.401), channel_id=1, source_target_pairs={{0,16},{8,24},{16,0},{24,8},{1,17},{9,25},{17,1},{25,9},{2,18},{10... | collective-permute-start | bytes 798728 | tf_op jit(solution)/shard_map/ppermute | solution.py:181
  389.5 16.5 %collective-permute-start.55 = (f32[80,1536]{1,0:T(8,128)S(1)}, f32[80,1536]{1,0:T(8,128)S(1)}, u32[]{:S(2)}, u32[]{:S(2)}) collective-permute-start(f32[80,1536]{1,0:T(8,128)S(1)} %convert_add_fusion.5), channel_id=1, source_target_pairs={{0,8},{8,0},{16,24},{24,16},{1,9},{9,1},{17,25},{25,17},{2,10},{10... | collective-permute-start | bytes 1474568 | tf_op jit(solution)/shard_map/ppermute | solution.py:184
  402.9 3.9 collective-permute-start.64
  536.2 43.5 %all-to-all-start.1 = ((bf16[5,8,80,160]{3,2,0,1:T(8,128)(2,1)}), bf16[5,8,80,160]{3,2,0,1:T(8,128)(2,1)}, u32[]{:S(2)}, u32[]{:S(2)}) async-start(bf16[5,8,80,160]{3,2,0,1:T(8,128)(2,1)} %copy.223), calls=%async_computation.1 | async-start | bytes 3276800 | tf_op jit(solution)/shard_map/all_to_all | solution.py:468
  579.7 27.0 %collective-permute-start.66 = (bf16[5,8,80,160]{3,2,0,1:T(8,128)(2,1)}, bf16[5,8,80,160]{3,2,0,1:T(8,128)(2,1)}, u32[]{:S(2)}, u32[]{:S(2)}) collective-permute-start(bf16[5,8,80,160]{3,2,0,1:T(8,128)(2,1)} %all-to-all-done.1), channel_id=1, source_target_pairs={{0,8},{8,0},{16,24},{24,16},{1,9},{9,1},{17,25},{25,17},{2,10},{10... | collective-permute-start | bytes 3072008 | tf_op jit(solution)/shard_map/ppermute | solution.py:475
  584.3 3.6 collective-permute-start.68
  591.4 3.6 collective-permute-start.70
  595.0 4.5 collective-permute-start.71
  (69 other events, 1461.7 us)
